TPU v7x, 32 devices: a whole 2x2x4 slice. The times are simulated.
32 devices in a mesh: dp: 8 (over z, y), mp: 4 (over x, core).
Axes of the slice: x: 2, y: 2, z: 4, core: 2. Of those that a mesh axis runs over, the one named last changes fastest.
Arguments:
- gradients: bfloat16 [8, 4, 192, 16384], P('dp', 'mp'), may hold values from -3000 to 3000
- owner_list: int32 [192], replicated, may hold values from 0 to 7, as said below
- master_weights: float32 [4, 288, 16384], P('mp', 'dp'), may hold values from -6 to 6
- first_moment: float32 [4, 288, 16384], P('mp', 'dp'), may hold values from -6 to 6
- second_moment: float32 [4, 288, 16384], P('mp', 'dp'), may hold values from 0.05 to 2
- average_weights: float32 [4, 288, 16384], P('mp', 'dp'), may hold values from -6 to 6
Outputs:
- new_params: bfloat16 [4, 192, 16384], P('mp')
- new_master: float32 [4, 288, 16384], P('mp', 'dp')
- new_first: float32 [4, 288, 16384], P('mp', 'dp')
- new_second: float32 [4, 288, 16384], P('mp', 'dp')
- average_rows: float32 [4, 192, 16384], P('mp', 'dp')
Inputs may be any that keep to these rules, and one draw needn't show every extreme that they name: `owner_list`: each data rank owns at most 36 segments, and some rank owns exactly 36.
All inputs are finite; a program needn't handle non-finite values.
Results may differ from a plain program's by a relative error of at most 0.015.
Values may be sent and summed in bfloat16 or wider, within the bound.
No kernel may reach another device: no remote copies, remote signals or barrier semaphores. Data moves between devices by JAX's collectives and lax.ppermute only.
A program may use at most 128 MiB of HBM per device.

v0:
```python
import math

import jax
import jax.numpy as jnp
from jax import lax
from jax.sharding import PartitionSpec as P


def ring_order(mesh):
    n = mesh.shape["dp"]
    try:
        coords = [tuple(mesh.devices[i, 0].coords) for i in range(n)]
        at = {(c[2], c[1]): i for i, c in enumerate(coords)}
        zs = sorted({z for z, _ in at})
        ys = sorted({y for _, y in at})
        if len(at) != n or len(zs) * len(ys) != n:
            return list(range(n))
        if len(ys) % 2:
            if len(zs) % 2:
                return list(range(n))
            at = {(y, z): i for (z, y), i in at.items()}
            zs, ys = ys, zs
        if len(zs) == 1 or len(ys) == 1:
            line = zs if len(ys) == 1 else ys
            return [at[(z, ys[0])] if len(ys) == 1 else at[(zs[0], z)] for z in line]
        cycle = [(z, ys[0]) for z in zs]
        for k, y in enumerate(ys[1:]):
            inner = zs[1:][::-1] if k % 2 == 0 else zs[1:]
            cycle += [(z, y) for z in inner]
        cycle += [(zs[0], y) for y in ys[1:][::-1]]
        return [at[c] for c in cycle]
    except (AttributeError, TypeError, IndexError, KeyError):
        return list(range(n))


def all_sum(v, axis, n):
    if n & (n - 1):
        return lax.psum(v, axis)
    k = 1
    while k < n:
        v = v + lax.ppermute(v, axis, [(i, i ^ k) for i in range(n)])
        k *= 2
    return v


def make_on_device(ring):
    n = len(ring)
    pos_of = [ring.index(r) for r in range(n)]
    fwd = [(ring[q], ring[(q + 1) % n]) for q in range(n)]
    bwd = [(ring[(q + 1) % n], ring[q]) for q in range(n)]

    def on_device(gradients, owner_list, master_weights, first_moment, second_moment, average_weights):
        local_grad = gradients[0, 0]
        nseg, seg = local_grad.shape
        cap = master_weights.shape[1]
        blocks = lax.axis_size("mp")
        per_rank = nseg // n
        half = seg // 2
        me = lax.axis_index("dp")
        rank_at = jnp.array(ring, jnp.int32)
        mypos = jnp.array(pos_of, jnp.int32)[me]

        position = jnp.arange(nseg, dtype=jnp.int32)
        same_owner = (owner_list[:, None] == owner_list[None, :]) & (position[None, :] < position[:, None])
        within = jnp.sum(same_owner.astype(jnp.int32), axis=1)
        slot = owner_list * cap + within
        hit = jnp.arange(n * cap, dtype=jnp.int32)[:, None] == slot[None, :]
        valid = jnp.any(hit, axis=1)
        placing = hit.astype(local_grad.dtype)
        by_owner = jnp.dot(placing, local_grad, preferred_element_type=jnp.bfloat16).reshape(n, cap, seg)
        left, right = by_owner[..., :half], by_owner[..., half:]

        def own(x, p):
            return lax.dynamic_index_in_dim(x, rank_at[p % n], 0, keepdims=False).astype(jnp.float32)

        send_a = own(left, mypos - 1 + n).astype(jnp.bfloat16)
        send_b = own(right, mypos + 1).astype(jnp.bfloat16)
        for t in range(n - 1):
            got_a = lax.ppermute(send_a, "dp", fwd)
            got_b = lax.ppermute(send_b, "dp", bwd)
            acc_a = got_a.astype(jnp.float32) + own(left, mypos - 2 - t + 2 * n)
            acc_b = got_b.astype(jnp.float32) + own(right, mypos + 2 + t)
            if t < n - 2:
                send_a, send_b = acc_a.astype(jnp.bfloat16), acc_b.astype(jnp.bfloat16)
        owned = jnp.concatenate([acc_a, acc_b], axis=1)

        total_sq = all_sum(all_sum(jnp.sum(owned * owned).reshape(1, 1), "dp", n), "mp", blocks)[0, 0]
        clip_factor = jnp.minimum(1.0, math.sqrt(blocks * nseg * seg) / (jnp.sqrt(total_sq) + 1e-06))
        in_use = lax.dynamic_index_in_dim(valid.reshape(n, cap), me, 0, keepdims=False)
        in_use = in_use.astype(jnp.float32)[:, None]
        owned_grad = clip_factor * owned
        new_first = in_use * (0.9 * first_moment[0] + 0.1 * owned_grad)
        new_second = in_use * (0.95 * second_moment[0] + 0.05 * owned_grad * owned_grad)
        first_hat = new_first / (1.0 - 0.9**20)
        second_hat = new_second / (1.0 - 0.95**20)
        old_master = master_weights[0]
        new_master = in_use * (
            old_master - 0.02 * (first_hat / (jnp.sqrt(second_hat) + 1e-08) + 0.1 * old_master)
        )
        averaged = 0.9 * average_weights[0] + 0.1 * new_master

        payload = jnp.concatenate([new_master, averaged], axis=0).astype(jnp.bfloat16)
        send_a, send_b = payload[:, :half], payload[:, half:]
        placing_t = placing.T
        mine_t = lax.dynamic_slice_in_dim(placing_t, me * per_rank, per_rank, 0)

        def spread(rows_t, chunk, p, kind):
            cols = lax.dynamic_slice_in_dim(rows_t, rank_at[p % n] * cap, cap, 1)
            return jnp.dot(cols, chunk, preferred_element_type=kind)

        def place(acc, p_a, a, p_b, b):
            parts = (
                spread(placing_t, a[:cap], p_a, jnp.bfloat16),
                spread(placing_t, b[:cap], p_b, jnp.bfloat16),
                spread(mine_t, a[cap:], p_a, jnp.float32),
                spread(mine_t, b[cap:], p_b, jnp.float32),
            )
            if acc is None:
                return parts
            return tuple(x + y for x, y in zip(acc, parts))

        acc = place(None, mypos, send_a, mypos, send_b)
        for t in range(n - 1):
            send_a = lax.ppermute(send_a, "dp", fwd)
            send_b = lax.ppermute(send_b, "dp", bwd)
            acc = place(acc, mypos - 1 - t + n, send_a, mypos + 1 + t, send_b)
        new_params = jnp.concatenate([acc[0], acc[1]], axis=1)
        average_rows = jnp.concatenate([acc[2], acc[3]], axis=1)
        return (
            new_params[None],
            new_master[None],
            new_first[None],
            new_second[None],
            average_rows[None],
        )

    return on_device


def solution(mesh):
    return jax.shard_map(
        make_on_device(ring_order(mesh)),
        mesh=mesh,
        in_specs=(
            P("dp", "mp", None, None),
            P(),
            P("mp", "dp", None),
            P("mp", "dp", None),
            P("mp", "dp", None),
            P("mp", "dp", None),
        ),
        out_specs=(
            P("mp", None, None),
            P("mp", "dp", None),
            P("mp", "dp", None),
            P("mp", "dp", None),
            P("mp", "dp", None),
        ),
        check_vma=False,
    )
```

profile of v0, /device:TPU:0, one launch (start us, length us, event | category | flops | bytes accessed | tf_op | source)
XLA Modules:
  0.0 385.0 jit_solution(10756747171418572953)
XLA Ops:
  0.6 1.2 dynamic_slice.85
  13.2 2.0 fusion.122
  17.9 8.4 %fusion = bf16[8,36,16384]{2,1,0:T(8,128)(2,1)} fusion(bf16[1,1,192,16384]{3,2,1,0:T(8,128)(2,1)} %param.8, s32[192]{0:T(256)S(1)} %multiply_add_fusion.1, s32[8,36]{1,0:T(8,128)S(1)} %multiply_add_fusion), kind=kOutput, calls=%fused_computation.29 | convolution fusion | flops 1811994624 | bytes 15730560 | tf_op jit(solution)/shard_map/dot_general | solution.py:70
  26.2 9.4 %fusion.121 = (bf16[8,36,8192]{2,1,0:T(8,128)(2,1)}, bf16[8,36,8192]{2,1,0:T(8,128)(2,1)}) fusion(bf16[8,36,16384]{2,1,0:T(8,128)(2,1)} %fusion), kind=kLoop, calls=%fused_computation.188 | loop fusion | bytes 18874368 | tf_op jit(solution)/shard_map/slice | solution.py:71
  37.3 3.1 collective-permute-start
  71.8 1.4 fusion.26
  73.2 2.1 collective-permute-start.1
  75.3 1.2 fusion.20
  76.8 12.7 %collective-permute-done.1 = bf16[36,8192]{1,0:T(8,128)(2,1)S(1)} collective-permute-done((bf16[36,8192]{1,0:T(8,128)(2,1)S(1)}, bf16[36,8192]{1,0:T(8,128)(2,1)S(1)}, u32[]{:S(2)}, u32[]{:S(2)}) %collective-permute-start.1) | collective-permute-done | bytes 589856 | tf_op jit(solution)/shard_map/ppermute | solution.py:79
  89.5 1.2 fusion.25
  90.7 1.8 collective-permute-start.2
  93.0 13.0 %collective-permute-done.2 = bf16[36,8192]{1,0:T(8,128)(2,1)S(1)} collective-permute-done((bf16[36,8192]{1,0:T(8,128)(2,1)S(1)}, bf16[36,8192]{1,0:T(8,128)(2,1)S(1)}, u32[]{:S(2)}, u32[]{:S(2)}) %collective-permute-start.2) | collective-permute-done | bytes 589856 | tf_op jit(solution)/shard_map/ppermute | solution.py:79
  106.1 1.2 fusion.24
  107.3 1.5 collective-permute-start.3
  109.6 12.4 %collective-permute-done.3 = bf16[36,8192]{1,0:T(8,128)(2,1)S(1)} collective-permute-done((bf16[36,8192]{1,0:T(8,128)(2,1)S(1)}, bf16[36,8192]{1,0:T(8,128)(2,1)S(1)}, u32[]{:S(2)}, u32[]{:S(2)}) %collective-permute-start.3) | collective-permute-done | bytes 589856 | tf_op jit(solution)/shard_map/ppermute | solution.py:79
  122.2 1.5 collective-permute-start.4
  124.5 12.5 %collective-permute-done.4 = bf16[36,8192]{1,0:T(8,128)(2,1)S(1)} collective-permute-done((bf16[36,8192]{1,0:T(8,128)(2,1)S(1)}, bf16[36,8192]{1,0:T(8,128)(2,1)S(1)}, u32[]{:S(2)}, u32[]{:S(2)}) %collective-permute-start.4) | collective-permute-done | bytes 589856 | tf_op jit(solution)/shard_map/ppermute | solution.py:79
  137.1 1.5 collective-permute-start.5
  139.4 12.5 %collective-permute-done.5 = bf16[36,8192]{1,0:T(8,128)(2,1)S(1)} collective-permute-done((bf16[36,8192]{1,0:T(8,128)(2,1)S(1)}, bf16[36,8192]{1,0:T(8,128)(2,1)S(1)}, u32[]{:S(2)}, u32[]{:S(2)}) %collective-permute-start.5) | collective-permute-done | bytes 589856 | tf_op jit(solution)/shard_map/ppermute | solution.py:79
  152.0 1.5 collective-permute-start.6
  154.5 9.4 %collective-permute-done.6 = bf16[36,8192]{1,0:T(8,128)(2,1)S(1)} collective-permute-done((bf16[36,8192]{1,0:T(8,128)(2,1)S(1)}, bf16[36,8192]{1,0:T(8,128)(2,1)S(1)}, u32[]{:S(2)}, u32[]{:S(2)}) %collective-permute-start.6) | collective-permute-done | bytes 589856 | tf_op jit(solution)/shard_map/ppermute | solution.py:79
  165.1 1.3 multiply_reduce_fusion
  167.2 2.8 collective-permute-done.14
  171.3 3.0 collective-permute-start.15
  175.5 4.0 %collective-permute-start.16 = (f32[1,1]{1,0:T(1,128)}, f32[1,1]{1,0:T(1,128)}, u32[]{:S(2)}, u32[]{:S(2)}) collective-permute-start(f32[1,1]{1,0:T(1,128)} %add.710), channel_id=1, source_target_pairs={{0,16},{4,20},{8,24},{12,28},{16,0},{20,4},{24,8},{28,12},{1,17},{... | collective-permute-start | bytes 20 | tf_op jit(solution)/shard_map/ppermute | solution.py:41
  182.5 2.9 collective-permute-start.18
  186.9 9.1 %fusion.12 = (bf16[36,16384]{1,0:T(8,128)(2,1)S(1)}, bf16[36,16384]{1,0:T(8,128)(2,1)S(1)}) fusion(f32[1,36,16384]{2,0,1:T(1,128)S(1)} %copy-done.5, f32[1,36,16384]{2,0,1:T(1,128)S(1)} %copy-done.2, f32[36,8192]{1,0:T(8,128)S(1)} %convert_add_fusion, f32[36,8192]{1,0:T(8,128)S(1)} %convert_add_fusion.7, f32[]{:T(128)} %bitcast.37, ...), kind=kLoop, calls=%fused_computation.48 | loop fusion | flops 14745600 | bytes 14155924 | tf_op jit(solution)/shard_map/convert.16
  196.3 1.6 collective-permute-start.19
  198.4 7.5 %subtract_multiply_fusion = (f32[1,36,16384]{2,1,0:T(8,128)S(1)}, f32[1,36,16384]{2,1,0:T(8,128)S(1)}, f32[1,36,16384]{2,1,0:T(8,128)S(1)}) fusion(f32[1,36,16384]{2,0,1:T(1,128)S(1)} %copy-done.4, f32[36]{0:T(128)S(1)} %fusion.118, f32[1,36,8192]{2,1,0:T(8,128)S(1)} %bitcast.108, f32[1,36,8192]{2,1,0:T(8,128)S(1)} %bitcast.107, f32[]{:T(128)} %bitcast.37, ...), kind=kLoop, calls=%fused_computation.55 | loop fusion | flops 11796480 | bytes 16515220 | tf_op jit(solution)/shard_map/mul | solution.py:97
  206.0 3.8 copy.26
  209.8 3.8 copy.27
  213.6 3.8 copy.28
  220.4 3.1 collective-permute-done.19
  223.5 1.6 collective-permute-start.20
  228.8 20.8 %collective-permute-done.20 = bf16[72,8192]{1,0:T(8,128)(2,1)S(1)} collective-permute-done((bf16[72,8192]{1,0:T(8,128)(2,1)S(1)}, bf16[72,8192]{1,0:T(8,128)(2,1)S(1)}, u32[]{:S(2)}, u32[]{:S(2)}) %collective-permute-start.20) | collective-permute-done | bytes 1179680 | tf_op jit(solution)/shard_map/ppermute | solution.py:124
  249.7 1.6 collective-permute-start.21
  255.0 20.8 %collective-permute-done.21 = bf16[72,8192]{1,0:T(8,128)(2,1)S(1)} collective-permute-done((bf16[72,8192]{1,0:T(8,128)(2,1)S(1)}, bf16[72,8192]{1,0:T(8,128)(2,1)S(1)}, u32[]{:S(2)}, u32[]{:S(2)}) %collective-permute-start.21) | collective-permute-done | bytes 1179680 | tf_op jit(solution)/shard_map/ppermute | solution.py:124
  275.8 1.6 collective-permute-start.22
  281.1 20.8 %collective-permute-done.22 = bf16[72,8192]{1,0:T(8,128)(2,1)S(1)} collective-permute-done((bf16[72,8192]{1,0:T(8,128)(2,1)S(1)}, bf16[72,8192]{1,0:T(8,128)(2,1)S(1)}, u32[]{:S(2)}, u32[]{:S(2)}) %collective-permute-start.22) | collective-permute-done | bytes 1179680 | tf_op jit(solution)/shard_map/ppermute | solution.py:124
  301.9 1.6 collective-permute-start.23
  307.2 20.9 %collective-permute-done.23 = bf16[72,8192]{1,0:T(8,128)(2,1)S(1)} collective-permute-done((bf16[72,8192]{1,0:T(8,128)(2,1)S(1)}, bf16[72,8192]{1,0:T(8,128)(2,1)S(1)}, u32[]{:S(2)}, u32[]{:S(2)}) %collective-permute-start.23) | collective-permute-done | bytes 1179680 | tf_op jit(solution)/shard_map/ppermute | solution.py:124
  328.1 1.6 collective-permute-start.24
  333.3 21.0 %collective-permute-done.24 = bf16[72,8192]{1,0:T(8,128)(2,1)S(1)} collective-permute-done((bf16[72,8192]{1,0:T(8,128)(2,1)S(1)}, bf16[72,8192]{1,0:T(8,128)(2,1)S(1)}, u32[]{:S(2)}, u32[]{:S(2)}) %collective-permute-start.24) | collective-permute-done | bytes 1179680 | tf_op jit(solution)/shard_map/ppermute | solution.py:124
  354.2 1.6 collective-permute-start.25
  359.2 16.9 %collective-permute-done.25 = bf16[72,8192]{1,0:T(8,128)(2,1)S(1)} collective-permute-done((bf16[72,8192]{1,0:T(8,128)(2,1)S(1)}, bf16[72,8192]{1,0:T(8,128)(2,1)S(1)}, u32[]{:S(2)}, u32[]{:S(2)}) %collective-permute-start.25) | collective-permute-done | bytes 1179680 | tf_op jit(solution)/shard_map/ppermute | solution.py:124
  376.5 1.3 collective-permute-done.32
  378.2 1.2 maximum_bitcast_fusion.1
  381.5 3.3 maximum_bitcast_fusion
  (97 shorter events, 42.1 us)
Async XLA Ops:
  37.3 34.5 %collective-permute-start = (bf16[36,8192]{1,0:T(8,128)(2,1)S(1)}, bf16[36,8192]{1,0:T(8,128)(2,1)S(1)}, u32[]{:S(2)}, u32[]{:S(2)}) collective-permute-start(bf16[36,8192]{1,0:T(8,128)(2,1)S(1)} %dynamic-slice_bitcast_fusion.1), channel_id=1, source_target_pairs={{0,8},{8,16},{16,24},{24,28},{28,20},{20,12},{12,4},{4,0},{1,9},{9... | collective-permute-start | bytes 1769480 | tf_op jit(solution)/shard_map/ppermute | solution.py:79
  43.6 31.7 %collective-permute-start.7 = (bf16[36,8192]{1,0:T(8,128)(2,1)S(1)}, bf16[36,8192]{1,0:T(8,128)(2,1)S(1)}, u32[]{:S(2)}, u32[]{:S(2)}) collective-permute-start(bf16[36,8192]{1,0:T(8,128)(2,1)S(1)} %dynamic-slice_bitcast_fusion), channel_id=1, source_target_pairs={{8,0},{16,8},{24,16},{28,24},{20,28},{12,20},{4,12},{0,4},{9,1},{1... | collective-permute-start | bytes 1769480 | tf_op jit(solution)/shard_map/ppermute | solution.py:80
  71.8 20.7 %copy-start = (bf16[8,36,8192]{2,1,0:T(8,128)(2,1)S(1)}, bf16[8,36,8192]{2,1,0:T(8,128)(2,1)}, u32[]{:S(2)}) copy-start(bf16[8,36,8192]{2,1,0:T(8,128)(2,1)} %get-tuple-element.21) | copy-start | bytes 14155780
  73.2 16.2 %collective-permute-start.1 = (bf16[36,8192]{1,0:T(8,128)(2,1)S(1)}, bf16[36,8192]{1,0:T(8,128)(2,1)S(1)}, u32[]{:S(2)}, u32[]{:S(2)}) collective-permute-start(bf16[36,8192]{1,0:T(8,128)(2,1)S(1)} %fusion.26), channel_id=1, source_target_pairs={{0,8},{8,16},{16,24},{24,28},{28,20},{20,12},{12,4},{4,0},{1,9},{9... | collective-permute-start | bytes 1769480 | tf_op jit(solution)/shard_map/ppermute | solution.py:79
  76.6 16.0 %collective-permute-start.8 = (bf16[36,8192]{1,0:T(8,128)(2,1)S(1)}, bf16[36,8192]{1,0:T(8,128)(2,1)S(1)}, u32[]{:S(2)}, u32[]{:S(2)}) collective-permute-start(bf16[36,8192]{1,0:T(8,128)(2,1)S(1)} %fusion.20), channel_id=1, source_target_pairs={{8,0},{16,8},{24,16},{28,24},{20,28},{12,20},{4,12},{0,4},{9,1},{1... | collective-permute-start | bytes 1769480 | tf_op jit(solution)/shard_map/ppermute | solution.py:80
  90.7 31.3 %copy-start.1 = (bf16[8,36,8192]{2,1,0:T(8,128)(2,1)S(1)}, bf16[8,36,8192]{2,1,0:T(8,128)(2,1)}, u32[]{:S(2)}) copy-start(bf16[8,36,8192]{2,1,0:T(8,128)(2,1)} %get-tuple-element.20) | copy-start | bytes 14155780
  90.7 15.3 %collective-permute-start.2 = (bf16[36,8192]{1,0:T(8,128)(2,1)S(1)}, bf16[36,8192]{1,0:T(8,128)(2,1)S(1)}, u32[]{:S(2)}, u32[]{:S(2)}) collective-permute-start(bf16[36,8192]{1,0:T(8,128)(2,1)S(1)} %fusion.25), channel_id=1, source_target_pairs={{0,8},{8,16},{16,24},{24,28},{28,20},{20,12},{12,4},{4,0},{1,9},{9... | collective-permute-start | bytes 1769480 | tf_op jit(solution)/shard_map/ppermute | solution.py:79
  92.7 16.1 %collective-permute-start.9 = (bf16[36,8192]{1,0:T(8,128)(2,1)S(1)}, bf16[36,8192]{1,0:T(8,128)(2,1)S(1)}, u32[]{:S(2)}, u32[]{:S(2)}) collective-permute-start(bf16[36,8192]{1,0:T(8,128)(2,1)S(1)} %fusion.19), channel_id=1, source_target_pairs={{8,0},{16,8},{24,16},{28,24},{20,28},{12,20},{4,12},{0,4},{9,1},{1... | collective-permute-start | bytes 1769480 | tf_op jit(solution)/shard_map/ppermute | solution.py:80
  107.3 14.7 %collective-permute-start.3 = (bf16[36,8192]{1,0:T(8,128)(2,1)S(1)}, bf16[36,8192]{1,0:T(8,128)(2,1)S(1)}, u32[]{:S(2)}, u32[]{:S(2)}) collective-permute-start(bf16[36,8192]{1,0:T(8,128)(2,1)S(1)} %fusion.24), channel_id=1, source_target_pairs={{0,8},{8,16},{16,24},{24,28},{28,20},{20,12},{12,4},{4,0},{1,9},{9... | collective-permute-start | bytes 1769480 | tf_op jit(solution)/shard_map/ppermute | solution.py:79
  109.0 14.7 %collective-permute-start.10 = (bf16[36,8192]{1,0:T(8,128)(2,1)S(1)}, bf16[36,8192]{1,0:T(8,128)(2,1)S(1)}, u32[]{:S(2)}, u32[]{:S(2)}) collective-permute-start(bf16[36,8192]{1,0:T(8,128)(2,1)S(1)} %fusion.18), channel_id=1, source_target_pairs={{8,0},{16,8},{24,16},{28,24},{20,28},{12,20},{4,12},{0,4},{9,1},{1... | collective-permute-start | bytes 1769480 | tf_op jit(solution)/shard_map/ppermute | solution.py:80
  122.2 14.7 %collective-permute-start.4 = (bf16[36,8192]{1,0:T(8,128)(2,1)S(1)}, bf16[36,8192]{1,0:T(8,128)(2,1)S(1)}, u32[]{:S(2)}, u32[]{:S(2)}) collective-permute-start(bf16[36,8192]{1,0:T(8,128)(2,1)S(1)} %fusion.23), channel_id=1, source_target_pairs={{0,8},{8,16},{16,24},{24,28},{28,20},{20,12},{12,4},{4,0},{1,9},{9... | collective-permute-start | bytes 1769480 | tf_op jit(solution)/shard_map/ppermute | solution.py:79
  123.9 14.7 %collective-permute-start.11 = (bf16[36,8192]{1,0:T(8,128)(2,1)S(1)}, bf16[36,8192]{1,0:T(8,128)(2,1)S(1)}, u32[]{:S(2)}, u32[]{:S(2)}) collective-permute-start(bf16[36,8192]{1,0:T(8,128)(2,1)S(1)} %fusion.17), channel_id=1, source_target_pairs={{8,0},{16,8},{24,16},{28,24},{20,28},{12,20},{4,12},{0,4},{9,1},{1... | collective-permute-start | bytes 1769480 | tf_op jit(solution)/shard_map/ppermute | solution.py:80
  137.1 14.7 %collective-permute-start.5 = (bf16[36,8192]{1,0:T(8,128)(2,1)S(1)}, bf16[36,8192]{1,0:T(8,128)(2,1)S(1)}, u32[]{:S(2)}, u32[]{:S(2)}) collective-permute-start(bf16[36,8192]{1,0:T(8,128)(2,1)S(1)} %fusion.22), channel_id=1, source_target_pairs={{0,8},{8,16},{16,24},{24,28},{28,20},{20,12},{12,4},{4,0},{1,9},{9... | collective-permute-start | bytes 1769480 | tf_op jit(solution)/shard_map/ppermute | solution.py:79
  138.8 14.7 %collective-permute-start.12 = (bf16[36,8192]{1,0:T(8,128)(2,1)S(1)}, bf16[36,8192]{1,0:T(8,128)(2,1)S(1)}, u32[]{:S(2)}, u32[]{:S(2)}) collective-permute-start(bf16[36,8192]{1,0:T(8,128)(2,1)S(1)} %fusion.16), channel_id=1, source_target_pairs={{8,0},{16,8},{24,16},{28,24},{20,28},{12,20},{4,12},{0,4},{9,1},{1... | collective-permute-start | bytes 1769480 | tf_op jit(solution)/shard_map/ppermute | solution.py:80
  152.0 11.8 %collective-permute-start.6 = (bf16[36,8192]{1,0:T(8,128)(2,1)S(1)}, bf16[36,8192]{1,0:T(8,128)(2,1)S(1)}, u32[]{:S(2)}, u32[]{:S(2)}) collective-permute-start(bf16[36,8192]{1,0:T(8,128)(2,1)S(1)} %fusion.21), channel_id=1, source_target_pairs={{0,8},{8,16},{16,24},{24,28},{28,20},{20,12},{12,4},{4,0},{1,9},{9... | collective-permute-start | bytes 1769480 | tf_op jit(solution)/shard_map/ppermute | solution.py:79
  153.5 33.3 %copy-start.5 = (f32[1,36,16384]{2,0,1:T(1,128)S(1)}, f32[1,36,16384]{2,0,1:T(1,128)}, u32[]{:S(2)}) copy-start(f32[1,36,16384]{2,0,1:T(1,128)} %param.13) | copy-start | bytes 7077892
  153.7 11.3 %collective-permute-start.13 = (bf16[36,8192]{1,0:T(8,128)(2,1)S(1)}, bf16[36,8192]{1,0:T(8,128)(2,1)S(1)}, u32[]{:S(2)}, u32[]{:S(2)}) collective-permute-start(bf16[36,8192]{1,0:T(8,128)(2,1)S(1)} %fusion.15), channel_id=1, source_target_pairs={{8,0},{16,8},{24,16},{28,24},{20,28},{12,20},{4,12},{0,4},{9,1},{1... | collective-permute-start | bytes 1769480 | tf_op jit(solution)/shard_map/ppermute | solution.py:80
  163.9 23.0 %copy-start.4 = (f32[1,36,16384]{2,0,1:T(1,128)S(1)}, f32[1,36,16384]{2,0,1:T(1,128)}, u32[]{:S(2)}) copy-start(f32[1,36,16384]{2,0,1:T(1,128)} %param.10) | copy-start | bytes 7077892
  164.0 22.9 %copy-start.2 = (f32[1,36,16384]{2,0,1:T(1,128)S(1)}, f32[1,36,16384]{2,0,1:T(1,128)}, u32[]{:S(2)}) copy-start(f32[1,36,16384]{2,0,1:T(1,128)} %param.12) | copy-start | bytes 7077892
  164.0 22.9 %copy-start.3 = (f32[1,36,16384]{2,0,1:T(1,128)S(1)}, f32[1,36,16384]{2,0,1:T(1,128)}, u32[]{:S(2)}) copy-start(f32[1,36,16384]{2,0,1:T(1,128)} %param.11) | copy-start | bytes 7077892
  166.4 3.6 collective-permute-start.14
  171.3 3.6 collective-permute-start.15
  175.5 4.5 %collective-permute-start.16 = (f32[1,1]{1,0:T(1,128)}, f32[1,1]{1,0:T(1,128)}, u32[]{:S(2)}, u32[]{:S(2)}) collective-permute-start(f32[1,1]{1,0:T(1,128)} %add.710), channel_id=1, source_target_pairs={{0,16},{4,20},{8,24},{12,28},{16,0},{20,4},{24,8},{28,12},{1,17},{... | collective-permute-start | bytes 20 | tf_op jit(solution)/shard_map/ppermute | solution.py:41
  180.7 1.2 collective-permute-start.17
  182.5 3.6 collective-permute-start.18
  196.3 27.2 %collective-permute-start.19 = (bf16[72,8192]{1,0:T(8,128)(2,1)S(1)}, bf16[72,8192]{1,0:T(8,128)(2,1)S(1)}, u32[]{:S(2)}, u32[]{:S(2)}) collective-permute-start(bf16[72,8192]{1,0:T(8,128)(2,1)S(1)} %get-tuple-element.22), channel_id=1, source_target_pairs={{0,8},{8,16},{16,24},{24,28},{28,20},{20,12},{12,4},{4,0},{1,9},{9... | collective-permute-start | bytes 3538952 | tf_op jit(solution)/shard_map/ppermute | solution.py:124
  198.0 27.1 %collective-permute-start.26 = (bf16[72,8192]{1,0:T(8,128)(2,1)S(1)}, bf16[72,8192]{1,0:T(8,128)(2,1)S(1)}, u32[]{:S(2)}, u32[]{:S(2)}) collective-permute-start(bf16[72,8192]{1,0:T(8,128)(2,1)S(1)} %get-tuple-element.23), channel_id=1, source_target_pairs={{8,0},{16,8},{24,16},{28,24},{20,28},{12,20},{4,12},{0,4},{9,1},{1... | collective-permute-start | bytes 3538952 | tf_op jit(solution)/shard_map/ppermute | solution.py:125
  223.5 26.2 %collective-permute-start.20 = (bf16[72,8192]{1,0:T(8,128)(2,1)S(1)}, bf16[72,8192]{1,0:T(8,128)(2,1)S(1)}, u32[]{:S(2)}, u32[]{:S(2)}) collective-permute-start(bf16[72,8192]{1,0:T(8,128)(2,1)S(1)} %collective-permute-done.19), channel_id=1, source_target_pairs={{0,8},{8,16},{16,24},{24,28},{28,20},{20,12},{12,4},{4,0},{1,9},{9... | collective-permute-start | bytes 3538952 | tf_op jit(solution)/shard_map/ppermute | solution.py:124
  225.1 26.5 %collective-permute-start.27 = (bf16[72,8192]{1,0:T(8,128)(2,1)S(1)}, bf16[72,8192]{1,0:T(8,128)(2,1)S(1)}, u32[]{:S(2)}, u32[]{:S(2)}) collective-permute-start(bf16[72,8192]{1,0:T(8,128)(2,1)S(1)} %collective-permute-done.26), channel_id=1, source_target_pairs={{8,0},{16,8},{24,16},{28,24},{20,28},{12,20},{4,12},{0,4},{9,1},{1... | collective-permute-start | bytes 3538952 | tf_op jit(solution)/shard_map/ppermute | solution.py:125
  249.7 26.1 %collective-permute-start.21 = (bf16[72,8192]{1,0:T(8,128)(2,1)S(1)}, bf16[72,8192]{1,0:T(8,128)(2,1)S(1)}, u32[]{:S(2)}, u32[]{:S(2)}) collective-permute-start(bf16[72,8192]{1,0:T(8,128)(2,1)S(1)} %collective-permute-done.20), channel_id=1, source_target_pairs={{0,8},{8,16},{16,24},{24,28},{28,20},{20,12},{12,4},{4,0},{1,9},{9... | collective-permute-start | bytes 3538952 | tf_op jit(solution)/shard_map/ppermute | solution.py:124
  251.6 26.1 %collective-permute-start.28 = (bf16[72,8192]{1,0:T(8,128)(2,1)S(1)}, bf16[72,8192]{1,0:T(8,128)(2,1)S(1)}, u32[]{:S(2)}, u32[]{:S(2)}) collective-permute-start(bf16[72,8192]{1,0:T(8,128)(2,1)S(1)} %collective-permute-done.27), channel_id=1, source_target_pairs={{8,0},{16,8},{24,16},{28,24},{20,28},{12,20},{4,12},{0,4},{9,1},{1... | collective-permute-start | bytes 3538952 | tf_op jit(solution)/shard_map/ppermute | solution.py:125
  275.8 26.1 %collective-permute-start.22 = (bf16[72,8192]{1,0:T(8,128)(2,1)S(1)}, bf16[72,8192]{1,0:T(8,128)(2,1)S(1)}, u32[]{:S(2)}, u32[]{:S(2)}) collective-permute-start(bf16[72,8192]{1,0:T(8,128)(2,1)S(1)} %collective-permute-done.21), channel_id=1, source_target_pairs={{0,8},{8,16},{16,24},{24,28},{28,20},{20,12},{12,4},{4,0},{1,9},{9... | collective-permute-start | bytes 3538952 | tf_op jit(solution)/shard_map/ppermute | solution.py:124
  277.7 26.1 %collective-permute-start.29 = (bf16[72,8192]{1,0:T(8,128)(2,1)S(1)}, bf16[72,8192]{1,0:T(8,128)(2,1)S(1)}, u32[]{:S(2)}, u32[]{:S(2)}) collective-permute-start(bf16[72,8192]{1,0:T(8,128)(2,1)S(1)} %collective-permute-done.28), channel_id=1, source_target_pairs={{8,0},{16,8},{24,16},{28,24},{20,28},{12,20},{4,12},{0,4},{9,1},{1... | collective-permute-start | bytes 3538952 | tf_op jit(solution)/shard_map/ppermute | solution.py:125
  301.9 26.1 %collective-permute-start.23 = (bf16[72,8192]{1,0:T(8,128)(2,1)S(1)}, bf16[72,8192]{1,0:T(8,128)(2,1)S(1)}, u32[]{:S(2)}, u32[]{:S(2)}) collective-permute-start(bf16[72,8192]{1,0:T(8,128)(2,1)S(1)} %collective-permute-done.22), channel_id=1, source_target_pairs={{0,8},{8,16},{16,24},{24,28},{28,20},{20,12},{12,4},{4,0},{1,9},{9... | collective-permute-start | bytes 3538952 | tf_op jit(solution)/shard_map/ppermute | solution.py:124
  303.9 26.2 %collective-permute-start.30 = (bf16[72,8192]{1,0:T(8,128)(2,1)S(1)}, bf16[72,8192]{1,0:T(8,128)(2,1)S(1)}, u32[]{:S(2)}, u32[]{:S(2)}) collective-permute-start(bf16[72,8192]{1,0:T(8,128)(2,1)S(1)} %collective-permute-done.29), channel_id=1, source_target_pairs={{8,0},{16,8},{24,16},{28,24},{20,28},{12,20},{4,12},{0,4},{9,1},{1... | collective-permute-start | bytes 3538952 | tf_op jit(solution)/shard_map/ppermute | solution.py:125
  328.1 26.1 %collective-permute-start.24 = (bf16[72,8192]{1,0:T(8,128)(2,1)S(1)}, bf16[72,8192]{1,0:T(8,128)(2,1)S(1)}, u32[]{:S(2)}, u32[]{:S(2)}) collective-permute-start(bf16[72,8192]{1,0:T(8,128)(2,1)S(1)} %collective-permute-done.23), channel_id=1, source_target_pairs={{0,8},{8,16},{16,24},{24,28},{28,20},{20,12},{12,4},{4,0},{1,9},{9... | collective-permute-start | bytes 3538952 | tf_op jit(solution)/shard_map/ppermute | solution.py:124
  330.1 26.1 %collective-permute-start.31 = (bf16[72,8192]{1,0:T(8,128)(2,1)S(1)}, bf16[72,8192]{1,0:T(8,128)(2,1)S(1)}, u32[]{:S(2)}, u32[]{:S(2)}) collective-permute-start(bf16[72,8192]{1,0:T(8,128)(2,1)S(1)} %collective-permute-done.30), channel_id=1, source_target_pairs={{8,0},{16,8},{24,16},{28,24},{20,28},{12,20},{4,12},{0,4},{9,1},{1... | collective-permute-start | bytes 3538952 | tf_op jit(solution)/shard_map/ppermute | solution.py:125
  354.2 21.9 %collective-permute-start.25 = (bf16[72,8192]{1,0:T(8,128)(2,1)S(1)}, bf16[72,8192]{1,0:T(8,128)(2,1)S(1)}, u32[]{:S(2)}, u32[]{:S(2)}) collective-permute-start(bf16[72,8192]{1,0:T(8,128)(2,1)S(1)} %collective-permute-done.24), channel_id=1, source_target_pairs={{0,8},{8,16},{16,24},{24,28},{28,20},{20,12},{12,4},{4,0},{1,9},{9... | collective-permute-start | bytes 3538952 | tf_op jit(solution)/shard_map/ppermute | solution.py:124
  356.2 21.5 %collective-permute-start.32 = (bf16[72,8192]{1,0:T(8,128)(2,1)S(1)}, bf16[72,8192]{1,0:T(8,128)(2,1)S(1)}, u32[]{:S(2)}, u32[]{:S(2)}) collective-permute-start(bf16[72,8192]{1,0:T(8,128)(2,1)S(1)} %collective-permute-done.31), channel_id=1, source_target_pairs={{8,0},{16,8},{24,16},{28,24},{20,28},{12,20},{4,12},{0,4},{9,1},{1... | collective-permute-start | bytes 3538952 | tf_op jit(solution)/shard_map/ppermute | solution.py:125
where the time goes:
time: 391 us; the launch traced here: 385 us
  waiting for transfers between devices  205 us (52%)
  between operations  48.3 us (12%)
  starting transfers between devices  42.7 us (11%)
  matrix products  31.5 us (8%)
  other arithmetic  31.2 us (8%)
  local copies, waits for them, and re-layouts  26.5 us (7%)
    ppermute x7, waiting for transfers between devices, on_device(): send_a = lax.ppermute(send_a, 'dp', fwd)  124 us
    ppermute x7, waiting for transfers between devices, on_device(): got_a = lax.ppermute(send_a, 'dp', fwd)  72.4 us
    dot_general x32, matrix products, spread(): return jnp.dot(cols, chunk, preferred_element_type=kind)  23.2 us
    ppermute x7, starting transfers between devices, on_device(): got_a = lax.ppermute(send_a, 'dp', fwd)  12.9 us
    ppermute x5, starting transfers between devices, all_sum(): v = v + lax.ppermute(v, axis, [(i, i ^ k) for i in range(n)])  11.5 us
    unnamed x15, local copies, waits for them, and re-layouts  11.5 us
    ppermute x7, starting transfers between devices, on_device(): send_a = lax.ppermute(send_a, 'dp', fwd)  11.2 us
    slice x1, local copies, waits for them, and re-layouts, on_device(): left, right = (by_owner[..., :half], by_owner[..., half:])  9.36 us
  transfers between devices with their start and end apart: 33, of which 23 were waited for; matrix products, arithmetic and copies ran while one was open for 12% of the time, Pallas kernels for 0%

commit v1 on v0

--- a/solution.py
+++ b/solution.py
@@ -57,37 +57,36 @@
         per_rank = nseg // n
         half = seg // 2
         me = lax.axis_index("dp")
-        rank_at = jnp.array(ring, jnp.int32)
         mypos = jnp.array(pos_of, jnp.int32)[me]
+
+        warm = jnp.zeros((8, 128), jnp.bfloat16)
+        warm = lax.ppermute(warm, "dp", fwd) + lax.ppermute(warm, "dp", bwd)
 
         position = jnp.arange(nseg, dtype=jnp.int32)
         same_owner = (owner_list[:, None] == owner_list[None, :]) & (position[None, :] < position[:, None])
         within = jnp.sum(same_owner.astype(jnp.int32), axis=1)
-        slot = owner_list * cap + within
+        ahead = (jnp.array(pos_of, jnp.int32)[owner_list] - mypos + n) % n
+        slot = ahead * cap + within
         hit = jnp.arange(n * cap, dtype=jnp.int32)[:, None] == slot[None, :]
-        valid = jnp.any(hit, axis=1)
+        valid = jnp.any(hit[:cap], axis=1)
         placing = hit.astype(local_grad.dtype)
-        by_owner = jnp.dot(placing, local_grad, preferred_element_type=jnp.bfloat16).reshape(n, cap, seg)
-        left, right = by_owner[..., :half], by_owner[..., half:]
+        left = jnp.dot(placing, local_grad[:, :half], preferred_element_type=jnp.bfloat16).reshape(n, cap, half)
+        right = jnp.dot(placing, local_grad[:, half:], preferred_element_type=jnp.bfloat16).reshape(n, cap, half)
 
-        def own(x, p):
-            return lax.dynamic_index_in_dim(x, rank_at[p % n], 0, keepdims=False).astype(jnp.float32)
-
-        send_a = own(left, mypos - 1 + n).astype(jnp.bfloat16)
-        send_b = own(right, mypos + 1).astype(jnp.bfloat16)
+        send_a = left[n - 1] + warm[:1, :1]
+        send_b = right[1]
         for t in range(n - 1):
             got_a = lax.ppermute(send_a, "dp", fwd)
             got_b = lax.ppermute(send_b, "dp", bwd)
-            acc_a = got_a.astype(jnp.float32) + own(left, mypos - 2 - t + 2 * n)
-            acc_b = got_b.astype(jnp.float32) + own(right, mypos + 2 + t)
+            acc_a = got_a.astype(jnp.float32) + left[(2 * n - 2 - t) % n].astype(jnp.float32)
+            acc_b = got_b.astype(jnp.float32) + right[(2 + t) % n].astype(jnp.float32)
             if t < n - 2:
                 send_a, send_b = acc_a.astype(jnp.bfloat16), acc_b.astype(jnp.bfloat16)
         owned = jnp.concatenate([acc_a, acc_b], axis=1)
 
         total_sq = all_sum(all_sum(jnp.sum(owned * owned).reshape(1, 1), "dp", n), "mp", blocks)[0, 0]
         clip_factor = jnp.minimum(1.0, math.sqrt(blocks * nseg * seg) / (jnp.sqrt(total_sq) + 1e-06))
-        in_use = lax.dynamic_index_in_dim(valid.reshape(n, cap), me, 0, keepdims=False)
-        in_use = in_use.astype(jnp.float32)[:, None]
+        in_use = valid.astype(jnp.float32)[:, None]
         owned_grad = clip_factor * owned
         new_first = in_use * (0.9 * first_moment[0] + 0.1 * owned_grad)
         new_second = in_use * (0.95 * second_moment[0] + 0.05 * owned_grad * owned_grad)
@@ -104,26 +103,25 @@
         placing_t = placing.T
         mine_t = lax.dynamic_slice_in_dim(placing_t, me * per_rank, per_rank, 0)
 
-        def spread(rows_t, chunk, p, kind):
-            cols = lax.dynamic_slice_in_dim(rows_t, rank_at[p % n] * cap, cap, 1)
-            return jnp.dot(cols, chunk, preferred_element_type=kind)
+        def spread(rows_t, chunk, k, kind):
+            return jnp.dot(rows_t[:, k * cap:(k + 1) * cap], chunk, preferred_element_type=kind)
 
-        def place(acc, p_a, a, p_b, b):
+        def place(acc, k_a, a, k_b, b):
             parts = (
-                spread(placing_t, a[:cap], p_a, jnp.bfloat16),
-                spread(placing_t, b[:cap], p_b, jnp.bfloat16),
-                spread(mine_t, a[cap:], p_a, jnp.float32),
-                spread(mine_t, b[cap:], p_b, jnp.float32),
+                spread(placing_t, a[:cap], k_a, jnp.bfloat16),
+                spread(placing_t, b[:cap], k_b, jnp.bfloat16),
+                spread(mine_t, a[cap:], k_a, jnp.float32),
+                spread(mine_t, b[cap:], k_b, jnp.float32),
             )
             if acc is None:
                 return parts
             return tuple(x + y for x, y in zip(acc, parts))
 
-        acc = place(None, mypos, send_a, mypos, send_b)
+        acc = place(None, 0, send_a, 0, send_b)
         for t in range(n - 1):
             send_a = lax.ppermute(send_a, "dp", fwd)
             send_b = lax.ppermute(send_b, "dp", bwd)
-            acc = place(acc, mypos - 1 - t + n, send_a, mypos + 1 + t, send_b)
+            acc = place(acc, n - 1 - t, send_a, 1 + t, send_b)
         new_params = jnp.concatenate([acc[0], acc[1]], axis=1)
         average_rows = jnp.concatenate([acc[2], acc[3]], axis=1)
         return (

time: 391 us -> 350 us (0.90)
  between operations: 48.3 us -> 5.15 us
  waiting for transfers between devices: 205 us -> 216 us
  local copies, waits for them, and re-layouts: 26.5 us -> 15.7 us
    ppermute x7, waiting for transfers between devices: 0.94 us -> 52.2 us  [on_device(): got_b = lax.ppermute(send_b, 'dp', bwd)]
    ppermute x7, waiting for transfers between devices: 72.4 us -> 30.9 us  [on_device(): got_a = lax.ppermute(send_a, 'dp', fwd)]
    slice x1 -> x2, local copies, waits for them, and re-layouts: 9.36 us -> 0.67 us  [the longest x1 0.51 us: on_device(): send_a = left[n - 1] + warm[:1, :1]]
    ppermute x7, starting transfers between devices: 12.9 us -> 4.51 us  [on_device(): got_a = lax.ppermute(send_a, 'dp', fwd)]
    ppermute x7, starting transfers between devices: 3.36 us -> 9.4 us  [on_device(): got_b = lax.ppermute(send_b, 'dp', bwd)]
    dot_general x33 -> x34, matrix products: 31.5 us -> 28.8 us  [the longest x32 21.8 us: spread(): jnp.dot(rows_t[:, k * cap:(k + 1) * cap], chunk, preferred_element_type=k...]
    unnamed x15 -> x19, local copies, waits for them, and re-layouts: 11.5 us -> 13.7 us
  transfers between devices with their start and end apart: 33 -> 35, of which waited for: 23 -> 31; matrix products, arithmetic and copies ran while one was open for 12% -> 17% of each run, Pallas kernels for 0% -> 0%
where the time goes in v1:
time: 350 us; the launch traced here: 343 us
  waiting for transfers between devices  216 us (62%)
  starting transfers between devices  43.2 us (12%)
  other arithmetic  34.8 us (10%)
  matrix products  28.8 us (8%)
  local copies, waits for them, and re-layouts  15.7 us (4%)
  between operations  5.15 us (1%)
    ppermute x7, waiting for transfers between devices, on_device(): send_a = lax.ppermute(send_a, 'dp', fwd)  125 us
    ppermute x7, waiting for transfers between devices, on_device(): got_b = lax.ppermute(send_b, 'dp', bwd)  52.2 us
    ppermute x7, waiting for transfers between devices, on_device(): got_a = lax.ppermute(send_a, 'dp', fwd)  30.9 us
    dot_general x32, matrix products, spread(): jnp.dot(rows_t[:, k * cap:(k + 1) * cap], chunk, preferred_element_type=k...  21.8 us
    unnamed x19, local copies, waits for them, and re-layouts  13.7 us
    ppermute x5, starting transfers between devices, all_sum(): v = v + lax.ppermute(v, axis, [(i, i ^ k) for i in range(n)])  11.4 us
    ppermute x7, starting transfers between devices, on_device(): got_b = lax.ppermute(send_b, 'dp', bwd)  9.4 us
    another operation x1, other arithmetic  9.09 us
  transfers between devices with their start and end apart: 35, of which 31 were waited for; matrix products, arithmetic and copies ran while one was open for 17% of the time, Pallas kernels for 0%

profile of v1, /device:TPU:0, one launch (start us, length us, event | category | flops | bytes accessed | tf_op | source)
XLA Modules:
  0.0 343.4 jit_solution(10566355120284449105)
XLA Ops:
  0.6 3.0 collective-permute-start.1
  4.7 1.2 dynamic_slice.6
  6.0 1.3 fusion.90
  7.3 3.4 fusion
  10.8 2.2 copy-done.1
  13.1 2.0 collective-permute-start.9
  15.2 3.6 %fusion.2 = bf16[288,8192]{1,0:T(8,128)(2,1)} fusion(bf16[192,16384]{1,0:T(8,128)(2,1)S(1)} %bitcast.46, s32[192]{0:T(256)S(1)} %fusion.90), kind=kOutput, calls=%fused_computation.33 | convolution fusion | flops 906024960 | bytes 7865344 | tf_op jit(solution)/shard_map/dot_general | solution.py:73
  19.6 2.0 slice_add_fusion
  21.8 7.6 %collective-permute-done.9 = bf16[36,8192]{1,0:T(8,128)(2,1)S(1)} collective-permute-done((bf16[36,8192]{1,0:T(8,128)(2,1)S(1)}, bf16[36,8192]{1,0:T(8,128)(2,1)S(1)}, u32[]{:S(2)}, u32[]{:S(2)}) %collective-permute-start.9) | collective-permute-done | bytes 589856 | tf_op jit(solution)/shard_map/ppermute | solution.py:80
  29.3 1.2 add_convert_fusion.5
  30.6 1.7 collective-permute-start.10
  32.3 5.0 %collective-permute-done.2 = bf16[36,8192]{1,0:T(8,128)(2,1)S(1)} collective-permute-done((bf16[36,8192]{1,0:T(8,128)(2,1)S(1)}, bf16[36,8192]{1,0:T(8,128)(2,1)S(1)}, u32[]{:S(2)}, u32[]{:S(2)}) %collective-permute-start.2) | collective-permute-done | bytes 589856 | tf_op jit(solution)/shard_map/ppermute | solution.py:79
  37.3 1.2 add_convert_fusion.11
  39.0 6.9 %collective-permute-done.10 = bf16[36,8192]{1,0:T(8,128)(2,1)S(1)} collective-permute-done((bf16[36,8192]{1,0:T(8,128)(2,1)S(1)}, bf16[36,8192]{1,0:T(8,128)(2,1)S(1)}, u32[]{:S(2)}, u32[]{:S(2)}) %collective-permute-start.10) | collective-permute-done | bytes 589856 | tf_op jit(solution)/shard_map/ppermute | solution.py:80
  45.9 1.4 add_convert_fusion.4
  47.3 1.4 collective-permute-start.11
  48.7 4.6 %collective-permute-done.3 = bf16[36,8192]{1,0:T(8,128)(2,1)S(1)} collective-permute-done((bf16[36,8192]{1,0:T(8,128)(2,1)S(1)}, bf16[36,8192]{1,0:T(8,128)(2,1)S(1)}, u32[]{:S(2)}, u32[]{:S(2)}) %collective-permute-start.3) | collective-permute-done | bytes 589856 | tf_op jit(solution)/shard_map/ppermute | solution.py:79
  54.3 7.5 %collective-permute-done.11 = bf16[36,8192]{1,0:T(8,128)(2,1)S(1)} collective-permute-done((bf16[36,8192]{1,0:T(8,128)(2,1)S(1)}, bf16[36,8192]{1,0:T(8,128)(2,1)S(1)}, u32[]{:S(2)}, u32[]{:S(2)}) %collective-permute-start.11) | collective-permute-done | bytes 589856 | tf_op jit(solution)/shard_map/ppermute | solution.py:80
  61.7 1.2 add_convert_fusion.3
  64.1 4.2 %collective-permute-done.4 = bf16[36,8192]{1,0:T(8,128)(2,1)S(1)} collective-permute-done((bf16[36,8192]{1,0:T(8,128)(2,1)S(1)}, bf16[36,8192]{1,0:T(8,128)(2,1)S(1)}, u32[]{:S(2)}, u32[]{:S(2)}) %collective-permute-start.4) | collective-permute-done | bytes 589856 | tf_op jit(solution)/shard_map/ppermute | solution.py:79
  69.2 8.5 %collective-permute-done.12 = bf16[36,8192]{1,0:T(8,128)(2,1)S(1)} collective-permute-done((bf16[36,8192]{1,0:T(8,128)(2,1)S(1)}, bf16[36,8192]{1,0:T(8,128)(2,1)S(1)}, u32[]{:S(2)}, u32[]{:S(2)}) %collective-permute-start.12) | collective-permute-done | bytes 589856 | tf_op jit(solution)/shard_map/ppermute | solution.py:80
  79.0 4.1 %collective-permute-done.5 = bf16[36,8192]{1,0:T(8,128)(2,1)S(1)} collective-permute-done((bf16[36,8192]{1,0:T(8,128)(2,1)S(1)}, bf16[36,8192]{1,0:T(8,128)(2,1)S(1)}, u32[]{:S(2)}, u32[]{:S(2)}) %collective-permute-start.5) | collective-permute-done | bytes 589856 | tf_op jit(solution)/shard_map/ppermute | solution.py:79
  84.1 8.6 %collective-permute-done.13 = bf16[36,8192]{1,0:T(8,128)(2,1)S(1)} collective-permute-done((bf16[36,8192]{1,0:T(8,128)(2,1)S(1)}, bf16[36,8192]{1,0:T(8,128)(2,1)S(1)}, u32[]{:S(2)}, u32[]{:S(2)}) %collective-permute-start.13) | collective-permute-done | bytes 589856 | tf_op jit(solution)/shard_map/ppermute | solution.py:80
  93.9 4.2 %collective-permute-done.6 = bf16[36,8192]{1,0:T(8,128)(2,1)S(1)} collective-permute-done((bf16[36,8192]{1,0:T(8,128)(2,1)S(1)}, bf16[36,8192]{1,0:T(8,128)(2,1)S(1)}, u32[]{:S(2)}, u32[]{:S(2)}) %collective-permute-start.6) | collective-permute-done | bytes 589856 | tf_op jit(solution)/shard_map/ppermute | solution.py:79
  99.0 8.5 %collective-permute-done.14 = bf16[36,8192]{1,0:T(8,128)(2,1)S(1)} collective-permute-done((bf16[36,8192]{1,0:T(8,128)(2,1)S(1)}, bf16[36,8192]{1,0:T(8,128)(2,1)S(1)}, u32[]{:S(2)}, u32[]{:S(2)}) %collective-permute-start.14) | collective-permute-done | bytes 589856 | tf_op jit(solution)/shard_map/ppermute | solution.py:80
  108.8 3.9 %collective-permute-done.7 = bf16[36,8192]{1,0:T(8,128)(2,1)S(1)} collective-permute-done((bf16[36,8192]{1,0:T(8,128)(2,1)S(1)}, bf16[36,8192]{1,0:T(8,128)(2,1)S(1)}, u32[]{:S(2)}, u32[]{:S(2)}) %collective-permute-start.7) | collective-permute-done | bytes 589856 | tf_op jit(solution)/shard_map/ppermute | solution.py:79
  113.9 4.7 %collective-permute-done.15 = bf16[36,8192]{1,0:T(8,128)(2,1)S(1)} collective-permute-done((bf16[36,8192]{1,0:T(8,128)(2,1)S(1)}, bf16[36,8192]{1,0:T(8,128)(2,1)S(1)}, u32[]{:S(2)}, u32[]{:S(2)}) %collective-permute-start.15) | collective-permute-done | bytes 589856 | tf_op jit(solution)/shard_map/ppermute | solution.py:80
  118.8 4.9 %collective-permute-done.8 = bf16[36,8192]{1,0:T(8,128)(2,1)S(1)} collective-permute-done((bf16[36,8192]{1,0:T(8,128)(2,1)S(1)}, bf16[36,8192]{1,0:T(8,128)(2,1)S(1)}, u32[]{:S(2)}, u32[]{:S(2)}) %collective-permute-start.8) | collective-permute-done | bytes 589856 | tf_op jit(solution)/shard_map/ppermute | solution.py:79
  123.9 1.3 multiply_reduce_fusion
  125.2 1.6 collective-permute-start.16
  126.8 2.2 collective-permute-done.16
  130.3 2.5 collective-permute-start.17
  134.6 3.5 %collective-permute-start.18 = (f32[1,1]{1,0:T(1,128)}, f32[1,1]{1,0:T(1,128)}, u32[]{:S(2)}, u32[]{:S(2)}) collective-permute-start(f32[1,1]{1,0:T(1,128)} %add.249), channel_id=1, source_target_pairs={{0,16},{4,20},{8,24},{12,28},{16,0},{20,4},{24,8},{28,12},{1,17},{... | collective-permute-start | bytes 20 | tf_op jit(solution)/shard_map/ppermute | solution.py:41
  141.8 2.9 collective-permute-start.20
  146.2 9.1 %fusion.14 = (bf16[36,16384]{1,0:T(8,128)(2,1)S(1)}, bf16[36,16384]{1,0:T(8,128)(2,1)S(1)}) fusion(f32[1,36,16384]{2,0,1:T(1,128)S(1)} %copy-done.7, f32[1,36,16384]{2,0,1:T(1,128)S(1)} %copy-done.3, f32[36,8192]{1,0:T(8,128)S(1)} %get-tuple-element.23, f32[36,8192]{1,0:T(8,128)S(1)} %get-tuple-element.21, f32[]{:T(128)} %bitcast.5, ...), kind=kLoop, calls=%fused_computation.50 | loop fusion | flops 14745600 | bytes 14155924 | tf_op jit(solution)/shard_map/convert.1
  157.8 7.8 %subtract_multiply_fusion = (f32[1,36,16384]{2,1,0:T(8,128)S(1)}, f32[1,36,16384]{2,1,0:T(8,128)S(1)}, f32[1,36,16384]{2,1,0:T(8,128)S(1)}) fusion(f32[1,36,16384]{2,0,1:T(1,128)S(1)} %copy-done.5, f32[36]{0:T(128)S(1)} %convert_element_type.133, f32[1,36,8192]{2,1,0:T(8,128)S(1)} %get-tuple-element.22, f32[1,36,8192]{2,1,0:T(8,128)S(1)} %get-tuple-element.20, ...), kind=kLoop, calls=%fused_computation.57 | loop fusion | flops 11796480 | bytes 16515220 | tf_op jit(solution)/shard_map/mul | solution.py:96
  165.6 3.8 %copy.26 = f32[1,36,16384]{2,0,1:T(1,128)} copy(f32[1,36,16384]{2,1,0:T(8,128)S(1)} %get-tuple-element.15) | data formatting | bytes 4718592
  169.5 3.8 %copy.27 = f32[1,36,16384]{2,0,1:T(1,128)} copy(f32[1,36,16384]{2,1,0:T(8,128)S(1)} %get-tuple-element.16) | data formatting | bytes 4718592
  173.3 3.8 %copy.28 = f32[1,36,16384]{2,0,1:T(1,128)} copy(f32[1,36,16384]{2,1,0:T(8,128)S(1)} %get-tuple-element.17) | data formatting | bytes 4718592
  179.7 2.8 collective-permute-done.21
  187.6 21.1 %collective-permute-done.22 = bf16[72,8192]{1,0:T(8,128)(2,1)S(1)} collective-permute-done((bf16[72,8192]{1,0:T(8,128)(2,1)S(1)}, bf16[72,8192]{1,0:T(8,128)(2,1)S(1)}, u32[]{:S(2)}, u32[]{:S(2)}) %collective-permute-start.22) | collective-permute-done | bytes 1179680 | tf_op jit(solution)/shard_map/ppermute | solution.py:122
  213.6 21.2 %collective-permute-done.23 = bf16[72,8192]{1,0:T(8,128)(2,1)S(1)} collective-permute-done((bf16[72,8192]{1,0:T(8,128)(2,1)S(1)}, bf16[72,8192]{1,0:T(8,128)(2,1)S(1)}, u32[]{:S(2)}, u32[]{:S(2)}) %collective-permute-start.23) | collective-permute-done | bytes 1179680 | tf_op jit(solution)/shard_map/ppermute | solution.py:122
  239.7 21.2 %collective-permute-done.24 = bf16[72,8192]{1,0:T(8,128)(2,1)S(1)} collective-permute-done((bf16[72,8192]{1,0:T(8,128)(2,1)S(1)}, bf16[72,8192]{1,0:T(8,128)(2,1)S(1)}, u32[]{:S(2)}, u32[]{:S(2)}) %collective-permute-start.24) | collective-permute-done | bytes 1179680 | tf_op jit(solution)/shard_map/ppermute | solution.py:122
  265.9 21.2 %collective-permute-done.25 = bf16[72,8192]{1,0:T(8,128)(2,1)S(1)} collective-permute-done((bf16[72,8192]{1,0:T(8,128)(2,1)S(1)}, bf16[72,8192]{1,0:T(8,128)(2,1)S(1)}, u32[]{:S(2)}, u32[]{:S(2)}) %collective-permute-start.25) | collective-permute-done | bytes 1179680 | tf_op jit(solution)/shard_map/ppermute | solution.py:122
  292.2 21.1 %collective-permute-done.26 = bf16[72,8192]{1,0:T(8,128)(2,1)S(1)} collective-permute-done((bf16[72,8192]{1,0:T(8,128)(2,1)S(1)}, bf16[72,8192]{1,0:T(8,128)(2,1)S(1)}, u32[]{:S(2)}, u32[]{:S(2)}) %collective-permute-start.26) | collective-permute-done | bytes 1179680 | tf_op jit(solution)/shard_map/ppermute | solution.py:122
  318.1 16.7 %collective-permute-done.27 = bf16[72,8192]{1,0:T(8,128)(2,1)S(1)} collective-permute-done((bf16[72,8192]{1,0:T(8,128)(2,1)S(1)}, bf16[72,8192]{1,0:T(8,128)(2,1)S(1)}, u32[]{:S(2)}, u32[]{:S(2)}) %collective-permute-start.27) | collective-permute-done | bytes 1179680 | tf_op jit(solution)/shard_map/ppermute | solution.py:122
  336.6 1.2 maximum_bitcast_fusion.1
  339.9 3.3 maximum_bitcast_fusion
  (108 shorter events, 56.2 us)
Async XLA Ops:
  0.6 18.4 %collective-permute-start.1 = (bf16[8,128]{1,0:T(8,128)(2,1)S(1)}, bf16[8,128]{1,0:T(8,128)(2,1)S(1)}, u32[]{:S(2)}, u32[]{:S(2)}) collective-permute-start(bf16[8,128]{1,0:T(8,128)(2,1)S(1)} %broadcast_in_dim.9), channel_id=1, source_target_pairs={{8,0},{16,8},{24,16},{28,24},{20,28},{12,20},{4,12},{0,4},{9,1},{1... | collective-permute-start | bytes 6152 | tf_op jit(solution)/shard_map/ppermute | solution.py:63
  3.7 15.4 %collective-permute-start = (bf16[8,128]{1,0:T(8,128)(2,1)S(1)}, bf16[8,128]{1,0:T(8,128)(2,1)S(1)}, u32[]{:S(2)}, u32[]{:S(2)}) collective-permute-start(bf16[8,128]{1,0:T(8,128)(2,1)S(1)} %broadcast_in_dim.9), channel_id=1, source_target_pairs={{0,8},{8,16},{16,24},{24,28},{28,20},{20,12},{12,4},{4,0},{1,9},{9... | collective-permute-start | bytes 6152 | tf_op jit(solution)/shard_map/ppermute | solution.py:63
  7.3 7.9 %copy-start.6 = (bf16[1,1,192,16384]{3,2,1,0:T(8,128)(2,1)S(1)}, bf16[1,1,192,16384]{3,2,1,0:T(8,128)(2,1)}, u32[]{:S(2)}) copy-start(bf16[1,1,192,16384]{3,2,1,0:T(8,128)(2,1)} %param.8) | copy-start | bytes 18874372
  10.8 2.2 copy-start.1
  13.1 16.2 %collective-permute-start.9 = (bf16[36,8192]{1,0:T(8,128)(2,1)S(1)}, bf16[36,8192]{1,0:T(8,128)(2,1)S(1)}, u32[]{:S(2)}, u32[]{:S(2)}) collective-permute-start(bf16[36,8192]{1,0:T(8,128)(2,1)S(1)} %slice.341), channel_id=1, source_target_pairs={{8,0},{16,8},{24,16},{28,24},{20,28},{12,20},{4,12},{0,4},{9,1},{1... | collective-permute-start | bytes 1769480 | tf_op jit(solution)/shard_map/ppermute | solution.py:80
  21.6 31.7 %copy-start = (bf16[288,8192]{1,0:T(8,128)(2,1)S(1)}, bf16[288,8192]{1,0:T(8,128)(2,1)}, u32[]{:S(2)}) copy-start(bf16[288,8192]{1,0:T(8,128)(2,1)} %fusion.2) | copy-start | bytes 14155780
  21.6 15.7 %collective-permute-start.2 = (bf16[36,8192]{1,0:T(8,128)(2,1)S(1)}, bf16[36,8192]{1,0:T(8,128)(2,1)S(1)}, u32[]{:S(2)}, u32[]{:S(2)}) collective-permute-start(bf16[36,8192]{1,0:T(8,128)(2,1)S(1)} %slice_add_fusion), channel_id=1, source_target_pairs={{0,8},{8,16},{16,24},{24,28},{28,20},{20,12},{12,4},{4,0},{1,9},{9... | collective-permute-start | bytes 1769480 | tf_op jit(solution)/shard_map/ppermute | solution.py:79
  30.6 15.3 %collective-permute-start.10 = (bf16[36,8192]{1,0:T(8,128)(2,1)S(1)}, bf16[36,8192]{1,0:T(8,128)(2,1)S(1)}, u32[]{:S(2)}, u32[]{:S(2)}) collective-permute-start(bf16[36,8192]{1,0:T(8,128)(2,1)S(1)} %add_convert_fusion.5), channel_id=1, source_target_pairs={{8,0},{16,8},{24,16},{28,24},{20,28},{12,20},{4,12},{0,4},{9,1},{1... | collective-permute-start | bytes 1769480 | tf_op jit(solution)/shard_map/ppermute | solution.py:80
  38.5 14.8 %collective-permute-start.3 = (bf16[36,8192]{1,0:T(8,128)(2,1)S(1)}, bf16[36,8192]{1,0:T(8,128)(2,1)S(1)}, u32[]{:S(2)}, u32[]{:S(2)}) collective-permute-start(bf16[36,8192]{1,0:T(8,128)(2,1)S(1)} %add_convert_fusion.11), channel_id=1, source_target_pairs={{0,8},{8,16},{16,24},{24,28},{28,20},{20,12},{12,4},{4,0},{1,9},{9... | collective-permute-start | bytes 1769480 | tf_op jit(solution)/shard_map/ppermute | solution.py:79
  47.3 30.3 %copy-start.2 = (bf16[288,8192]{1,0:T(8,128)(2,1)S(1)}, bf16[288,8192]{1,0:T(8,128)(2,1)}, u32[]{:S(2)}) copy-start(bf16[288,8192]{1,0:T(8,128)(2,1)} %copy-done.1) | copy-start | bytes 14155780
  47.3 14.4 %collective-permute-start.11 = (bf16[36,8192]{1,0:T(8,128)(2,1)S(1)}, bf16[36,8192]{1,0:T(8,128)(2,1)S(1)}, u32[]{:S(2)}, u32[]{:S(2)}) collective-permute-start(bf16[36,8192]{1,0:T(8,128)(2,1)S(1)} %add_convert_fusion.4), channel_id=1, source_target_pairs={{8,0},{16,8},{24,16},{28,24},{20,28},{12,20},{4,12},{0,4},{9,1},{1... | collective-permute-start | bytes 1769480 | tf_op jit(solution)/shard_map/ppermute | solution.py:80
  53.5 14.7 %collective-permute-start.4 = (bf16[36,8192]{1,0:T(8,128)(2,1)S(1)}, bf16[36,8192]{1,0:T(8,128)(2,1)S(1)}, u32[]{:S(2)}, u32[]{:S(2)}) collective-permute-start(bf16[36,8192]{1,0:T(8,128)(2,1)S(1)} %add_convert_fusion.10), channel_id=1, source_target_pairs={{0,8},{8,16},{16,24},{24,28},{28,20},{20,12},{12,4},{4,0},{1,9},{9... | collective-permute-start | bytes 1769480 | tf_op jit(solution)/shard_map/ppermute | solution.py:79
  63.0 14.6 %collective-permute-start.12 = (bf16[36,8192]{1,0:T(8,128)(2,1)S(1)}, bf16[36,8192]{1,0:T(8,128)(2,1)S(1)}, u32[]{:S(2)}, u32[]{:S(2)}) collective-permute-start(bf16[36,8192]{1,0:T(8,128)(2,1)S(1)} %add_convert_fusion.3), channel_id=1, source_target_pairs={{8,0},{16,8},{24,16},{28,24},{20,28},{12,20},{4,12},{0,4},{9,1},{1... | collective-permute-start | bytes 1769480 | tf_op jit(solution)/shard_map/ppermute | solution.py:80
  68.4 14.6 %collective-permute-start.5 = (bf16[36,8192]{1,0:T(8,128)(2,1)S(1)}, bf16[36,8192]{1,0:T(8,128)(2,1)S(1)}, u32[]{:S(2)}, u32[]{:S(2)}) collective-permute-start(bf16[36,8192]{1,0:T(8,128)(2,1)S(1)} %add_convert_fusion.9), channel_id=1, source_target_pairs={{0,8},{8,16},{16,24},{24,28},{28,20},{20,12},{12,4},{4,0},{1,9},{9... | collective-permute-start | bytes 1769480 | tf_op jit(solution)/shard_map/ppermute | solution.py:79
  77.9 14.7 %collective-permute-start.13 = (bf16[36,8192]{1,0:T(8,128)(2,1)S(1)}, bf16[36,8192]{1,0:T(8,128)(2,1)S(1)}, u32[]{:S(2)}, u32[]{:S(2)}) collective-permute-start(bf16[36,8192]{1,0:T(8,128)(2,1)S(1)} %add_convert_fusion.2), channel_id=1, source_target_pairs={{8,0},{16,8},{24,16},{28,24},{20,28},{12,20},{4,12},{0,4},{9,1},{1... | collective-permute-start | bytes 1769480 | tf_op jit(solution)/shard_map/ppermute | solution.py:80
  83.3 14.7 %collective-permute-start.6 = (bf16[36,8192]{1,0:T(8,128)(2,1)S(1)}, bf16[36,8192]{1,0:T(8,128)(2,1)S(1)}, u32[]{:S(2)}, u32[]{:S(2)}) collective-permute-start(bf16[36,8192]{1,0:T(8,128)(2,1)S(1)} %add_convert_fusion.8), channel_id=1, source_target_pairs={{0,8},{8,16},{16,24},{24,28},{28,20},{20,12},{12,4},{4,0},{1,9},{9... | collective-permute-start | bytes 1769480 | tf_op jit(solution)/shard_map/ppermute | solution.py:79
  92.8 14.7 %collective-permute-start.14 = (bf16[36,8192]{1,0:T(8,128)(2,1)S(1)}, bf16[36,8192]{1,0:T(8,128)(2,1)S(1)}, u32[]{:S(2)}, u32[]{:S(2)}) collective-permute-start(bf16[36,8192]{1,0:T(8,128)(2,1)S(1)} %add_convert_fusion.1), channel_id=1, source_target_pairs={{8,0},{16,8},{24,16},{28,24},{20,28},{12,20},{4,12},{0,4},{9,1},{1... | collective-permute-start | bytes 1769480 | tf_op jit(solution)/shard_map/ppermute | solution.py:80
  98.2 14.4 %collective-permute-start.7 = (bf16[36,8192]{1,0:T(8,128)(2,1)S(1)}, bf16[36,8192]{1,0:T(8,128)(2,1)S(1)}, u32[]{:S(2)}, u32[]{:S(2)}) collective-permute-start(bf16[36,8192]{1,0:T(8,128)(2,1)S(1)} %add_convert_fusion.7), channel_id=1, source_target_pairs={{0,8},{8,16},{16,24},{24,28},{28,20},{20,12},{12,4},{4,0},{1,9},{9... | collective-permute-start | bytes 1769480 | tf_op jit(solution)/shard_map/ppermute | solution.py:79
  107.7 10.9 %collective-permute-start.15 = (bf16[36,8192]{1,0:T(8,128)(2,1)S(1)}, bf16[36,8192]{1,0:T(8,128)(2,1)S(1)}, u32[]{:S(2)}, u32[]{:S(2)}) collective-permute-start(bf16[36,8192]{1,0:T(8,128)(2,1)S(1)} %add_convert_fusion), channel_id=1, source_target_pairs={{8,0},{16,8},{24,16},{28,24},{20,28},{12,20},{4,12},{0,4},{9,1},{1... | collective-permute-start | bytes 1769480 | tf_op jit(solution)/shard_map/ppermute | solution.py:80
  112.9 10.9 %collective-permute-start.8 = (bf16[36,8192]{1,0:T(8,128)(2,1)S(1)}, bf16[36,8192]{1,0:T(8,128)(2,1)S(1)}, u32[]{:S(2)}, u32[]{:S(2)}) collective-permute-start(bf16[36,8192]{1,0:T(8,128)(2,1)S(1)} %add_convert_fusion.6), channel_id=1, source_target_pairs={{0,8},{8,16},{16,24},{24,28},{28,20},{20,12},{12,4},{4,0},{1,9},{9... | collective-permute-start | bytes 1769480 | tf_op jit(solution)/shard_map/ppermute | solution.py:79
  118.6 27.6 %copy-start.5 = (f32[1,36,16384]{2,0,1:T(1,128)S(1)}, f32[1,36,16384]{2,0,1:T(1,128)}, u32[]{:S(2)}) copy-start(f32[1,36,16384]{2,0,1:T(1,128)} %param.10) | copy-start | bytes 7077892
  118.6 27.6 %copy-start.7 = (f32[1,36,16384]{2,0,1:T(1,128)S(1)}, f32[1,36,16384]{2,0,1:T(1,128)}, u32[]{:S(2)}) copy-start(f32[1,36,16384]{2,0,1:T(1,128)} %param.13) | copy-start | bytes 7077892
  118.8 27.4 %copy-start.3 = (f32[1,36,16384]{2,0,1:T(1,128)S(1)}, f32[1,36,16384]{2,0,1:T(1,128)}, u32[]{:S(2)}) copy-start(f32[1,36,16384]{2,0,1:T(1,128)} %param.12) | copy-start | bytes 7077892
  118.8 27.4 %copy-start.4 = (f32[1,36,16384]{2,0,1:T(1,128)S(1)}, f32[1,36,16384]{2,0,1:T(1,128)}, u32[]{:S(2)}) copy-start(f32[1,36,16384]{2,0,1:T(1,128)} %param.11) | copy-start | bytes 7077892
  125.2 3.8 %collective-permute-start.16 = (f32[1,1]{1,0:T(1,128)}, f32[1,1]{1,0:T(1,128)}, u32[]{:S(2)}, u32[]{:S(2)}) collective-permute-start(f32[1,1]{1,0:T(1,128)} %bitcast.4), channel_id=1, source_target_pairs={{0,4},{4,0},{8,12},{12,8},{16,20},{20,16},{24,28},{28,24},{1,5},{5... | collective-permute-start | bytes 20 | tf_op jit(solution)/shard_map/ppermute | solution.py:41
  130.3 3.7 %collective-permute-start.17 = (f32[1,1]{1,0:T(1,128)}, f32[1,1]{1,0:T(1,128)}, u32[]{:S(2)}, u32[]{:S(2)}) collective-permute-start(f32[1,1]{1,0:T(1,128)} %add.248), channel_id=1, source_target_pairs={{0,8},{4,12},{8,0},{12,4},{16,24},{20,28},{24,16},{28,20},{1,9},{5... | collective-permute-start | bytes 20 | tf_op jit(solution)/shard_map/ppermute | solution.py:41
  134.6 4.6 %collective-permute-start.18 = (f32[1,1]{1,0:T(1,128)}, f32[1,1]{1,0:T(1,128)}, u32[]{:S(2)}, u32[]{:S(2)}) collective-permute-start(f32[1,1]{1,0:T(1,128)} %add.249), channel_id=1, source_target_pairs={{0,16},{4,20},{8,24},{12,28},{16,0},{20,4},{24,8},{28,12},{1,17},{... | collective-permute-start | bytes 20 | tf_op jit(solution)/shard_map/ppermute | solution.py:41
  139.8 1.3 collective-permute-start.19
  141.8 3.7 %collective-permute-start.20 = (f32[1,1]{1,0:T(1,128)}, f32[1,1]{1,0:T(1,128)}, u32[]{:S(2)}, u32[]{:S(2)}) collective-permute-start(f32[1,1]{1,0:T(1,128)} %add.251), channel_id=1, source_target_pairs={{0,2},{1,3},{2,0},{3,1},{4,6},{5,7},{6,4},{7,5},{8,10},{9,11},{10,... | collective-permute-start | bytes 20 | tf_op jit(solution)/shard_map/ppermute | solution.py:41
  155.7 26.8 %collective-permute-start.21 = (bf16[72,8192]{1,0:T(8,128)(2,1)S(1)}, bf16[72,8192]{1,0:T(8,128)(2,1)S(1)}, u32[]{:S(2)}, u32[]{:S(2)}) collective-permute-start(bf16[72,8192]{1,0:T(8,128)(2,1)S(1)} %get-tuple-element.24), channel_id=1, source_target_pairs={{0,8},{8,16},{16,24},{24,28},{28,20},{20,12},{12,4},{4,0},{1,9},{9... | collective-permute-start | bytes 3538952 | tf_op jit(solution)/shard_map/ppermute | solution.py:122
  156.9 27.1 %collective-permute-start.28 = (bf16[72,8192]{1,0:T(8,128)(2,1)S(1)}, bf16[72,8192]{1,0:T(8,128)(2,1)S(1)}, u32[]{:S(2)}, u32[]{:S(2)}) collective-permute-start(bf16[72,8192]{1,0:T(8,128)(2,1)S(1)} %get-tuple-element.25), channel_id=1, source_target_pairs={{8,0},{16,8},{24,16},{28,24},{20,28},{12,20},{4,12},{0,4},{9,1},{1... | collective-permute-start | bytes 3538952 | tf_op jit(solution)/shard_map/ppermute | solution.py:123
  182.6 26.1 %collective-permute-start.22 = (bf16[72,8192]{1,0:T(8,128)(2,1)S(1)}, bf16[72,8192]{1,0:T(8,128)(2,1)S(1)}, u32[]{:S(2)}, u32[]{:S(2)}) collective-permute-start(bf16[72,8192]{1,0:T(8,128)(2,1)S(1)} %collective-permute-done.21), channel_id=1, source_target_pairs={{0,8},{8,16},{16,24},{24,28},{28,20},{20,12},{12,4},{4,0},{1,9},{9... | collective-permute-start | bytes 3538952 | tf_op jit(solution)/shard_map/ppermute | solution.py:122
  184.0 26.2 %collective-permute-start.29 = (bf16[72,8192]{1,0:T(8,128)(2,1)S(1)}, bf16[72,8192]{1,0:T(8,128)(2,1)S(1)}, u32[]{:S(2)}, u32[]{:S(2)}) collective-permute-start(bf16[72,8192]{1,0:T(8,128)(2,1)S(1)} %collective-permute-done.28), channel_id=1, source_target_pairs={{8,0},{16,8},{24,16},{28,24},{20,28},{12,20},{4,12},{0,4},{9,1},{1... | collective-permute-start | bytes 3538952 | tf_op jit(solution)/shard_map/ppermute | solution.py:123
  208.7 26.1 %collective-permute-start.23 = (bf16[72,8192]{1,0:T(8,128)(2,1)S(1)}, bf16[72,8192]{1,0:T(8,128)(2,1)S(1)}, u32[]{:S(2)}, u32[]{:S(2)}) collective-permute-start(bf16[72,8192]{1,0:T(8,128)(2,1)S(1)} %collective-permute-done.22), channel_id=1, source_target_pairs={{0,8},{8,16},{16,24},{24,28},{28,20},{20,12},{12,4},{4,0},{1,9},{9... | collective-permute-start | bytes 3538952 | tf_op jit(solution)/shard_map/ppermute | solution.py:122
  210.3 26.1 %collective-permute-start.30 = (bf16[72,8192]{1,0:T(8,128)(2,1)S(1)}, bf16[72,8192]{1,0:T(8,128)(2,1)S(1)}, u32[]{:S(2)}, u32[]{:S(2)}) collective-permute-start(bf16[72,8192]{1,0:T(8,128)(2,1)S(1)} %collective-permute-done.29), channel_id=1, source_target_pairs={{8,0},{16,8},{24,16},{28,24},{20,28},{12,20},{4,12},{0,4},{9,1},{1... | collective-permute-start | bytes 3538952 | tf_op jit(solution)/shard_map/ppermute | solution.py:123
  234.8 26.1 %collective-permute-start.24 = (bf16[72,8192]{1,0:T(8,128)(2,1)S(1)}, bf16[72,8192]{1,0:T(8,128)(2,1)S(1)}, u32[]{:S(2)}, u32[]{:S(2)}) collective-permute-start(bf16[72,8192]{1,0:T(8,128)(2,1)S(1)} %collective-permute-done.23), channel_id=1, source_target_pairs={{0,8},{8,16},{16,24},{24,28},{28,20},{20,12},{12,4},{4,0},{1,9},{9... | collective-permute-start | bytes 3538952 | tf_op jit(solution)/shard_map/ppermute | solution.py:122
  236.4 26.1 %collective-permute-start.31 = (bf16[72,8192]{1,0:T(8,128)(2,1)S(1)}, bf16[72,8192]{1,0:T(8,128)(2,1)S(1)}, u32[]{:S(2)}, u32[]{:S(2)}) collective-permute-start(bf16[72,8192]{1,0:T(8,128)(2,1)S(1)} %collective-permute-done.30), channel_id=1, source_target_pairs={{8,0},{16,8},{24,16},{28,24},{20,28},{12,20},{4,12},{0,4},{9,1},{1... | collective-permute-start | bytes 3538952 | tf_op jit(solution)/shard_map/ppermute | solution.py:123
  261.0 26.1 %collective-permute-start.25 = (bf16[72,8192]{1,0:T(8,128)(2,1)S(1)}, bf16[72,8192]{1,0:T(8,128)(2,1)S(1)}, u32[]{:S(2)}, u32[]{:S(2)}) collective-permute-start(bf16[72,8192]{1,0:T(8,128)(2,1)S(1)} %collective-permute-done.24), channel_id=1, source_target_pairs={{0,8},{8,16},{16,24},{24,28},{28,20},{20,12},{12,4},{4,0},{1,9},{9... | collective-permute-start | bytes 3538952 | tf_op jit(solution)/shard_map/ppermute | solution.py:122
  262.5 26.0 %collective-permute-start.32 = (bf16[72,8192]{1,0:T(8,128)(2,1)S(1)}, bf16[72,8192]{1,0:T(8,128)(2,1)S(1)}, u32[]{:S(2)}, u32[]{:S(2)}) collective-permute-start(bf16[72,8192]{1,0:T(8,128)(2,1)S(1)} %collective-permute-done.31), channel_id=1, source_target_pairs={{8,0},{16,8},{24,16},{28,24},{20,28},{12,20},{4,12},{0,4},{9,1},{1... | collective-permute-start | bytes 3538952 | tf_op jit(solution)/shard_map/ppermute | solution.py:123
  287.1 26.1 %collective-permute-start.26 = (bf16[72,8192]{1,0:T(8,128)(2,1)S(1)}, bf16[72,8192]{1,0:T(8,128)(2,1)S(1)}, u32[]{:S(2)}, u32[]{:S(2)}) collective-permute-start(bf16[72,8192]{1,0:T(8,128)(2,1)S(1)} %collective-permute-done.25), channel_id=1, source_target_pairs={{0,8},{8,16},{16,24},{24,28},{28,20},{20,12},{12,4},{4,0},{1,9},{9... | collective-permute-start | bytes 3538952 | tf_op jit(solution)/shard_map/ppermute | solution.py:122
  288.6 26.3 %collective-permute-start.33 = (bf16[72,8192]{1,0:T(8,128)(2,1)S(1)}, bf16[72,8192]{1,0:T(8,128)(2,1)S(1)}, u32[]{:S(2)}, u32[]{:S(2)}) collective-permute-start(bf16[72,8192]{1,0:T(8,128)(2,1)S(1)} %collective-permute-done.32), channel_id=1, source_target_pairs={{8,0},{16,8},{24,16},{28,24},{20,28},{12,20},{4,12},{0,4},{9,1},{1... | collective-permute-start | bytes 3538952 | tf_op jit(solution)/shard_map/ppermute | solution.py:123
  313.2 21.6 %collective-permute-start.27 = (bf16[72,8192]{1,0:T(8,128)(2,1)S(1)}, bf16[72,8192]{1,0:T(8,128)(2,1)S(1)}, u32[]{:S(2)}, u32[]{:S(2)}) collective-permute-start(bf16[72,8192]{1,0:T(8,128)(2,1)S(1)} %collective-permute-done.26), channel_id=1, source_target_pairs={{0,8},{8,16},{16,24},{24,28},{28,20},{20,12},{12,4},{4,0},{1,9},{9... | collective-permute-start | bytes 3538952 | tf_op jit(solution)/shard_map/ppermute | solution.py:122
  314.8 21.4 %collective-permute-start.34 = (bf16[72,8192]{1,0:T(8,128)(2,1)S(1)}, bf16[72,8192]{1,0:T(8,128)(2,1)S(1)}, u32[]{:S(2)}, u32[]{:S(2)}) collective-permute-start(bf16[72,8192]{1,0:T(8,128)(2,1)S(1)} %collective-permute-done.33), channel_id=1, source_target_pairs={{8,0},{16,8},{24,16},{28,24},{20,28},{12,20},{4,12},{0,4},{9,1},{1... | collective-permute-start | bytes 3538952 | tf_op jit(solution)/shard_map/ppermute | solution.py:123

commit v2 on v1

--- a/solution.py
+++ b/solution.py
@@ -98,32 +98,37 @@
         )
         averaged = 0.9 * average_weights[0] + 0.1 * new_master
 
-        payload = jnp.concatenate([new_master, averaged], axis=0).astype(jnp.bfloat16)
+        rank_ahead = jnp.array(ring, jnp.int32)[(mypos + jnp.arange(n, dtype=jnp.int32)) % n]
+        seg_ahead = (rank_ahead[:, None] * per_rank + jnp.arange(per_rank, dtype=jnp.int32)[None, :]).reshape(-1)
+        to_rows = (jnp.arange(cap, dtype=jnp.int32)[:, None] == slot[seg_ahead][None, :]).astype(jnp.bfloat16)
+        spread_avg = jnp.dot(to_rows.T, averaged.astype(jnp.bfloat16), preferred_element_type=jnp.bfloat16)
+        spread_avg = spread_avg.reshape(n, per_rank, seg)
+        avg_l, avg_r = spread_avg[..., :half], spread_avg[..., half:]
+
+        payload = new_master.astype(jnp.bfloat16)
         send_a, send_b = payload[:, :half], payload[:, half:]
         placing_t = placing.T
-        mine_t = lax.dynamic_slice_in_dim(placing_t, me * per_rank, per_rank, 0)
 
-        def spread(rows_t, chunk, k, kind):
-            return jnp.dot(rows_t[:, k * cap:(k + 1) * cap], chunk, preferred_element_type=kind)
+        def spread(chunk, k):
+            return jnp.dot(placing_t[:, k * cap:(k + 1) * cap], chunk, preferred_element_type=jnp.bfloat16)
 
-        def place(acc, k_a, a, k_b, b):
-            parts = (
-                spread(placing_t, a[:cap], k_a, jnp.bfloat16),
-                spread(placing_t, b[:cap], k_b, jnp.bfloat16),
-                spread(mine_t, a[cap:], k_a, jnp.float32),
-                spread(mine_t, b[cap:], k_b, jnp.float32),
-            )
-            if acc is None:
-                return parts
-            return tuple(x + y for x, y in zip(acc, parts))
-
-        acc = place(None, 0, send_a, 0, send_b)
+        out_a = spread(send_a, 0)
+        out_b = spread(send_b, 0)
+        sum_a = avg_l[n - 1]
+        sum_b = avg_r[1]
         for t in range(n - 1):
             send_a = lax.ppermute(send_a, "dp", fwd)
             send_b = lax.ppermute(send_b, "dp", bwd)
-            acc = place(acc, n - 1 - t, send_a, 1 + t, send_b)
-        new_params = jnp.concatenate([acc[0], acc[1]], axis=1)
-        average_rows = jnp.concatenate([acc[2], acc[3]], axis=1)
+            got_a = lax.ppermute(sum_a, "dp", fwd)
+            got_b = lax.ppermute(sum_b, "dp", bwd)
+            out_a = out_a + spread(send_a, n - 1 - t)
+            out_b = out_b + spread(send_b, 1 + t)
+            fin_a = got_a.astype(jnp.float32) + avg_l[(2 * n - 2 - t) % n].astype(jnp.float32)
+            fin_b = got_b.astype(jnp.float32) + avg_r[(2 + t) % n].astype(jnp.float32)
+            if t < n - 2:
+                sum_a, sum_b = fin_a.astype(jnp.bfloat16), fin_b.astype(jnp.bfloat16)
+        new_params = jnp.concatenate([out_a, out_b], axis=1)
+        average_rows = jnp.concatenate([fin_a, fin_b], axis=1)
         return (
             new_params[None],
             new_master[None],

time: 350 us -> 340 us (0.971)
  waiting for transfers between devices: 216 us -> 194 us
  starting transfers between devices: 43.2 us -> 58.4 us
    ppermute x7, waiting for transfers between devices: 125 us -> 45.5 us  [on_device(): send_a = lax.ppermute(send_a, 'dp', fwd)]
    ppermute x0 -> x14, waiting for transfers between devices: none -> 59.2 us  [the longest x7 51.2 us: on_device(): got_a = lax.ppermute(sum_a, 'dp', fwd)]
    ppermute x7, waiting for transfers between devices: 52.2 us -> 30 us  [on_device(): got_b = lax.ppermute(send_b, 'dp', bwd)]
    ppermute x7, waiting for transfers between devices: 30.9 us -> 53 us  [on_device(): got_a = lax.ppermute(send_a, 'dp', fwd)]
    ppermute x0 -> x14, starting transfers between devices: none -> 14.7 us  [the longest x7 9.31 us: on_device(): got_a = lax.ppermute(sum_a, 'dp', fwd)]
    another operation x1 -> x0, other arithmetic: 9.09 us -> none
    convert_element_type x0 -> x7, other arithmetic: none -> 8.22 us  [the longest x1 7.11 us: on_device(): payload = new_master.astype(jnp.bfloat16)]
    dot_general x32 -> x17, matrix products: 21.8 us -> 18.8 us  [the longest x16 16.4 us: spread(): jnp.dot(placing_t[:, k * cap:(k + 1) * cap], chunk, preferred_element_typ...]
  transfers between devices with their start and end apart: 35 -> 49, of which waited for: 31 -> 38; matrix products, arithmetic and copies ran while one was open for 17% -> 16% of each run, Pallas kernels for 0% -> 0%
where the time goes in v2:
time: 340 us; the launch traced here: 333 us
  waiting for transfers between devices  194 us (57%)
  starting transfers between devices  58.4 us (17%)
  other arithmetic  34.2 us (10%)
  matrix products  25.8 us (8%)
  local copies, waits for them, and re-layouts  15.9 us (5%)
  between operations  4.87 us (1%)
    ppermute x7, waiting for transfers between devices, on_device(): got_a = lax.ppermute(send_a, 'dp', fwd)  53 us
    ppermute x7, waiting for transfers between devices, on_device(): got_a = lax.ppermute(sum_a, 'dp', fwd)  51.2 us
    ppermute x7, waiting for transfers between devices, on_device(): send_a = lax.ppermute(send_a, 'dp', fwd)  45.5 us
    ppermute x7, waiting for transfers between devices, on_device(): got_b = lax.ppermute(send_b, 'dp', bwd)  30 us
    dot_general x16, matrix products, spread(): jnp.dot(placing_t[:, k * cap:(k + 1) * cap], chunk, preferred_element_typ...  16.4 us
    unnamed x21, local copies, waits for them, and re-layouts  11.5 us
    ppermute x5, starting transfers between devices, all_sum(): v = v + lax.ppermute(v, axis, [(i, i ^ k) for i in range(n)])  11.5 us
    ppermute x7, starting transfers between devices, on_device(): got_b = lax.ppermute(send_b, 'dp', bwd)  9.75 us
  transfers between devices with their start and end apart: 49, of which 38 were waited for; matrix products, arithmetic and copies ran while one was open for 16% of the time, Pallas kernels for 0%

profile of v2, /device:TPU:0, one launch (start us, length us, event | category | flops | bytes accessed | tf_op | source)
XLA Modules:
  0.0 333.4 jit_solution(16231962290553876031)
XLA Ops:
  0.6 3.1 collective-permute-start
  7.3 3.4 %fusion = bf16[288,8192]{1,0:T(8,128)(2,1)S(1)} fusion(bf16[192,16384]{1,0:T(8,128)(2,1)} %bitcast.135, s32[192]{0:T(256)S(1)} %fusion.58), kind=kOutput, calls=%fused_computation.19 | convolution fusion | flops 906024960 | bytes 7865088 | tf_op jit(solution)/shard_map/dot_general | solution.py:74
  10.9 2.0 collective-permute-start.9
  12.9 3.6 %fusion.2 = bf16[288,8192]{1,0:T(8,128)(2,1)} fusion(bf16[192,16384]{1,0:T(8,128)(2,1)S(1)} %bitcast.136, s32[192]{0:T(256)S(1)} %fusion.58), kind=kOutput, calls=%fused_computation.21 | convolution fusion | flops 906024960 | bytes 7865344 | tf_op jit(solution)/shard_map/dot_general | solution.py:73
  18.2 1.6 gather_fusion.1
  20.6 2.0 slice_add_fusion
  22.7 4.4 %collective-permute-done.9 = bf16[36,8192]{1,0:T(8,128)(2,1)S(1)} collective-permute-done((bf16[36,8192]{1,0:T(8,128)(2,1)S(1)}, bf16[36,8192]{1,0:T(8,128)(2,1)S(1)}, u32[]{:S(2)}, u32[]{:S(2)}) %collective-permute-start.9) | collective-permute-done | bytes 589856 | tf_op jit(solution)/shard_map/ppermute | solution.py:80
  28.4 1.7 collective-permute-start.10
  30.1 8.1 %collective-permute-done.2 = bf16[36,8192]{1,0:T(8,128)(2,1)S(1)} collective-permute-done((bf16[36,8192]{1,0:T(8,128)(2,1)S(1)}, bf16[36,8192]{1,0:T(8,128)(2,1)S(1)}, u32[]{:S(2)}, u32[]{:S(2)}) %collective-permute-start.2) | collective-permute-done | bytes 589856 | tf_op jit(solution)/shard_map/ppermute | solution.py:79
  39.9 3.8 %collective-permute-done.10 = bf16[36,8192]{1,0:T(8,128)(2,1)S(1)} collective-permute-done((bf16[36,8192]{1,0:T(8,128)(2,1)S(1)}, bf16[36,8192]{1,0:T(8,128)(2,1)S(1)}, u32[]{:S(2)}, u32[]{:S(2)}) %collective-permute-start.10) | collective-permute-done | bytes 589856 | tf_op jit(solution)/shard_map/ppermute | solution.py:80
  46.5 7.7 %collective-permute-done.3 = bf16[36,8192]{1,0:T(8,128)(2,1)S(1)} collective-permute-done((bf16[36,8192]{1,0:T(8,128)(2,1)S(1)}, bf16[36,8192]{1,0:T(8,128)(2,1)S(1)}, u32[]{:S(2)}, u32[]{:S(2)}) %collective-permute-start.3) | collective-permute-done | bytes 589856 | tf_op jit(solution)/shard_map/ppermute | solution.py:79
  55.2 4.3 %collective-permute-done.11 = bf16[36,8192]{1,0:T(8,128)(2,1)S(1)} collective-permute-done((bf16[36,8192]{1,0:T(8,128)(2,1)S(1)}, bf16[36,8192]{1,0:T(8,128)(2,1)S(1)}, u32[]{:S(2)}, u32[]{:S(2)}) %collective-permute-start.11) | collective-permute-done | bytes 589856 | tf_op jit(solution)/shard_map/ppermute | solution.py:80
  61.9 7.3 %collective-permute-done.4 = bf16[36,8192]{1,0:T(8,128)(2,1)S(1)} collective-permute-done((bf16[36,8192]{1,0:T(8,128)(2,1)S(1)}, bf16[36,8192]{1,0:T(8,128)(2,1)S(1)}, u32[]{:S(2)}, u32[]{:S(2)}) %collective-permute-start.4) | collective-permute-done | bytes 589856 | tf_op jit(solution)/shard_map/ppermute | solution.py:79
  70.1 5.3 %collective-permute-done.12 = bf16[36,8192]{1,0:T(8,128)(2,1)S(1)} collective-permute-done((bf16[36,8192]{1,0:T(8,128)(2,1)S(1)}, bf16[36,8192]{1,0:T(8,128)(2,1)S(1)}, u32[]{:S(2)}, u32[]{:S(2)}) %collective-permute-start.12) | collective-permute-done | bytes 589856 | tf_op jit(solution)/shard_map/ppermute | solution.py:80
  76.8 7.2 %collective-permute-done.5 = bf16[36,8192]{1,0:T(8,128)(2,1)S(1)} collective-permute-done((bf16[36,8192]{1,0:T(8,128)(2,1)S(1)}, bf16[36,8192]{1,0:T(8,128)(2,1)S(1)}, u32[]{:S(2)}, u32[]{:S(2)}) %collective-permute-start.5) | collective-permute-done | bytes 589856 | tf_op jit(solution)/shard_map/ppermute | solution.py:79
  85.0 5.4 %collective-permute-done.13 = bf16[36,8192]{1,0:T(8,128)(2,1)S(1)} collective-permute-done((bf16[36,8192]{1,0:T(8,128)(2,1)S(1)}, bf16[36,8192]{1,0:T(8,128)(2,1)S(1)}, u32[]{:S(2)}, u32[]{:S(2)}) %collective-permute-start.13) | collective-permute-done | bytes 589856 | tf_op jit(solution)/shard_map/ppermute | solution.py:80
  91.7 7.3 %collective-permute-done.6 = bf16[36,8192]{1,0:T(8,128)(2,1)S(1)} collective-permute-done((bf16[36,8192]{1,0:T(8,128)(2,1)S(1)}, bf16[36,8192]{1,0:T(8,128)(2,1)S(1)}, u32[]{:S(2)}, u32[]{:S(2)}) %collective-permute-start.6) | collective-permute-done | bytes 589856 | tf_op jit(solution)/shard_map/ppermute | solution.py:79
  99.9 5.3 %collective-permute-done.14 = bf16[36,8192]{1,0:T(8,128)(2,1)S(1)} collective-permute-done((bf16[36,8192]{1,0:T(8,128)(2,1)S(1)}, bf16[36,8192]{1,0:T(8,128)(2,1)S(1)}, u32[]{:S(2)}, u32[]{:S(2)}) %collective-permute-start.14) | collective-permute-done | bytes 589856 | tf_op jit(solution)/shard_map/ppermute | solution.py:80
  106.6 7.1 %collective-permute-done.7 = bf16[36,8192]{1,0:T(8,128)(2,1)S(1)} collective-permute-done((bf16[36,8192]{1,0:T(8,128)(2,1)S(1)}, bf16[36,8192]{1,0:T(8,128)(2,1)S(1)}, u32[]{:S(2)}, u32[]{:S(2)}) %collective-permute-start.7) | collective-permute-done | bytes 589856 | tf_op jit(solution)/shard_map/ppermute | solution.py:79
  116.6 8.2 %collective-permute-done.8 = bf16[36,8192]{1,0:T(8,128)(2,1)S(1)} collective-permute-done((bf16[36,8192]{1,0:T(8,128)(2,1)S(1)}, bf16[36,8192]{1,0:T(8,128)(2,1)S(1)}, u32[]{:S(2)}, u32[]{:S(2)}) %collective-permute-start.8) | collective-permute-done | bytes 589856 | tf_op jit(solution)/shard_map/ppermute | solution.py:79
  127.8 2.2 collective-permute-done.16
  131.2 2.5 collective-permute-start.17
  135.4 3.5 %collective-permute-start.18 = (f32[1,1]{1,0:T(1,128)}, f32[1,1]{1,0:T(1,128)}, u32[]{:S(2)}, u32[]{:S(2)}) collective-permute-start(f32[1,1]{1,0:T(1,128)} %add.324), channel_id=1, source_target_pairs={{0,16},{4,20},{8,24},{12,28},{16,0},{20,4},{24,8},{28,12},{1,17},{... | collective-permute-start | bytes 20 | tf_op jit(solution)/shard_map/ppermute | solution.py:41
  142.5 2.9 collective-permute-start.20
  146.9 7.1 %fusion.14 = bf16[36,16384]{1,0:T(8,128)(2,1)S(1)} fusion(f32[1,36,16384]{2,0,1:T(1,128)S(1)} %copy-done.4, f32[1,36,16384]{2,0,1:T(1,128)S(1)} %copy-done.5, f32[1,36,16384]{2,0,1:T(1,128)S(1)} %copy-done.6, f32[36,8192]{1,0:T(8,128)S(1)} %get-tuple-element.42, f32[36,8192]{1,0:T(8,128)S(1)} %get-tuple-element.40, f32[]{:T(128)} %bitcast.5, ...), kind=kLoop, calls=%fused_computation.37 | loop fusion | flops 12386304 | bytes 10616980 | tf_op jit(solution)/shard_map/convert_element_type | solution.py:108
  154.0 7.4 %subtract_multiply_fusion = (f32[1,36,16384]{2,1,0:T(8,128)S(1)}, f32[1,36,16384]{2,1,0:T(8,128)S(1)}, f32[1,36,16384]{2,1,0:T(8,128)S(1)}) fusion(f32[1,36,16384]{2,0,1:T(1,128)S(1)} %copy-done.4, f32[36]{0:T(128)S(1)} %convert_element_type.304, f32[1,36,8192]{2,1,0:T(8,128)S(1)} %get-tuple-element.41, f32[1,36,8192]{2,1,0:T(8,128)S(1)} %get-tuple-element.39, ...), kind=kLoop, calls=%fused_computation.46 | loop fusion | flops 11796480 | bytes 16515220 | tf_op jit(solution)/shard_map/mul | solution.py:96
  161.5 2.4 fusion.20
  167.3 3.8 %copy.35 = f32[1,36,16384]{2,0,1:T(1,128)} copy(f32[1,36,16384]{2,1,0:T(8,128)S(1)} %get-tuple-element.20) | data formatting | bytes 4718592
  173.1 3.8 %copy.36 = f32[1,36,16384]{2,0,1:T(1,128)} copy(f32[1,36,16384]{2,1,0:T(8,128)S(1)} %get-tuple-element.21) | data formatting | bytes 4718592
  177.0 3.8 %copy.37 = f32[1,36,16384]{2,0,1:T(1,128)} copy(f32[1,36,16384]{2,1,0:T(8,128)S(1)} %get-tuple-element.22) | data formatting | bytes 4718592
  184.1 5.7 %collective-permute-done.21 = bf16[36,8192]{1,0:T(8,128)(2,1)S(1)} collective-permute-done((bf16[36,8192]{1,0:T(8,128)(2,1)S(1)}, bf16[36,8192]{1,0:T(8,128)(2,1)S(1)}, u32[]{:S(2)}, u32[]{:S(2)}) %collective-permute-start.21) | collective-permute-done | bytes 589856 | tf_op jit(solution)/shard_map/ppermute | solution.py:120
  194.3 3.9 %collective-permute-done.36 = bf16[24,8192]{1,0:T(8,128)(2,1)S(1)} collective-permute-done((bf16[24,8192]{1,0:T(8,128)(2,1)S(1)}, bf16[24,8192]{1,0:T(8,128)(2,1)S(1)}, u32[]{:S(2)}, u32[]{:S(2)}) %collective-permute-start.36) | collective-permute-done | bytes 393248 | tf_op jit(solution)/shard_map/ppermute | solution.py:122
  199.6 1.6 collective-permute-start.37
  201.7 10.6 %collective-permute-done.22 = bf16[36,8192]{1,0:T(8,128)(2,1)S(1)} collective-permute-done((bf16[36,8192]{1,0:T(8,128)(2,1)S(1)}, bf16[36,8192]{1,0:T(8,128)(2,1)S(1)}, u32[]{:S(2)}, u32[]{:S(2)}) %collective-permute-start.22) | collective-permute-done | bytes 589856 | tf_op jit(solution)/shard_map/ppermute | solution.py:120
  215.4 5.3 %collective-permute-done.37 = bf16[24,8192]{1,0:T(8,128)(2,1)S(1)} collective-permute-done((bf16[24,8192]{1,0:T(8,128)(2,1)S(1)}, bf16[24,8192]{1,0:T(8,128)(2,1)S(1)}, u32[]{:S(2)}, u32[]{:S(2)}) %collective-permute-start.37) | collective-permute-done | bytes 393248 | tf_op jit(solution)/shard_map/ppermute | solution.py:122
  222.1 1.6 collective-permute-start.38
  225.2 16.1 %collective-permute-done.38 = bf16[24,8192]{1,0:T(8,128)(2,1)S(1)} collective-permute-done((bf16[24,8192]{1,0:T(8,128)(2,1)S(1)}, bf16[24,8192]{1,0:T(8,128)(2,1)S(1)}, u32[]{:S(2)}, u32[]{:S(2)}) %collective-permute-start.38) | collective-permute-done | bytes 393248 | tf_op jit(solution)/shard_map/ppermute | solution.py:122
  242.6 1.6 collective-permute-start.39
  244.6 1.6 collective-permute-start.24
  248.8 5.9 %collective-permute-done.39 = bf16[24,8192]{1,0:T(8,128)(2,1)S(1)} collective-permute-done((bf16[24,8192]{1,0:T(8,128)(2,1)S(1)}, bf16[24,8192]{1,0:T(8,128)(2,1)S(1)}, u32[]{:S(2)}, u32[]{:S(2)}) %collective-permute-start.39) | collective-permute-done | bytes 393248 | tf_op jit(solution)/shard_map/ppermute | solution.py:122
  254.7 1.6 collective-permute-done.46
  258.5 10.2 %collective-permute-done.24 = bf16[36,8192]{1,0:T(8,128)(2,1)S(1)} collective-permute-done((bf16[36,8192]{1,0:T(8,128)(2,1)S(1)}, bf16[36,8192]{1,0:T(8,128)(2,1)S(1)}, u32[]{:S(2)}, u32[]{:S(2)}) %collective-permute-start.24) | collective-permute-done | bytes 589856 | tf_op jit(solution)/shard_map/ppermute | solution.py:120
  268.7 1.6 collective-permute-start.25
  271.8 5.4 %collective-permute-done.40 = bf16[24,8192]{1,0:T(8,128)(2,1)S(1)} collective-permute-done((bf16[24,8192]{1,0:T(8,128)(2,1)S(1)}, bf16[24,8192]{1,0:T(8,128)(2,1)S(1)}, u32[]{:S(2)}, u32[]{:S(2)}) %collective-permute-start.40) | collective-permute-done | bytes 393248 | tf_op jit(solution)/shard_map/ppermute | solution.py:122
  282.0 14.7 %collective-permute-done.41 = bf16[24,8192]{1,0:T(8,128)(2,1)S(1)} collective-permute-done((bf16[24,8192]{1,0:T(8,128)(2,1)S(1)}, bf16[24,8192]{1,0:T(8,128)(2,1)S(1)}, u32[]{:S(2)}, u32[]{:S(2)}) %collective-permute-start.41) | collective-permute-done | bytes 393248 | tf_op jit(solution)/shard_map/ppermute | solution.py:122
  303.6 10.7 %collective-permute-done.26 = bf16[36,8192]{1,0:T(8,128)(2,1)S(1)} collective-permute-done((bf16[36,8192]{1,0:T(8,128)(2,1)S(1)}, bf16[36,8192]{1,0:T(8,128)(2,1)S(1)}, u32[]{:S(2)}, u32[]{:S(2)}) %collective-permute-start.26) | collective-permute-done | bytes 589856 | tf_op jit(solution)/shard_map/ppermute | solution.py:120
  318.7 8.4 %collective-permute-done.27 = bf16[36,8192]{1,0:T(8,128)(2,1)S(1)} collective-permute-done((bf16[36,8192]{1,0:T(8,128)(2,1)S(1)}, bf16[36,8192]{1,0:T(8,128)(2,1)S(1)}, u32[]{:S(2)}, u32[]{:S(2)}) %collective-permute-start.27) | collective-permute-done | bytes 589856 | tf_op jit(solution)/shard_map/ppermute | solution.py:120
  329.8 3.3 maximum_bitcast_fusion
  (140 shorter events, 80.4 us)
Async XLA Ops:
  0.6 19.4 %collective-permute-start = (bf16[8,128]{1,0:T(8,128)(2,1)S(1)}, bf16[8,128]{1,0:T(8,128)(2,1)S(1)}, u32[]{:S(2)}, u32[]{:S(2)}) collective-permute-start(bf16[8,128]{1,0:T(8,128)(2,1)S(1)} %broadcast_in_dim.9), channel_id=1, source_target_pairs={{0,8},{8,16},{16,24},{24,28},{28,20},{20,12},{12,4},{4,0},{1,9},{9... | collective-permute-start | bytes 6152 | tf_op jit(solution)/shard_map/ppermute | solution.py:63
  3.7 16.3 %collective-permute-start.1 = (bf16[8,128]{1,0:T(8,128)(2,1)S(1)}, bf16[8,128]{1,0:T(8,128)(2,1)S(1)}, u32[]{:S(2)}, u32[]{:S(2)}) collective-permute-start(bf16[8,128]{1,0:T(8,128)(2,1)S(1)} %broadcast_in_dim.9), channel_id=1, source_target_pairs={{8,0},{16,8},{24,16},{28,24},{20,28},{12,20},{4,12},{0,4},{9,1},{1... | collective-permute-start | bytes 6152 | tf_op jit(solution)/shard_map/ppermute | solution.py:63
  10.9 16.2 %collective-permute-start.9 = (bf16[36,8192]{1,0:T(8,128)(2,1)S(1)}, bf16[36,8192]{1,0:T(8,128)(2,1)S(1)}, u32[]{:S(2)}, u32[]{:S(2)}) collective-permute-start(bf16[36,8192]{1,0:T(8,128)(2,1)S(1)} %slice.251), channel_id=1, source_target_pairs={{8,0},{16,8},{24,16},{28,24},{20,28},{12,20},{4,12},{0,4},{9,1},{1... | collective-permute-start | bytes 1769480 | tf_op jit(solution)/shard_map/ppermute | solution.py:80
  22.6 15.7 %collective-permute-start.2 = (bf16[36,8192]{1,0:T(8,128)(2,1)S(1)}, bf16[36,8192]{1,0:T(8,128)(2,1)S(1)}, u32[]{:S(2)}, u32[]{:S(2)}) collective-permute-start(bf16[36,8192]{1,0:T(8,128)(2,1)S(1)} %slice_add_fusion), channel_id=1, source_target_pairs={{0,8},{8,16},{16,24},{24,28},{28,20},{20,12},{12,4},{4,0},{1,9},{9... | collective-permute-start | bytes 1769480 | tf_op jit(solution)/shard_map/ppermute | solution.py:79
  28.4 15.3 %collective-permute-start.10 = (bf16[36,8192]{1,0:T(8,128)(2,1)S(1)}, bf16[36,8192]{1,0:T(8,128)(2,1)S(1)}, u32[]{:S(2)}, u32[]{:S(2)}) collective-permute-start(bf16[36,8192]{1,0:T(8,128)(2,1)S(1)} %add_convert_fusion.5), channel_id=1, source_target_pairs={{8,0},{16,8},{24,16},{28,24},{20,28},{12,20},{4,12},{0,4},{9,1},{1... | collective-permute-start | bytes 1769480 | tf_op jit(solution)/shard_map/ppermute | solution.py:80
  39.5 14.8 %collective-permute-start.3 = (bf16[36,8192]{1,0:T(8,128)(2,1)S(1)}, bf16[36,8192]{1,0:T(8,128)(2,1)S(1)}, u32[]{:S(2)}, u32[]{:S(2)}) collective-permute-start(bf16[36,8192]{1,0:T(8,128)(2,1)S(1)} %add_convert_fusion.11), channel_id=1, source_target_pairs={{0,8},{8,16},{16,24},{24,28},{28,20},{20,12},{12,4},{4,0},{1,9},{9... | collective-permute-start | bytes 1769480 | tf_op jit(solution)/shard_map/ppermute | solution.py:79
  45.1 14.4 %collective-permute-start.11 = (bf16[36,8192]{1,0:T(8,128)(2,1)S(1)}, bf16[36,8192]{1,0:T(8,128)(2,1)S(1)}, u32[]{:S(2)}, u32[]{:S(2)}) collective-permute-start(bf16[36,8192]{1,0:T(8,128)(2,1)S(1)} %add_convert_fusion.4), channel_id=1, source_target_pairs={{8,0},{16,8},{24,16},{28,24},{20,28},{12,20},{4,12},{0,4},{9,1},{1... | collective-permute-start | bytes 1769480 | tf_op jit(solution)/shard_map/ppermute | solution.py:80
  54.5 14.7 %collective-permute-start.4 = (bf16[36,8192]{1,0:T(8,128)(2,1)S(1)}, bf16[36,8192]{1,0:T(8,128)(2,1)S(1)}, u32[]{:S(2)}, u32[]{:S(2)}) collective-permute-start(bf16[36,8192]{1,0:T(8,128)(2,1)S(1)} %add_convert_fusion.10), channel_id=1, source_target_pairs={{0,8},{8,16},{16,24},{24,28},{28,20},{20,12},{12,4},{4,0},{1,9},{9... | collective-permute-start | bytes 1769480 | tf_op jit(solution)/shard_map/ppermute | solution.py:79
  60.8 14.6 %collective-permute-start.12 = (bf16[36,8192]{1,0:T(8,128)(2,1)S(1)}, bf16[36,8192]{1,0:T(8,128)(2,1)S(1)}, u32[]{:S(2)}, u32[]{:S(2)}) collective-permute-start(bf16[36,8192]{1,0:T(8,128)(2,1)S(1)} %add_convert_fusion.3), channel_id=1, source_target_pairs={{8,0},{16,8},{24,16},{28,24},{20,28},{12,20},{4,12},{0,4},{9,1},{1... | collective-permute-start | bytes 1769480 | tf_op jit(solution)/shard_map/ppermute | solution.py:80
  69.4 14.6 %collective-permute-start.5 = (bf16[36,8192]{1,0:T(8,128)(2,1)S(1)}, bf16[36,8192]{1,0:T(8,128)(2,1)S(1)}, u32[]{:S(2)}, u32[]{:S(2)}) collective-permute-start(bf16[36,8192]{1,0:T(8,128)(2,1)S(1)} %add_convert_fusion.9), channel_id=1, source_target_pairs={{0,8},{8,16},{16,24},{24,28},{28,20},{20,12},{12,4},{4,0},{1,9},{9... | collective-permute-start | bytes 1769480 | tf_op jit(solution)/shard_map/ppermute | solution.py:79
  75.7 14.7 %collective-permute-start.13 = (bf16[36,8192]{1,0:T(8,128)(2,1)S(1)}, bf16[36,8192]{1,0:T(8,128)(2,1)S(1)}, u32[]{:S(2)}, u32[]{:S(2)}) collective-permute-start(bf16[36,8192]{1,0:T(8,128)(2,1)S(1)} %add_convert_fusion.2), channel_id=1, source_target_pairs={{8,0},{16,8},{24,16},{28,24},{20,28},{12,20},{4,12},{0,4},{9,1},{1... | collective-permute-start | bytes 1769480 | tf_op jit(solution)/shard_map/ppermute | solution.py:80
  84.3 14.7 %collective-permute-start.6 = (bf16[36,8192]{1,0:T(8,128)(2,1)S(1)}, bf16[36,8192]{1,0:T(8,128)(2,1)S(1)}, u32[]{:S(2)}, u32[]{:S(2)}) collective-permute-start(bf16[36,8192]{1,0:T(8,128)(2,1)S(1)} %add_convert_fusion.8), channel_id=1, source_target_pairs={{0,8},{8,16},{16,24},{24,28},{28,20},{20,12},{12,4},{4,0},{1,9},{9... | collective-permute-start | bytes 1769480 | tf_op jit(solution)/shard_map/ppermute | solution.py:79
  90.6 14.7 %collective-permute-start.14 = (bf16[36,8192]{1,0:T(8,128)(2,1)S(1)}, bf16[36,8192]{1,0:T(8,128)(2,1)S(1)}, u32[]{:S(2)}, u32[]{:S(2)}) collective-permute-start(bf16[36,8192]{1,0:T(8,128)(2,1)S(1)} %add_convert_fusion.1), channel_id=1, source_target_pairs={{8,0},{16,8},{24,16},{28,24},{20,28},{12,20},{4,12},{0,4},{9,1},{1... | collective-permute-start | bytes 1769480 | tf_op jit(solution)/shard_map/ppermute | solution.py:80
  99.2 14.5 %collective-permute-start.7 = (bf16[36,8192]{1,0:T(8,128)(2,1)S(1)}, bf16[36,8192]{1,0:T(8,128)(2,1)S(1)}, u32[]{:S(2)}, u32[]{:S(2)}) collective-permute-start(bf16[36,8192]{1,0:T(8,128)(2,1)S(1)} %add_convert_fusion.7), channel_id=1, source_target_pairs={{0,8},{8,16},{16,24},{24,28},{28,20},{20,12},{12,4},{4,0},{1,9},{9... | collective-permute-start | bytes 1769480 | tf_op jit(solution)/shard_map/ppermute | solution.py:79
  105.4 10.9 %collective-permute-start.15 = (bf16[36,8192]{1,0:T(8,128)(2,1)S(1)}, bf16[36,8192]{1,0:T(8,128)(2,1)S(1)}, u32[]{:S(2)}, u32[]{:S(2)}) collective-permute-start(bf16[36,8192]{1,0:T(8,128)(2,1)S(1)} %add_convert_fusion), channel_id=1, source_target_pairs={{8,0},{16,8},{24,16},{28,24},{20,28},{12,20},{4,12},{0,4},{9,1},{1... | collective-permute-start | bytes 1769480 | tf_op jit(solution)/shard_map/ppermute | solution.py:80
  113.9 10.8 %collective-permute-start.8 = (bf16[36,8192]{1,0:T(8,128)(2,1)S(1)}, bf16[36,8192]{1,0:T(8,128)(2,1)S(1)}, u32[]{:S(2)}, u32[]{:S(2)}) collective-permute-start(bf16[36,8192]{1,0:T(8,128)(2,1)S(1)} %add_convert_fusion.6), channel_id=1, source_target_pairs={{0,8},{8,16},{16,24},{24,28},{28,20},{20,12},{12,4},{4,0},{1,9},{9... | collective-permute-start | bytes 1769480 | tf_op jit(solution)/shard_map/ppermute | solution.py:79
  126.2 3.8 %collective-permute-start.16 = (f32[1,1]{1,0:T(1,128)}, f32[1,1]{1,0:T(1,128)}, u32[]{:S(2)}, u32[]{:S(2)}) collective-permute-start(f32[1,1]{1,0:T(1,128)} %bitcast.4), channel_id=1, source_target_pairs={{0,4},{4,0},{8,12},{12,8},{16,20},{20,16},{24,28},{28,24},{1,5},{5... | collective-permute-start | bytes 20 | tf_op jit(solution)/shard_map/ppermute | solution.py:41
  131.2 3.7 %collective-permute-start.17 = (f32[1,1]{1,0:T(1,128)}, f32[1,1]{1,0:T(1,128)}, u32[]{:S(2)}, u32[]{:S(2)}) collective-permute-start(f32[1,1]{1,0:T(1,128)} %add.323), channel_id=1, source_target_pairs={{0,8},{4,12},{8,0},{12,4},{16,24},{20,28},{24,16},{28,20},{1,9},{5... | collective-permute-start | bytes 20 | tf_op jit(solution)/shard_map/ppermute | solution.py:41
  135.4 4.6 %collective-permute-start.18 = (f32[1,1]{1,0:T(1,128)}, f32[1,1]{1,0:T(1,128)}, u32[]{:S(2)}, u32[]{:S(2)}) collective-permute-start(f32[1,1]{1,0:T(1,128)} %add.324), channel_id=1, source_target_pairs={{0,16},{4,20},{8,24},{12,28},{16,0},{20,4},{24,8},{28,12},{1,17},{... | collective-permute-start | bytes 20 | tf_op jit(solution)/shard_map/ppermute | solution.py:41
  142.5 3.7 %collective-permute-start.20 = (f32[1,1]{1,0:T(1,128)}, f32[1,1]{1,0:T(1,128)}, u32[]{:S(2)}, u32[]{:S(2)}) collective-permute-start(f32[1,1]{1,0:T(1,128)} %add.326), channel_id=1, source_target_pairs={{0,2},{1,3},{2,0},{3,1},{4,6},{5,7},{6,4},{7,5},{8,10},{9,11},{10,... | collective-permute-start | bytes 20 | tf_op jit(solution)/shard_map/ppermute | solution.py:41
  163.9 17.9 %collective-permute-start.35 = (bf16[24,8192]{1,0:T(8,128)(2,1)S(1)}, bf16[24,8192]{1,0:T(8,128)(2,1)S(1)}, u32[]{:S(2)}, u32[]{:S(2)}) collective-permute-start(bf16[24,8192]{1,0:T(8,128)(2,1)S(1)} %get-tuple-element.37), channel_id=1, source_target_pairs={{0,8},{8,16},{16,24},{24,28},{28,20},{20,12},{12,4},{4,0},{1,9},{9... | collective-permute-start | bytes 1179656 | tf_op jit(solution)/shard_map/ppermute | solution.py:122
  165.1 16.7 %collective-permute-start.42 = (bf16[24,8192]{1,0:T(8,128)(2,1)S(1)}, bf16[24,8192]{1,0:T(8,128)(2,1)S(1)}, u32[]{:S(2)}, u32[]{:S(2)}) collective-permute-start(bf16[24,8192]{1,0:T(8,128)(2,1)S(1)} %get-tuple-element.38), channel_id=1, source_target_pairs={{8,0},{16,8},{24,16},{28,24},{20,28},{12,20},{4,12},{0,4},{9,1},{1... | collective-permute-start | bytes 1179656 | tf_op jit(solution)/shard_map/ppermute | solution.py:123
  171.1 18.6 %collective-permute-start.21 = (bf16[36,8192]{1,0:T(8,128)(2,1)S(1)}, bf16[36,8192]{1,0:T(8,128)(2,1)S(1)}, u32[]{:S(2)}, u32[]{:S(2)}) collective-permute-start(bf16[36,8192]{1,0:T(8,128)(2,1)S(1)} %get-tuple-element.43), channel_id=1, source_target_pairs={{0,8},{8,16},{16,24},{24,28},{28,20},{20,12},{12,4},{4,0},{1,9},{9... | collective-permute-start | bytes 1769480 | tf_op jit(solution)/shard_map/ppermute | solution.py:120
  172.2 19.7 %collective-permute-start.28 = (bf16[36,8192]{1,0:T(8,128)(2,1)S(1)}, bf16[36,8192]{1,0:T(8,128)(2,1)S(1)}, u32[]{:S(2)}, u32[]{:S(2)}) collective-permute-start(bf16[36,8192]{1,0:T(8,128)(2,1)S(1)} %get-tuple-element.44), channel_id=1, source_target_pairs={{8,0},{16,8},{24,16},{28,24},{20,28},{12,20},{4,12},{0,4},{9,1},{1... | collective-permute-start | bytes 1769480 | tf_op jit(solution)/shard_map/ppermute | solution.py:121
  182.0 16.2 %collective-permute-start.36 = (bf16[24,8192]{1,0:T(8,128)(2,1)S(1)}, bf16[24,8192]{1,0:T(8,128)(2,1)S(1)}, u32[]{:S(2)}, u32[]{:S(2)}) collective-permute-start(bf16[24,8192]{1,0:T(8,128)(2,1)S(1)} %get-tuple-element.35), channel_id=1, source_target_pairs={{0,8},{8,16},{16,24},{24,28},{28,20},{20,12},{12,4},{4,0},{1,9},{9... | collective-permute-start | bytes 1179656 | tf_op jit(solution)/shard_map/ppermute | solution.py:122
  183.2 16.2 %collective-permute-start.43 = (bf16[24,8192]{1,0:T(8,128)(2,1)S(1)}, bf16[24,8192]{1,0:T(8,128)(2,1)S(1)}, u32[]{:S(2)}, u32[]{:S(2)}) collective-permute-start(bf16[24,8192]{1,0:T(8,128)(2,1)S(1)} %get-tuple-element.36), channel_id=1, source_target_pairs={{8,0},{16,8},{24,16},{28,24},{20,28},{12,20},{4,12},{0,4},{9,1},{1... | collective-permute-start | bytes 1179656 | tf_op jit(solution)/shard_map/ppermute | solution.py:123
  189.8 22.5 %collective-permute-start.22 = (bf16[36,8192]{1,0:T(8,128)(2,1)S(1)}, bf16[36,8192]{1,0:T(8,128)(2,1)S(1)}, u32[]{:S(2)}, u32[]{:S(2)}) collective-permute-start(bf16[36,8192]{1,0:T(8,128)(2,1)S(1)} %collective-permute-done.21), channel_id=1, source_target_pairs={{0,8},{8,16},{16,24},{24,28},{28,20},{20,12},{12,4},{4,0},{1,9},{9... | collective-permute-start | bytes 1769480 | tf_op jit(solution)/shard_map/ppermute | solution.py:120
  191.9 21.5 %collective-permute-start.29 = (bf16[36,8192]{1,0:T(8,128)(2,1)S(1)}, bf16[36,8192]{1,0:T(8,128)(2,1)S(1)}, u32[]{:S(2)}, u32[]{:S(2)}) collective-permute-start(bf16[36,8192]{1,0:T(8,128)(2,1)S(1)} %collective-permute-done.28), channel_id=1, source_target_pairs={{8,0},{16,8},{24,16},{28,24},{20,28},{12,20},{4,12},{0,4},{9,1},{1... | collective-permute-start | bytes 1769480 | tf_op jit(solution)/shard_map/ppermute | solution.py:121
  199.6 21.1 %collective-permute-start.37 = (bf16[24,8192]{1,0:T(8,128)(2,1)S(1)}, bf16[24,8192]{1,0:T(8,128)(2,1)S(1)}, u32[]{:S(2)}, u32[]{:S(2)}) collective-permute-start(bf16[24,8192]{1,0:T(8,128)(2,1)S(1)} %get-tuple-element.33), channel_id=1, source_target_pairs={{0,8},{8,16},{16,24},{24,28},{28,20},{20,12},{12,4},{4,0},{1,9},{9... | collective-permute-start | bytes 1179656 | tf_op jit(solution)/shard_map/ppermute | solution.py:122
  201.2 20.6 %collective-permute-start.44 = (bf16[24,8192]{1,0:T(8,128)(2,1)S(1)}, bf16[24,8192]{1,0:T(8,128)(2,1)S(1)}, u32[]{:S(2)}, u32[]{:S(2)}) collective-permute-start(bf16[24,8192]{1,0:T(8,128)(2,1)S(1)} %get-tuple-element.34), channel_id=1, source_target_pairs={{8,0},{16,8},{24,16},{28,24},{20,28},{12,20},{4,12},{0,4},{9,1},{1... | collective-permute-start | bytes 1179656 | tf_op jit(solution)/shard_map/ppermute | solution.py:123
  212.2 32.4 %collective-permute-start.23 = (bf16[36,8192]{1,0:T(8,128)(2,1)S(1)}, bf16[36,8192]{1,0:T(8,128)(2,1)S(1)}, u32[]{:S(2)}, u32[]{:S(2)}) collective-permute-start(bf16[36,8192]{1,0:T(8,128)(2,1)S(1)} %collective-permute-done.22), channel_id=1, source_target_pairs={{0,8},{8,16},{16,24},{24,28},{28,20},{20,12},{12,4},{4,0},{1,9},{9... | collective-permute-start | bytes 1769480 | tf_op jit(solution)/shard_map/ppermute | solution.py:120
  213.5 33.8 %collective-permute-start.30 = (bf16[36,8192]{1,0:T(8,128)(2,1)S(1)}, bf16[36,8192]{1,0:T(8,128)(2,1)S(1)}, u32[]{:S(2)}, u32[]{:S(2)}) collective-permute-start(bf16[36,8192]{1,0:T(8,128)(2,1)S(1)} %collective-permute-done.29), channel_id=1, source_target_pairs={{8,0},{16,8},{24,16},{28,24},{20,28},{12,20},{4,12},{0,4},{9,1},{1... | collective-permute-start | bytes 1769480 | tf_op jit(solution)/shard_map/ppermute | solution.py:121
  222.1 19.3 %collective-permute-start.38 = (bf16[24,8192]{1,0:T(8,128)(2,1)S(1)}, bf16[24,8192]{1,0:T(8,128)(2,1)S(1)}, u32[]{:S(2)}, u32[]{:S(2)}) collective-permute-start(bf16[24,8192]{1,0:T(8,128)(2,1)S(1)} %get-tuple-element.31), channel_id=1, source_target_pairs={{0,8},{8,16},{16,24},{24,28},{28,20},{20,12},{12,4},{4,0},{1,9},{9... | collective-permute-start | bytes 1179656 | tf_op jit(solution)/shard_map/ppermute | solution.py:122
  223.7 18.7 %collective-permute-start.45 = (bf16[24,8192]{1,0:T(8,128)(2,1)S(1)}, bf16[24,8192]{1,0:T(8,128)(2,1)S(1)}, u32[]{:S(2)}, u32[]{:S(2)}) collective-permute-start(bf16[24,8192]{1,0:T(8,128)(2,1)S(1)} %get-tuple-element.32), channel_id=1, source_target_pairs={{8,0},{16,8},{24,16},{28,24},{20,28},{12,20},{4,12},{0,4},{9,1},{1... | collective-permute-start | bytes 1179656 | tf_op jit(solution)/shard_map/ppermute | solution.py:123
  242.6 12.1 %collective-permute-start.39 = (bf16[24,8192]{1,0:T(8,128)(2,1)S(1)}, bf16[24,8192]{1,0:T(8,128)(2,1)S(1)}, u32[]{:S(2)}, u32[]{:S(2)}) collective-permute-start(bf16[24,8192]{1,0:T(8,128)(2,1)S(1)} %get-tuple-element.29), channel_id=1, source_target_pairs={{0,8},{8,16},{16,24},{24,28},{28,20},{20,12},{12,4},{4,0},{1,9},{9... | collective-permute-start | bytes 1179656 | tf_op jit(solution)/shard_map/ppermute | solution.py:122
  244.2 12.1 %collective-permute-start.46 = (bf16[24,8192]{1,0:T(8,128)(2,1)S(1)}, bf16[24,8192]{1,0:T(8,128)(2,1)S(1)}, u32[]{:S(2)}, u32[]{:S(2)}) collective-permute-start(bf16[24,8192]{1,0:T(8,128)(2,1)S(1)} %get-tuple-element.30), channel_id=1, source_target_pairs={{8,0},{16,8},{24,16},{28,24},{20,28},{12,20},{4,12},{0,4},{9,1},{1... | collective-permute-start | bytes 1179656 | tf_op jit(solution)/shard_map/ppermute | solution.py:123
  244.6 24.1 %collective-permute-start.24 = (bf16[36,8192]{1,0:T(8,128)(2,1)S(1)}, bf16[36,8192]{1,0:T(8,128)(2,1)S(1)}, u32[]{:S(2)}, u32[]{:S(2)}) collective-permute-start(bf16[36,8192]{1,0:T(8,128)(2,1)S(1)} %collective-permute-done.23), channel_id=1, source_target_pairs={{0,8},{8,16},{16,24},{24,28},{28,20},{20,12},{12,4},{4,0},{1,9},{9... | collective-permute-start | bytes 1769480 | tf_op jit(solution)/shard_map/ppermute | solution.py:120
  247.3 23.0 %collective-permute-start.31 = (bf16[36,8192]{1,0:T(8,128)(2,1)S(1)}, bf16[36,8192]{1,0:T(8,128)(2,1)S(1)}, u32[]{:S(2)}, u32[]{:S(2)}) collective-permute-start(bf16[36,8192]{1,0:T(8,128)(2,1)S(1)} %collective-permute-done.30), channel_id=1, source_target_pairs={{8,0},{16,8},{24,16},{28,24},{20,28},{12,20},{4,12},{0,4},{9,1},{1... | collective-permute-start | bytes 1769480 | tf_op jit(solution)/shard_map/ppermute | solution.py:121
  256.4 20.7 %collective-permute-start.40 = (bf16[24,8192]{1,0:T(8,128)(2,1)S(1)}, bf16[24,8192]{1,0:T(8,128)(2,1)S(1)}, u32[]{:S(2)}, u32[]{:S(2)}) collective-permute-start(bf16[24,8192]{1,0:T(8,128)(2,1)S(1)} %get-tuple-element.27), channel_id=1, source_target_pairs={{0,8},{8,16},{16,24},{24,28},{28,20},{20,12},{12,4},{4,0},{1,9},{9... | collective-permute-start | bytes 1179656 | tf_op jit(solution)/shard_map/ppermute | solution.py:122
  257.5 21.3 %collective-permute-start.47 = (bf16[24,8192]{1,0:T(8,128)(2,1)S(1)}, bf16[24,8192]{1,0:T(8,128)(2,1)S(1)}, u32[]{:S(2)}, u32[]{:S(2)}) collective-permute-start(bf16[24,8192]{1,0:T(8,128)(2,1)S(1)} %get-tuple-element.28), channel_id=1, source_target_pairs={{8,0},{16,8},{24,16},{28,24},{20,28},{12,20},{4,12},{0,4},{9,1},{1... | collective-permute-start | bytes 1179656 | tf_op jit(solution)/shard_map/ppermute | solution.py:123
  268.7 30.7 %collective-permute-start.25 = (bf16[36,8192]{1,0:T(8,128)(2,1)S(1)}, bf16[36,8192]{1,0:T(8,128)(2,1)S(1)}, u32[]{:S(2)}, u32[]{:S(2)}) collective-permute-start(bf16[36,8192]{1,0:T(8,128)(2,1)S(1)} %collective-permute-done.24), channel_id=1, source_target_pairs={{0,8},{8,16},{16,24},{24,28},{28,20},{20,12},{12,4},{4,0},{1,9},{9... | collective-permute-start | bytes 1769480 | tf_op jit(solution)/shard_map/ppermute | solution.py:120
  270.3 31.1 %collective-permute-start.32 = (bf16[36,8192]{1,0:T(8,128)(2,1)S(1)}, bf16[36,8192]{1,0:T(8,128)(2,1)S(1)}, u32[]{:S(2)}, u32[]{:S(2)}) collective-permute-start(bf16[36,8192]{1,0:T(8,128)(2,1)S(1)} %collective-permute-done.31), channel_id=1, source_target_pairs={{8,0},{16,8},{24,16},{28,24},{20,28},{12,20},{4,12},{0,4},{9,1},{1... | collective-permute-start | bytes 1769480 | tf_op jit(solution)/shard_map/ppermute | solution.py:121
  278.9 17.8 %collective-permute-start.41 = (bf16[24,8192]{1,0:T(8,128)(2,1)S(1)}, bf16[24,8192]{1,0:T(8,128)(2,1)S(1)}, u32[]{:S(2)}, u32[]{:S(2)}) collective-permute-start(bf16[24,8192]{1,0:T(8,128)(2,1)S(1)} %get-tuple-element.25), channel_id=1, source_target_pairs={{0,8},{8,16},{16,24},{24,28},{28,20},{20,12},{12,4},{4,0},{1,9},{9... | collective-permute-start | bytes 1179656 | tf_op jit(solution)/shard_map/ppermute | solution.py:122
  279.9 18.1 %collective-permute-start.48 = (bf16[24,8192]{1,0:T(8,128)(2,1)S(1)}, bf16[24,8192]{1,0:T(8,128)(2,1)S(1)}, u32[]{:S(2)}, u32[]{:S(2)}) collective-permute-start(bf16[24,8192]{1,0:T(8,128)(2,1)S(1)} %get-tuple-element.26), channel_id=1, source_target_pairs={{8,0},{16,8},{24,16},{28,24},{20,28},{12,20},{4,12},{0,4},{9,1},{1... | collective-permute-start | bytes 1179656 | tf_op jit(solution)/shard_map/ppermute | solution.py:123
  299.4 14.9 %collective-permute-start.26 = (bf16[36,8192]{1,0:T(8,128)(2,1)S(1)}, bf16[36,8192]{1,0:T(8,128)(2,1)S(1)}, u32[]{:S(2)}, u32[]{:S(2)}) collective-permute-start(bf16[36,8192]{1,0:T(8,128)(2,1)S(1)} %collective-permute-done.25), channel_id=1, source_target_pairs={{0,8},{8,16},{16,24},{24,28},{28,20},{20,12},{12,4},{4,0},{1,9},{9... | collective-permute-start | bytes 1769480 | tf_op jit(solution)/shard_map/ppermute | solution.py:120
  301.4 14.9 %collective-permute-start.33 = (bf16[36,8192]{1,0:T(8,128)(2,1)S(1)}, bf16[36,8192]{1,0:T(8,128)(2,1)S(1)}, u32[]{:S(2)}, u32[]{:S(2)}) collective-permute-start(bf16[36,8192]{1,0:T(8,128)(2,1)S(1)} %collective-permute-done.32), channel_id=1, source_target_pairs={{8,0},{16,8},{24,16},{28,24},{20,28},{12,20},{4,12},{0,4},{9,1},{1... | collective-permute-start | bytes 1769480 | tf_op jit(solution)/shard_map/ppermute | solution.py:121
  314.3 12.7 %collective-permute-start.27 = (bf16[36,8192]{1,0:T(8,128)(2,1)S(1)}, bf16[36,8192]{1,0:T(8,128)(2,1)S(1)}, u32[]{:S(2)}, u32[]{:S(2)}) collective-permute-start(bf16[36,8192]{1,0:T(8,128)(2,1)S(1)} %collective-permute-done.26), channel_id=1, source_target_pairs={{0,8},{8,16},{16,24},{24,28},{28,20},{20,12},{12,4},{4,0},{1,9},{9... | collective-permute-start | bytes 1769480 | tf_op jit(solution)/shard_map/ppermute | solution.py:120
  316.3 12.5 %collective-permute-start.34 = (bf16[36,8192]{1,0:T(8,128)(2,1)S(1)}, bf16[36,8192]{1,0:T(8,128)(2,1)S(1)}, u32[]{:S(2)}, u32[]{:S(2)}) collective-permute-start(bf16[36,8192]{1,0:T(8,128)(2,1)S(1)} %collective-permute-done.33), channel_id=1, source_target_pairs={{8,0},{16,8},{24,16},{28,24},{20,28},{12,20},{4,12},{0,4},{9,1},{1... | collective-permute-start | bytes 1769480 | tf_op jit(solution)/shard_map/ppermute | solution.py:121
  (10 other events, 179.9 us)

commit v3 on v2

--- a/solution.py
+++ b/solution.py
@@ -117,10 +117,10 @@
         sum_a = avg_l[n - 1]
         sum_b = avg_r[1]
         for t in range(n - 1):
-            send_a = lax.ppermute(send_a, "dp", fwd)
-            send_b = lax.ppermute(send_b, "dp", bwd)
-            got_a = lax.ppermute(sum_a, "dp", fwd)
-            got_b = lax.ppermute(sum_b, "dp", bwd)
+            both_a = lax.ppermute(jnp.concatenate([send_a, sum_a], axis=0), "dp", fwd)
+            both_b = lax.ppermute(jnp.concatenate([send_b, sum_b], axis=0), "dp", bwd)
+            send_a, got_a = both_a[:cap], both_a[cap:]
+            send_b, got_b = both_b[:cap], both_b[cap:]
             out_a = out_a + spread(send_a, n - 1 - t)
             out_b = out_b + spread(send_b, 1 + t)
             fin_a = got_a.astype(jnp.float32) + avg_l[(2 * n - 2 - t) % n].astype(jnp.float32)

time: 340 us -> 356 us (1.047)
  matrix products: 25.8 us -> 44.4 us
  starting transfers between devices: 58.4 us -> 44.3 us
  waiting for transfers between devices: 194 us -> 202 us
    dot_general x16, matrix products: 16.4 us -> 34.9 us  [spread(): jnp.dot(placing_t[:, k * cap:(k + 1) * cap], chunk, preferred_element_typ...]
    ppermute x28 -> x14, starting transfers between devices: 29.7 us -> 15.7 us  [the longest x7 7.94 us: on_device(): both_b = lax.ppermute(jnp.concatenate([send_b, sum_b], axis=0), 'dp', bwd)]
    ppermute x28 -> x14, waiting for transfers between devices: 106 us -> 114 us  [the longest x7 84.2 us: on_device(): both_b = lax.ppermute(jnp.concatenate([send_b, sum_b], axis=0), 'dp', bwd)]
    unnamed x21 -> x35, local copies, waits for them, and re-layouts: 11.5 us -> 11.9 us
  transfers between devices with their start and end apart: 49 -> 35, of which waited for: 38 -> 31; matrix products, arithmetic and copies ran while one was open for 16% -> 16% of each run, Pallas kernels for 0% -> 0%
where the time goes in v3:
time: 356 us; the launch traced here: 350 us
  waiting for transfers between devices  202 us (57%)
  matrix products  44.4 us (12%)
  starting transfers between devices  44.3 us (12%)
  other arithmetic  36.9 us (10%)
  local copies, waits for them, and re-layouts  16.8 us (5%)
  between operations  5.6 us (2%)
    ppermute x7, waiting for transfers between devices, on_device(): both_b = lax.ppermute(jnp.concatenate([send_b, sum_b], axis=0), 'dp', bwd)  84.2 us
    ppermute x7, waiting for transfers between devices, on_device(): got_a = lax.ppermute(send_a, 'dp', fwd)  51.9 us
    dot_general x16, matrix products, spread(): jnp.dot(placing_t[:, k * cap:(k + 1) * cap], chunk, preferred_element_typ...  34.9 us
    ppermute x7, waiting for transfers between devices, on_device(): got_b = lax.ppermute(send_b, 'dp', bwd)  30.9 us
    ppermute x7, waiting for transfers between devices, on_device(): both_a = lax.ppermute(jnp.concatenate([send_a, sum_a], axis=0), 'dp', fwd)  29.8 us
    unnamed x35, local copies, waits for them, and re-layouts  11.9 us
    ppermute x5, starting transfers between devices, all_sum(): v = v + lax.ppermute(v, axis, [(i, i ^ k) for i in range(n)])  11.3 us
    ppermute x7, starting transfers between devices, on_device(): got_b = lax.ppermute(send_b, 'dp', bwd)  9.83 us
  transfers between devices with their start and end apart: 35, of which 31 were waited for; matrix products, arithmetic and copies ran while one was open for 16% of the time, Pallas kernels for 0%

profile of v3, /device:TPU:0, one launch (start us, length us, event | category | flops | bytes accessed | tf_op | source)
XLA Modules:
  0.0 350.0 jit_solution(16155986112094879724)
XLA Ops:
  0.6 3.1 collective-permute-start
  7.3 3.4 fusion.10
  10.9 2.0 collective-permute-start.9
  12.9 3.6 %fusion.12 = bf16[288,8192]{1,0:T(8,128)(2,1)} fusion(bf16[192,16384]{1,0:T(8,128)(2,1)S(1)} %bitcast.122, s32[192]{0:T(256)S(1)} %fusion.80), kind=kOutput, calls=%fused_computation.21 | convolution fusion | flops 906024960 | bytes 7865344 | tf_op jit(solution)/shard_map/dot_general | solution.py:73
  20.4 2.0 slice_add_fusion
  22.5 4.6 %collective-permute-done.9 = bf16[36,8192]{1,0:T(8,128)(2,1)S(1)} collective-permute-done((bf16[36,8192]{1,0:T(8,128)(2,1)S(1)}, bf16[36,8192]{1,0:T(8,128)(2,1)S(1)}, u32[]{:S(2)}, u32[]{:S(2)}) %collective-permute-start.9) | collective-permute-done | bytes 589856 | tf_op jit(solution)/shard_map/ppermute | solution.py:80
  28.4 1.7 collective-permute-start.10
  30.1 8.0 %collective-permute-done.2 = bf16[36,8192]{1,0:T(8,128)(2,1)S(1)} collective-permute-done((bf16[36,8192]{1,0:T(8,128)(2,1)S(1)}, bf16[36,8192]{1,0:T(8,128)(2,1)S(1)}, u32[]{:S(2)}, u32[]{:S(2)}) %collective-permute-start.2) | collective-permute-done | bytes 589856 | tf_op jit(solution)/shard_map/ppermute | solution.py:79
  39.8 3.9 %collective-permute-done.10 = bf16[36,8192]{1,0:T(8,128)(2,1)S(1)} collective-permute-done((bf16[36,8192]{1,0:T(8,128)(2,1)S(1)}, bf16[36,8192]{1,0:T(8,128)(2,1)S(1)}, u32[]{:S(2)}, u32[]{:S(2)}) %collective-permute-start.10) | collective-permute-done | bytes 589856 | tf_op jit(solution)/shard_map/ppermute | solution.py:80
  46.5 7.6 %collective-permute-done.3 = bf16[36,8192]{1,0:T(8,128)(2,1)S(1)} collective-permute-done((bf16[36,8192]{1,0:T(8,128)(2,1)S(1)}, bf16[36,8192]{1,0:T(8,128)(2,1)S(1)}, u32[]{:S(2)}, u32[]{:S(2)}) %collective-permute-start.3) | collective-permute-done | bytes 589856 | tf_op jit(solution)/shard_map/ppermute | solution.py:79
  55.1 4.4 %collective-permute-done.11 = bf16[36,8192]{1,0:T(8,128)(2,1)S(1)} collective-permute-done((bf16[36,8192]{1,0:T(8,128)(2,1)S(1)}, bf16[36,8192]{1,0:T(8,128)(2,1)S(1)}, u32[]{:S(2)}, u32[]{:S(2)}) %collective-permute-start.11) | collective-permute-done | bytes 589856 | tf_op jit(solution)/shard_map/ppermute | solution.py:80
  61.9 7.2 %collective-permute-done.4 = bf16[36,8192]{1,0:T(8,128)(2,1)S(1)} collective-permute-done((bf16[36,8192]{1,0:T(8,128)(2,1)S(1)}, bf16[36,8192]{1,0:T(8,128)(2,1)S(1)}, u32[]{:S(2)}, u32[]{:S(2)}) %collective-permute-start.4) | collective-permute-done | bytes 589856 | tf_op jit(solution)/shard_map/ppermute | solution.py:79
  70.0 5.4 %collective-permute-done.12 = bf16[36,8192]{1,0:T(8,128)(2,1)S(1)} collective-permute-done((bf16[36,8192]{1,0:T(8,128)(2,1)S(1)}, bf16[36,8192]{1,0:T(8,128)(2,1)S(1)}, u32[]{:S(2)}, u32[]{:S(2)}) %collective-permute-start.12) | collective-permute-done | bytes 589856 | tf_op jit(solution)/shard_map/ppermute | solution.py:80
  76.8 7.1 %collective-permute-done.5 = bf16[36,8192]{1,0:T(8,128)(2,1)S(1)} collective-permute-done((bf16[36,8192]{1,0:T(8,128)(2,1)S(1)}, bf16[36,8192]{1,0:T(8,128)(2,1)S(1)}, u32[]{:S(2)}, u32[]{:S(2)}) %collective-permute-start.5) | collective-permute-done | bytes 589856 | tf_op jit(solution)/shard_map/ppermute | solution.py:79
  84.9 5.5 %collective-permute-done.13 = bf16[36,8192]{1,0:T(8,128)(2,1)S(1)} collective-permute-done((bf16[36,8192]{1,0:T(8,128)(2,1)S(1)}, bf16[36,8192]{1,0:T(8,128)(2,1)S(1)}, u32[]{:S(2)}, u32[]{:S(2)}) %collective-permute-start.13) | collective-permute-done | bytes 589856 | tf_op jit(solution)/shard_map/ppermute | solution.py:80
  91.7 7.2 %collective-permute-done.6 = bf16[36,8192]{1,0:T(8,128)(2,1)S(1)} collective-permute-done((bf16[36,8192]{1,0:T(8,128)(2,1)S(1)}, bf16[36,8192]{1,0:T(8,128)(2,1)S(1)}, u32[]{:S(2)}, u32[]{:S(2)}) %collective-permute-start.6) | collective-permute-done | bytes 589856 | tf_op jit(solution)/shard_map/ppermute | solution.py:79
  99.8 5.4 %collective-permute-done.14 = bf16[36,8192]{1,0:T(8,128)(2,1)S(1)} collective-permute-done((bf16[36,8192]{1,0:T(8,128)(2,1)S(1)}, bf16[36,8192]{1,0:T(8,128)(2,1)S(1)}, u32[]{:S(2)}, u32[]{:S(2)}) %collective-permute-start.14) | collective-permute-done | bytes 589856 | tf_op jit(solution)/shard_map/ppermute | solution.py:80
  106.6 6.9 %collective-permute-done.7 = bf16[36,8192]{1,0:T(8,128)(2,1)S(1)} collective-permute-done((bf16[36,8192]{1,0:T(8,128)(2,1)S(1)}, bf16[36,8192]{1,0:T(8,128)(2,1)S(1)}, u32[]{:S(2)}, u32[]{:S(2)}) %collective-permute-start.7) | collective-permute-done | bytes 589856 | tf_op jit(solution)/shard_map/ppermute | solution.py:79
  116.6 8.0 %collective-permute-done.8 = bf16[36,8192]{1,0:T(8,128)(2,1)S(1)} collective-permute-done((bf16[36,8192]{1,0:T(8,128)(2,1)S(1)}, bf16[36,8192]{1,0:T(8,128)(2,1)S(1)}, u32[]{:S(2)}, u32[]{:S(2)}) %collective-permute-start.8) | collective-permute-done | bytes 589856 | tf_op jit(solution)/shard_map/ppermute | solution.py:79
  127.6 2.1 collective-permute-done.16
  131.0 2.5 collective-permute-start.17
  135.2 3.5 %collective-permute-start.18 = (f32[1,1]{1,0:T(1,128)}, f32[1,1]{1,0:T(1,128)}, u32[]{:S(2)}, u32[]{:S(2)}) collective-permute-start(f32[1,1]{1,0:T(1,128)} %add.324), channel_id=1, source_target_pairs={{0,16},{4,20},{8,24},{12,28},{16,0},{20,4},{24,8},{28,12},{1,17},{... | collective-permute-start | bytes 20 | tf_op jit(solution)/shard_map/ppermute | solution.py:41
  142.2 2.9 collective-permute-start.20
  146.6 7.1 %fusion.24 = bf16[36,16384]{1,0:T(8,128)(2,1)S(1)} fusion(f32[1,36,16384]{2,0,1:T(1,128)S(1)} %copy-done.7, f32[1,36,16384]{2,0,1:T(1,128)S(1)} %copy-done.8, f32[1,36,16384]{2,0,1:T(1,128)S(1)} %copy-done.9, f32[36,8192]{1,0:T(8,128)S(1)} %get-tuple-element.41, f32[36,8192]{1,0:T(8,128)S(1)} %get-tuple-element.39, f32[]{:T(128)} %bitcast.5, ...), kind=kLoop, calls=%fused_computation.37 | loop fusion | flops 12386304 | bytes 10616980 | tf_op jit(solution)/shard_map/convert_element_type | solution.py:108
  153.8 7.3 %subtract_multiply_fusion = (f32[1,36,16384]{2,1,0:T(8,128)S(1)}, f32[1,36,16384]{2,1,0:T(8,128)S(1)}, f32[1,36,16384]{2,1,0:T(8,128)S(1)}) fusion(f32[1,36,16384]{2,0,1:T(1,128)S(1)} %copy-done.7, f32[36]{0:T(128)S(1)} %convert_element_type.304, f32[1,36,8192]{2,1,0:T(8,128)S(1)} %get-tuple-element.42, f32[1,36,8192]{2,1,0:T(8,128)S(1)} %get-tuple-element.40, ...), kind=kLoop, calls=%fused_computation.46 | loop fusion | flops 11796480 | bytes 16515220 | tf_op jit(solution)/shard_map/mul | solution.py:96
  161.1 2.5 fusion.30
  166.5 21.7 %collective-permute-done.28 = bf16[60,8192]{1,0:T(8,128)(2,1)S(1)} collective-permute-done((bf16[60,8192]{1,0:T(8,128)(2,1)S(1)}, bf16[60,8192]{1,0:T(8,128)(2,1)S(1)}, u32[]{:S(2)}, u32[]{:S(2)}) %collective-permute-start.28) | collective-permute-done | bytes 983072 | tf_op jit(solution)/shard_map/ppermute | solution.py:121
  188.2 1.8 collective-permute-done.21
  192.8 20.8 %collective-permute-done.29 = bf16[60,8192]{1,0:T(8,128)(2,1)S(1)} collective-permute-done((bf16[60,8192]{1,0:T(8,128)(2,1)S(1)}, bf16[60,8192]{1,0:T(8,128)(2,1)S(1)}, u32[]{:S(2)}, u32[]{:S(2)}) %collective-permute-start.29) | collective-permute-done | bytes 983072 | tf_op jit(solution)/shard_map/ppermute | solution.py:121
  218.0 19.6 %collective-permute-done.30 = bf16[60,8192]{1,0:T(8,128)(2,1)S(1)} collective-permute-done((bf16[60,8192]{1,0:T(8,128)(2,1)S(1)}, bf16[60,8192]{1,0:T(8,128)(2,1)S(1)}, u32[]{:S(2)}, u32[]{:S(2)}) %collective-permute-start.30) | collective-permute-done | bytes 983072 | tf_op jit(solution)/shard_map/ppermute | solution.py:121
  237.6 2.2 collective-permute-done.23
  242.8 3.8 %copy.35 = f32[1,36,16384]{2,0,1:T(1,128)} copy(f32[1,36,16384]{2,1,0:T(8,128)S(1)} %get-tuple-element.20) | data formatting | bytes 4718592
  246.6 3.8 %copy.36 = f32[1,36,16384]{2,0,1:T(1,128)} copy(f32[1,36,16384]{2,1,0:T(8,128)S(1)} %get-tuple-element.21) | data formatting | bytes 4718592
  250.4 3.8 %copy.37 = f32[1,36,16384]{2,0,1:T(1,128)} copy(f32[1,36,16384]{2,1,0:T(8,128)S(1)} %get-tuple-element.22) | data formatting | bytes 4718592
  255.3 6.3 %collective-permute-done.31 = bf16[60,8192]{1,0:T(8,128)(2,1)S(1)} collective-permute-done((bf16[60,8192]{1,0:T(8,128)(2,1)S(1)}, bf16[60,8192]{1,0:T(8,128)(2,1)S(1)}, u32[]{:S(2)}, u32[]{:S(2)}) %collective-permute-start.31) | collective-permute-done | bytes 983072 | tf_op jit(solution)/shard_map/ppermute | solution.py:121
  269.0 15.9 %collective-permute-done.32 = bf16[60,8192]{1,0:T(8,128)(2,1)S(1)} collective-permute-done((bf16[60,8192]{1,0:T(8,128)(2,1)S(1)}, bf16[60,8192]{1,0:T(8,128)(2,1)S(1)}, u32[]{:S(2)}, u32[]{:S(2)}) %collective-permute-start.32) | collective-permute-done | bytes 983072 | tf_op jit(solution)/shard_map/ppermute | solution.py:121
  284.9 1.8 collective-permute-done.25
  294.0 16.6 %collective-permute-done.26 = bf16[60,8192]{1,0:T(8,128)(2,1)S(1)} collective-permute-done((bf16[60,8192]{1,0:T(8,128)(2,1)S(1)}, bf16[60,8192]{1,0:T(8,128)(2,1)S(1)}, u32[]{:S(2)}, u32[]{:S(2)}) %collective-permute-start.26) | collective-permute-done | bytes 983072 | tf_op jit(solution)/shard_map/ppermute | solution.py:120
  313.7 2.7 fusion.60
  316.4 2.7 fusion.66
  319.1 2.8 fusion.56
  321.9 2.7 fusion.70
  324.6 4.4 %collective-permute-done.27 = bf16[60,8192]{1,0:T(8,128)(2,1)S(1)} collective-permute-done((bf16[60,8192]{1,0:T(8,128)(2,1)S(1)}, bf16[60,8192]{1,0:T(8,128)(2,1)S(1)}, u32[]{:S(2)}, u32[]{:S(2)}) %collective-permute-start.27) | collective-permute-done | bytes 983072 | tf_op jit(solution)/shard_map/ppermute | solution.py:120
  330.6 2.7 fusion.48
  333.3 2.7 fusion.46
  336.0 6.3 %fusion.9 = bf16[192,8192]{1,0:T(8,128)(2,1)} fusion(bf16[192,8192]{1,0:T(8,128)(2,1)} %fusion.48, bf16[192,8192]{1,0:T(8,128)(2,1)} %fusion.56, bf16[192,8192]{1,0:T(8,128)(2,1)} %fusion.60, bf16[192,8192]{1,0:T(8,128)(2,1)S(1)} %fusion.64, bf16[192,8192]{1,0:T(8,128)(2,1)S(1)} %fusion.68, bf16[192,8192]{1,0:T(8,128)(2,1)S(1)} %convolution_add_fusion.3, ...), kind=kOutput, calls=%fused_computation.15 | convolution fusion | flops 122683392 | bytes 22700032 | tf_op jit(solution)/shard_map/dot_general | solution.py:113
  342.3 4.1 %fusion.6 = bf16[192,8192]{1,0:T(8,128)(2,1)S(1)} fusion(bf16[192,8192]{1,0:T(8,128)(2,1)} %fusion.46, bf16[192,8192]{1,0:T(8,128)(2,1)S(1)} %copy-done.5, bf16[192,8192]{1,0:T(8,128)(2,1)S(1)} %copy-done.4, bf16[192,8192]{1,0:T(8,128)(2,1)S(1)} %fusion.62, bf16[192,8192]{1,0:T(8,128)(2,1)S(1)} %fusion.58, bf16[192,8192]{1,0:T(8,128)(2,1)S(1)} %convolution_add_fusion.1, ...), kind=kOutput, calls=%fused_computation.12 | convolution fusion | flops 122683392 | bytes 22700032 | tf_op jit(solution)/shard_map/dot_general | solution.py:113
  346.4 3.3 maximum_bitcast_fusion
  (152 shorter events, 66.9 us)
Async XLA Ops:
  0.6 19.2 %collective-permute-start = (bf16[8,128]{1,0:T(8,128)(2,1)S(1)}, bf16[8,128]{1,0:T(8,128)(2,1)S(1)}, u32[]{:S(2)}, u32[]{:S(2)}) collective-permute-start(bf16[8,128]{1,0:T(8,128)(2,1)S(1)} %broadcast_in_dim.9), channel_id=1, source_target_pairs={{0,8},{8,16},{16,24},{24,28},{28,20},{20,12},{12,4},{4,0},{1,9},{9... | collective-permute-start | bytes 6152 | tf_op jit(solution)/shard_map/ppermute | solution.py:63
  3.7 16.2 %collective-permute-start.1 = (bf16[8,128]{1,0:T(8,128)(2,1)S(1)}, bf16[8,128]{1,0:T(8,128)(2,1)S(1)}, u32[]{:S(2)}, u32[]{:S(2)}) collective-permute-start(bf16[8,128]{1,0:T(8,128)(2,1)S(1)} %broadcast_in_dim.9), channel_id=1, source_target_pairs={{8,0},{16,8},{24,16},{28,24},{20,28},{12,20},{4,12},{0,4},{9,1},{1... | collective-permute-start | bytes 6152 | tf_op jit(solution)/shard_map/ppermute | solution.py:63
  7.3 5.6 %copy-start.10 = (bf16[1,1,192,16384]{3,2,1,0:T(8,128)(2,1)S(1)}, bf16[1,1,192,16384]{3,2,1,0:T(8,128)(2,1)}, u32[]{:S(2)}) copy-start(bf16[1,1,192,16384]{3,2,1,0:T(8,128)(2,1)} %param.9) | copy-start | bytes 18874372
  10.7 5.8 %copy-start.2 = (bf16[288,8192]{1,0:T(8,128)(2,1)}, bf16[288,8192]{1,0:T(8,128)(2,1)S(1)}, u32[]{:S(2)}) copy-start(bf16[288,8192]{1,0:T(8,128)(2,1)S(1)} %fusion.10) | copy-start | bytes 14155780
  10.9 6.3 %copy-start = (s32[8]{0:T(128)S(1)}, s32[8]{0:T(128)}, u32[]{:S(2)}) copy-start(s32[8]{0:T(128)} %constant.80.clone) | copy-start | bytes 100
  10.9 16.2 %collective-permute-start.9 = (bf16[36,8192]{1,0:T(8,128)(2,1)S(1)}, bf16[36,8192]{1,0:T(8,128)(2,1)S(1)}, u32[]{:S(2)}, u32[]{:S(2)}) collective-permute-start(bf16[36,8192]{1,0:T(8,128)(2,1)S(1)} %slice.363), channel_id=1, source_target_pairs={{8,0},{16,8},{24,16},{28,24},{20,28},{12,20},{4,12},{0,4},{9,1},{1... | collective-permute-start | bytes 1769480 | tf_op jit(solution)/shard_map/ppermute | solution.py:80
  22.4 31.7 %copy-start.1 = (bf16[288,8192]{1,0:T(8,128)(2,1)S(1)}, bf16[288,8192]{1,0:T(8,128)(2,1)}, u32[]{:S(2)}) copy-start(bf16[288,8192]{1,0:T(8,128)(2,1)} %fusion.12) | copy-start | bytes 14155780
  22.4 15.7 %collective-permute-start.2 = (bf16[36,8192]{1,0:T(8,128)(2,1)S(1)}, bf16[36,8192]{1,0:T(8,128)(2,1)S(1)}, u32[]{:S(2)}, u32[]{:S(2)}) collective-permute-start(bf16[36,8192]{1,0:T(8,128)(2,1)S(1)} %slice_add_fusion), channel_id=1, source_target_pairs={{0,8},{8,16},{16,24},{24,28},{28,20},{20,12},{12,4},{4,0},{1,9},{9... | collective-permute-start | bytes 1769480 | tf_op jit(solution)/shard_map/ppermute | solution.py:79
  28.4 15.3 %collective-permute-start.10 = (bf16[36,8192]{1,0:T(8,128)(2,1)S(1)}, bf16[36,8192]{1,0:T(8,128)(2,1)S(1)}, u32[]{:S(2)}, u32[]{:S(2)}) collective-permute-start(bf16[36,8192]{1,0:T(8,128)(2,1)S(1)} %add_convert_fusion.5), channel_id=1, source_target_pairs={{8,0},{16,8},{24,16},{28,24},{20,28},{12,20},{4,12},{0,4},{9,1},{1... | collective-permute-start | bytes 1769480 | tf_op jit(solution)/shard_map/ppermute | solution.py:80
  39.4 14.8 %collective-permute-start.3 = (bf16[36,8192]{1,0:T(8,128)(2,1)S(1)}, bf16[36,8192]{1,0:T(8,128)(2,1)S(1)}, u32[]{:S(2)}, u32[]{:S(2)}) collective-permute-start(bf16[36,8192]{1,0:T(8,128)(2,1)S(1)} %add_convert_fusion.11), channel_id=1, source_target_pairs={{0,8},{8,16},{16,24},{24,28},{28,20},{20,12},{12,4},{4,0},{1,9},{9... | collective-permute-start | bytes 1769480 | tf_op jit(solution)/shard_map/ppermute | solution.py:79
  45.1 30.3 %copy-start.3 = (bf16[288,8192]{1,0:T(8,128)(2,1)S(1)}, bf16[288,8192]{1,0:T(8,128)(2,1)}, u32[]{:S(2)}) copy-start(bf16[288,8192]{1,0:T(8,128)(2,1)} %copy-done.2) | copy-start | bytes 14155780
  45.1 14.4 %collective-permute-start.11 = (bf16[36,8192]{1,0:T(8,128)(2,1)S(1)}, bf16[36,8192]{1,0:T(8,128)(2,1)S(1)}, u32[]{:S(2)}, u32[]{:S(2)}) collective-permute-start(bf16[36,8192]{1,0:T(8,128)(2,1)S(1)} %add_convert_fusion.4), channel_id=1, source_target_pairs={{8,0},{16,8},{24,16},{28,24},{20,28},{12,20},{4,12},{0,4},{9,1},{1... | collective-permute-start | bytes 1769480 | tf_op jit(solution)/shard_map/ppermute | solution.py:80
  54.4 14.7 %collective-permute-start.4 = (bf16[36,8192]{1,0:T(8,128)(2,1)S(1)}, bf16[36,8192]{1,0:T(8,128)(2,1)S(1)}, u32[]{:S(2)}, u32[]{:S(2)}) collective-permute-start(bf16[36,8192]{1,0:T(8,128)(2,1)S(1)} %add_convert_fusion.10), channel_id=1, source_target_pairs={{0,8},{8,16},{16,24},{24,28},{28,20},{20,12},{12,4},{4,0},{1,9},{9... | collective-permute-start | bytes 1769480 | tf_op jit(solution)/shard_map/ppermute | solution.py:79
  60.7 14.6 %collective-permute-start.12 = (bf16[36,8192]{1,0:T(8,128)(2,1)S(1)}, bf16[36,8192]{1,0:T(8,128)(2,1)S(1)}, u32[]{:S(2)}, u32[]{:S(2)}) collective-permute-start(bf16[36,8192]{1,0:T(8,128)(2,1)S(1)} %add_convert_fusion.3), channel_id=1, source_target_pairs={{8,0},{16,8},{24,16},{28,24},{20,28},{12,20},{4,12},{0,4},{9,1},{1... | collective-permute-start | bytes 1769480 | tf_op jit(solution)/shard_map/ppermute | solution.py:80
  69.3 14.6 %collective-permute-start.5 = (bf16[36,8192]{1,0:T(8,128)(2,1)S(1)}, bf16[36,8192]{1,0:T(8,128)(2,1)S(1)}, u32[]{:S(2)}, u32[]{:S(2)}) collective-permute-start(bf16[36,8192]{1,0:T(8,128)(2,1)S(1)} %add_convert_fusion.9), channel_id=1, source_target_pairs={{0,8},{8,16},{16,24},{24,28},{28,20},{20,12},{12,4},{4,0},{1,9},{9... | collective-permute-start | bytes 1769480 | tf_op jit(solution)/shard_map/ppermute | solution.py:79
  75.6 14.7 %collective-permute-start.13 = (bf16[36,8192]{1,0:T(8,128)(2,1)S(1)}, bf16[36,8192]{1,0:T(8,128)(2,1)S(1)}, u32[]{:S(2)}, u32[]{:S(2)}) collective-permute-start(bf16[36,8192]{1,0:T(8,128)(2,1)S(1)} %add_convert_fusion.2), channel_id=1, source_target_pairs={{8,0},{16,8},{24,16},{28,24},{20,28},{12,20},{4,12},{0,4},{9,1},{1... | collective-permute-start | bytes 1769480 | tf_op jit(solution)/shard_map/ppermute | solution.py:80
  84.2 14.7 %collective-permute-start.6 = (bf16[36,8192]{1,0:T(8,128)(2,1)S(1)}, bf16[36,8192]{1,0:T(8,128)(2,1)S(1)}, u32[]{:S(2)}, u32[]{:S(2)}) collective-permute-start(bf16[36,8192]{1,0:T(8,128)(2,1)S(1)} %add_convert_fusion.8), channel_id=1, source_target_pairs={{0,8},{8,16},{16,24},{24,28},{28,20},{20,12},{12,4},{4,0},{1,9},{9... | collective-permute-start | bytes 1769480 | tf_op jit(solution)/shard_map/ppermute | solution.py:79
  90.5 14.7 %collective-permute-start.14 = (bf16[36,8192]{1,0:T(8,128)(2,1)S(1)}, bf16[36,8192]{1,0:T(8,128)(2,1)S(1)}, u32[]{:S(2)}, u32[]{:S(2)}) collective-permute-start(bf16[36,8192]{1,0:T(8,128)(2,1)S(1)} %add_convert_fusion.1), channel_id=1, source_target_pairs={{8,0},{16,8},{24,16},{28,24},{20,28},{12,20},{4,12},{0,4},{9,1},{1... | collective-permute-start | bytes 1769480 | tf_op jit(solution)/shard_map/ppermute | solution.py:80
  99.1 14.4 %collective-permute-start.7 = (bf16[36,8192]{1,0:T(8,128)(2,1)S(1)}, bf16[36,8192]{1,0:T(8,128)(2,1)S(1)}, u32[]{:S(2)}, u32[]{:S(2)}) collective-permute-start(bf16[36,8192]{1,0:T(8,128)(2,1)S(1)} %add_convert_fusion.7), channel_id=1, source_target_pairs={{0,8},{8,16},{16,24},{24,28},{28,20},{20,12},{12,4},{4,0},{1,9},{9... | collective-permute-start | bytes 1769480 | tf_op jit(solution)/shard_map/ppermute | solution.py:79
  105.4 10.9 %collective-permute-start.15 = (bf16[36,8192]{1,0:T(8,128)(2,1)S(1)}, bf16[36,8192]{1,0:T(8,128)(2,1)S(1)}, u32[]{:S(2)}, u32[]{:S(2)}) collective-permute-start(bf16[36,8192]{1,0:T(8,128)(2,1)S(1)} %add_convert_fusion), channel_id=1, source_target_pairs={{8,0},{16,8},{24,16},{28,24},{20,28},{12,20},{4,12},{0,4},{9,1},{1... | collective-permute-start | bytes 1769480 | tf_op jit(solution)/shard_map/ppermute | solution.py:80
  113.7 10.9 %collective-permute-start.8 = (bf16[36,8192]{1,0:T(8,128)(2,1)S(1)}, bf16[36,8192]{1,0:T(8,128)(2,1)S(1)}, u32[]{:S(2)}, u32[]{:S(2)}) collective-permute-start(bf16[36,8192]{1,0:T(8,128)(2,1)S(1)} %add_convert_fusion.6), channel_id=1, source_target_pairs={{0,8},{8,16},{16,24},{24,28},{28,20},{20,12},{12,4},{4,0},{1,9},{9... | collective-permute-start | bytes 1769480 | tf_op jit(solution)/shard_map/ppermute | solution.py:79
  116.4 30.2 %copy-start.9 = (f32[1,36,16384]{2,0,1:T(1,128)S(1)}, f32[1,36,16384]{2,0,1:T(1,128)}, u32[]{:S(2)}) copy-start(f32[1,36,16384]{2,0,1:T(1,128)} %param.13) | copy-start | bytes 7077892
  116.6 30.0 %copy-start.7 = (f32[1,36,16384]{2,0,1:T(1,128)S(1)}, f32[1,36,16384]{2,0,1:T(1,128)}, u32[]{:S(2)}) copy-start(f32[1,36,16384]{2,0,1:T(1,128)} %param.11) | copy-start | bytes 7077892
  116.6 30.0 %copy-start.8 = (f32[1,36,16384]{2,0,1:T(1,128)S(1)}, f32[1,36,16384]{2,0,1:T(1,128)}, u32[]{:S(2)}) copy-start(f32[1,36,16384]{2,0,1:T(1,128)} %param.12) | copy-start | bytes 7077892
  126.0 3.6 %collective-permute-start.16 = (f32[1,1]{1,0:T(1,128)}, f32[1,1]{1,0:T(1,128)}, u32[]{:S(2)}, u32[]{:S(2)}) collective-permute-start(f32[1,1]{1,0:T(1,128)} %bitcast.4), channel_id=1, source_target_pairs={{0,4},{4,0},{8,12},{12,8},{16,20},{20,16},{24,28},{28,24},{1,5},{5... | collective-permute-start | bytes 20 | tf_op jit(solution)/shard_map/ppermute | solution.py:41
  131.0 3.6 %collective-permute-start.17 = (f32[1,1]{1,0:T(1,128)}, f32[1,1]{1,0:T(1,128)}, u32[]{:S(2)}, u32[]{:S(2)}) collective-permute-start(f32[1,1]{1,0:T(1,128)} %add.323), channel_id=1, source_target_pairs={{0,8},{4,12},{8,0},{12,4},{16,24},{20,28},{24,16},{28,20},{1,9},{5... | collective-permute-start | bytes 20 | tf_op jit(solution)/shard_map/ppermute | solution.py:41
  135.2 4.5 %collective-permute-start.18 = (f32[1,1]{1,0:T(1,128)}, f32[1,1]{1,0:T(1,128)}, u32[]{:S(2)}, u32[]{:S(2)}) collective-permute-start(f32[1,1]{1,0:T(1,128)} %add.324), channel_id=1, source_target_pairs={{0,16},{4,20},{8,24},{12,28},{16,0},{20,4},{24,8},{28,12},{1,17},{... | collective-permute-start | bytes 20 | tf_op jit(solution)/shard_map/ppermute | solution.py:41
  140.4 1.2 collective-permute-start.19
  142.2 3.6 %collective-permute-start.20 = (f32[1,1]{1,0:T(1,128)}, f32[1,1]{1,0:T(1,128)}, u32[]{:S(2)}, u32[]{:S(2)}) collective-permute-start(f32[1,1]{1,0:T(1,128)} %add.326), channel_id=1, source_target_pairs={{0,2},{1,3},{2,0},{3,1},{4,6},{5,7},{6,4},{7,5},{8,10},{9,11},{10,... | collective-permute-start | bytes 20 | tf_op jit(solution)/shard_map/ppermute | solution.py:41
  153.8 7.4 %copy-start.11 = (f32[1,36,16384]{2,0,1:T(1,128)S(1)}, f32[1,36,16384]{2,0,1:T(1,128)}, u32[]{:S(2)}) copy-start(f32[1,36,16384]{2,0,1:T(1,128)} %param.14) | copy-start | bytes 7077892
  163.8 24.4 %collective-permute-start.28 = (bf16[60,8192]{1,0:T(8,128)(2,1)S(1)}, bf16[60,8192]{1,0:T(8,128)(2,1)S(1)}, u32[]{:S(2)}, u32[]{:S(2)}) collective-permute-start(bf16[60,8192]{1,0:T(8,128)(2,1)S(1)} %pad_maximum_fusion.8), channel_id=1, source_target_pairs={{8,0},{16,8},{24,16},{28,24},{20,28},{12,20},{4,12},{0,4},{9,1},{1... | collective-permute-start | bytes 2949128 | tf_op jit(solution)/shard_map/ppermute | solution.py:121
  165.6 24.5 %collective-permute-start.21 = (bf16[60,8192]{1,0:T(8,128)(2,1)S(1)}, bf16[60,8192]{1,0:T(8,128)(2,1)S(1)}, u32[]{:S(2)}, u32[]{:S(2)}) collective-permute-start(bf16[60,8192]{1,0:T(8,128)(2,1)S(1)} %pad_maximum_fusion.1), channel_id=1, source_target_pairs={{0,8},{8,16},{16,24},{24,28},{28,20},{20,12},{12,4},{4,0},{1,9},{9... | collective-permute-start | bytes 2949128 | tf_op jit(solution)/shard_map/ppermute | solution.py:120
  190.5 23.1 %collective-permute-start.29 = (bf16[60,8192]{1,0:T(8,128)(2,1)S(1)}, bf16[60,8192]{1,0:T(8,128)(2,1)S(1)}, u32[]{:S(2)}, u32[]{:S(2)}) collective-permute-start(bf16[60,8192]{1,0:T(8,128)(2,1)S(1)} %pad_maximum_fusion.9), channel_id=1, source_target_pairs={{8,0},{16,8},{24,16},{28,24},{20,28},{12,20},{4,12},{0,4},{9,1},{1... | collective-permute-start | bytes 2949128 | tf_op jit(solution)/shard_map/ppermute | solution.py:121
  192.3 22.9 %collective-permute-start.22 = (bf16[60,8192]{1,0:T(8,128)(2,1)S(1)}, bf16[60,8192]{1,0:T(8,128)(2,1)S(1)}, u32[]{:S(2)}, u32[]{:S(2)}) collective-permute-start(bf16[60,8192]{1,0:T(8,128)(2,1)S(1)} %pad_maximum_fusion.2), channel_id=1, source_target_pairs={{0,8},{8,16},{16,24},{24,28},{28,20},{20,12},{12,4},{4,0},{1,9},{9... | collective-permute-start | bytes 2949128 | tf_op jit(solution)/shard_map/ppermute | solution.py:120
  215.7 21.9 %collective-permute-start.30 = (bf16[60,8192]{1,0:T(8,128)(2,1)S(1)}, bf16[60,8192]{1,0:T(8,128)(2,1)S(1)}, u32[]{:S(2)}, u32[]{:S(2)}) collective-permute-start(bf16[60,8192]{1,0:T(8,128)(2,1)S(1)} %pad_maximum_fusion.10), channel_id=1, source_target_pairs={{8,0},{16,8},{24,16},{28,24},{20,28},{12,20},{4,12},{0,4},{9,1},{1... | collective-permute-start | bytes 2949128 | tf_op jit(solution)/shard_map/ppermute | solution.py:121
  217.5 22.4 %collective-permute-start.23 = (bf16[60,8192]{1,0:T(8,128)(2,1)S(1)}, bf16[60,8192]{1,0:T(8,128)(2,1)S(1)}, u32[]{:S(2)}, u32[]{:S(2)}) collective-permute-start(bf16[60,8192]{1,0:T(8,128)(2,1)S(1)} %pad_maximum_fusion.3), channel_id=1, source_target_pairs={{0,8},{8,16},{16,24},{24,28},{28,20},{20,12},{12,4},{4,0},{1,9},{9... | collective-permute-start | bytes 2949128 | tf_op jit(solution)/shard_map/ppermute | solution.py:120
  240.3 21.2 %collective-permute-start.31 = (bf16[60,8192]{1,0:T(8,128)(2,1)S(1)}, bf16[60,8192]{1,0:T(8,128)(2,1)S(1)}, u32[]{:S(2)}, u32[]{:S(2)}) collective-permute-start(bf16[60,8192]{1,0:T(8,128)(2,1)S(1)} %pad_maximum_fusion.11), channel_id=1, source_target_pairs={{8,0},{16,8},{24,16},{28,24},{20,28},{12,20},{4,12},{0,4},{9,1},{1... | collective-permute-start | bytes 2949128 | tf_op jit(solution)/shard_map/ppermute | solution.py:121
  241.2 21.8 %collective-permute-start.24 = (bf16[60,8192]{1,0:T(8,128)(2,1)S(1)}, bf16[60,8192]{1,0:T(8,128)(2,1)S(1)}, u32[]{:S(2)}, u32[]{:S(2)}) collective-permute-start(bf16[60,8192]{1,0:T(8,128)(2,1)S(1)} %pad_maximum_fusion.4), channel_id=1, source_target_pairs={{0,8},{8,16},{16,24},{24,28},{28,20},{20,12},{12,4},{4,0},{1,9},{9... | collective-permute-start | bytes 2949128 | tf_op jit(solution)/shard_map/ppermute | solution.py:120
  261.5 1.9 copy-start.12
  263.4 21.4 %collective-permute-start.32 = (bf16[60,8192]{1,0:T(8,128)(2,1)S(1)}, bf16[60,8192]{1,0:T(8,128)(2,1)S(1)}, u32[]{:S(2)}, u32[]{:S(2)}) collective-permute-start(bf16[60,8192]{1,0:T(8,128)(2,1)S(1)} %pad_maximum_fusion.12), channel_id=1, source_target_pairs={{8,0},{16,8},{24,16},{28,24},{20,28},{12,20},{4,12},{0,4},{9,1},{1... | collective-permute-start | bytes 2949128 | tf_op jit(solution)/shard_map/ppermute | solution.py:121
  264.4 22.3 %collective-permute-start.25 = (bf16[60,8192]{1,0:T(8,128)(2,1)S(1)}, bf16[60,8192]{1,0:T(8,128)(2,1)S(1)}, u32[]{:S(2)}, u32[]{:S(2)}) collective-permute-start(bf16[60,8192]{1,0:T(8,128)(2,1)S(1)} %pad_maximum_fusion.5), channel_id=1, source_target_pairs={{0,8},{8,16},{16,24},{24,28},{28,20},{20,12},{12,4},{4,0},{1,9},{9... | collective-permute-start | bytes 2949128 | tf_op jit(solution)/shard_map/ppermute | solution.py:120
  287.1 23.6 %collective-permute-start.33 = (bf16[60,8192]{1,0:T(8,128)(2,1)S(1)}, bf16[60,8192]{1,0:T(8,128)(2,1)S(1)}, u32[]{:S(2)}, u32[]{:S(2)}) collective-permute-start(bf16[60,8192]{1,0:T(8,128)(2,1)S(1)} %pad_maximum_fusion.13), channel_id=1, source_target_pairs={{8,0},{16,8},{24,16},{28,24},{20,28},{12,20},{4,12},{0,4},{9,1},{1... | collective-permute-start | bytes 2949128 | tf_op jit(solution)/shard_map/ppermute | solution.py:121
  287.8 22.8 %collective-permute-start.26 = (bf16[60,8192]{1,0:T(8,128)(2,1)S(1)}, bf16[60,8192]{1,0:T(8,128)(2,1)S(1)}, u32[]{:S(2)}, u32[]{:S(2)}) collective-permute-start(bf16[60,8192]{1,0:T(8,128)(2,1)S(1)} %pad_maximum_fusion.6), channel_id=1, source_target_pairs={{0,8},{8,16},{16,24},{24,28},{28,20},{20,12},{12,4},{4,0},{1,9},{9... | collective-permute-start | bytes 2949128 | tf_op jit(solution)/shard_map/ppermute | solution.py:120
  311.2 17.9 %collective-permute-start.27 = (bf16[60,8192]{1,0:T(8,128)(2,1)S(1)}, bf16[60,8192]{1,0:T(8,128)(2,1)S(1)}, u32[]{:S(2)}, u32[]{:S(2)}) collective-permute-start(bf16[60,8192]{1,0:T(8,128)(2,1)S(1)} %pad_maximum_fusion.7), channel_id=1, source_target_pairs={{0,8},{8,16},{16,24},{24,28},{28,20},{20,12},{12,4},{4,0},{1,9},{9... | collective-permute-start | bytes 2949128 | tf_op jit(solution)/shard_map/ppermute | solution.py:120
  312.6 16.5 %collective-permute-start.34 = (bf16[60,8192]{1,0:T(8,128)(2,1)S(1)}, bf16[60,8192]{1,0:T(8,128)(2,1)S(1)}, u32[]{:S(2)}, u32[]{:S(2)}) collective-permute-start(bf16[60,8192]{1,0:T(8,128)(2,1)S(1)} %pad_maximum_fusion.14), channel_id=1, source_target_pairs={{8,0},{16,8},{24,16},{28,24},{20,28},{12,20},{4,12},{0,4},{9,1},{1... | collective-permute-start | bytes 2949128 | tf_op jit(solution)/shard_map/ppermute | solution.py:121
  336.0 6.3 %copy-start.4 = (bf16[192,8192]{1,0:T(8,128)(2,1)S(1)}, bf16[192,8192]{1,0:T(8,128)(2,1)}, u32[]{:S(2)}) copy-start(bf16[192,8192]{1,0:T(8,128)(2,1)} %fusion.66) | copy-start | bytes 9437188
  336.0 6.3 %copy-start.5 = (bf16[192,8192]{1,0:T(8,128)(2,1)S(1)}, bf16[192,8192]{1,0:T(8,128)(2,1)}, u32[]{:S(2)}) copy-start(bf16[192,8192]{1,0:T(8,128)(2,1)} %fusion.70) | copy-start | bytes 9437188
  342.3 4.1 %copy-start.6 = (bf16[192,8192]{1,0:T(8,128)(2,1)S(1)}, bf16[192,8192]{1,0:T(8,128)(2,1)}, u32[]{:S(2)}) copy-start(bf16[192,8192]{1,0:T(8,128)(2,1)} %fusion.9) | copy-start | bytes 9437188
  (3 other events, 3.7 us)

commit v4 on v2

--- a/solution.py
+++ b/solution.py
@@ -82,31 +82,35 @@
             acc_b = got_b.astype(jnp.float32) + right[(2 + t) % n].astype(jnp.float32)
             if t < n - 2:
                 send_a, send_b = acc_a.astype(jnp.bfloat16), acc_b.astype(jnp.bfloat16)
-        owned = jnp.concatenate([acc_a, acc_b], axis=1)
-
-        total_sq = all_sum(all_sum(jnp.sum(owned * owned).reshape(1, 1), "dp", n), "mp", blocks)[0, 0]
+        total_sq = all_sum(all_sum((jnp.sum(acc_a * acc_a) + jnp.sum(acc_b * acc_b)).reshape(1, 1), "dp", n), "mp", blocks)[0, 0]
         clip_factor = jnp.minimum(1.0, math.sqrt(blocks * nseg * seg) / (jnp.sqrt(total_sq) + 1e-06))
         in_use = valid.astype(jnp.float32)[:, None]
-        owned_grad = clip_factor * owned
-        new_first = in_use * (0.9 * first_moment[0] + 0.1 * owned_grad)
-        new_second = in_use * (0.95 * second_moment[0] + 0.05 * owned_grad * owned_grad)
-        first_hat = new_first / (1.0 - 0.9**20)
-        second_hat = new_second / (1.0 - 0.95**20)
-        old_master = master_weights[0]
-        new_master = in_use * (
-            old_master - 0.02 * (first_hat / (jnp.sqrt(second_hat) + 1e-08) + 0.1 * old_master)
-        )
-        averaged = 0.9 * average_weights[0] + 0.1 * new_master
+
+        def update(cols, grad):
+            owned_grad = clip_factor * grad
+            new_first = in_use * (0.9 * first_moment[0][:, cols] + 0.1 * owned_grad)
+            new_second = in_use * (0.95 * second_moment[0][:, cols] + 0.05 * owned_grad * owned_grad)
+            first_hat = new_first / (1.0 - 0.9**20)
+            second_hat = new_second / (1.0 - 0.95**20)
+            old_master = master_weights[0][:, cols]
+            new_master = in_use * (
+                old_master - 0.02 * (first_hat / (jnp.sqrt(second_hat) + 1e-08) + 0.1 * old_master)
+            )
+            averaged = 0.9 * average_weights[0][:, cols] + 0.1 * new_master
+            return new_first, new_second, new_master, averaged
+
+        upd_a = update(slice(0, half), acc_a)
+        upd_b = update(slice(half, seg), acc_b)
+        new_first, new_second, new_master = (jnp.concatenate([x, y], axis=1) for x, y in zip(upd_a[:3], upd_b[:3]))
 
         rank_ahead = jnp.array(ring, jnp.int32)[(mypos + jnp.arange(n, dtype=jnp.int32)) % n]
         seg_ahead = (rank_ahead[:, None] * per_rank + jnp.arange(per_rank, dtype=jnp.int32)[None, :]).reshape(-1)
         to_rows = (jnp.arange(cap, dtype=jnp.int32)[:, None] == slot[seg_ahead][None, :]).astype(jnp.bfloat16)
-        spread_avg = jnp.dot(to_rows.T, averaged.astype(jnp.bfloat16), preferred_element_type=jnp.bfloat16)
-        spread_avg = spread_avg.reshape(n, per_rank, seg)
-        avg_l, avg_r = spread_avg[..., :half], spread_avg[..., half:]
-
-        payload = new_master.astype(jnp.bfloat16)
-        send_a, send_b = payload[:, :half], payload[:, half:]
+        avg_l, avg_r = (
+            jnp.dot(to_rows.T, u[3].astype(jnp.bfloat16), preferred_element_type=jnp.bfloat16).reshape(n, per_rank, half)
+            for u in (upd_a, upd_b)
+        )
+        send_a, send_b = upd_a[2].astype(jnp.bfloat16), upd_b[2].astype(jnp.bfloat16)
         placing_t = placing.T
 
         def spread(chunk, k):

time: 340 us -> 337 us (level)
  waiting for transfers between devices: 194 us -> 181 us
  local copies, waits for them, and re-layouts: 15.9 us -> 27.9 us
  other arithmetic: 34.2 us -> 28.5 us
    unnamed x21 -> x25, local copies, waits for them, and re-layouts: 11.5 us -> 23.6 us
    mul x1 -> x0, other arithmetic: 7.43 us -> none  [on_device(): in_use * (old_master - 0.02 * (first_hat / (jnp.sqrt(second_hat) + 1e-08)...]
    ppermute x7, waiting for transfers between devices: 53 us -> 46.2 us  [on_device(): got_a = lax.ppermute(send_a, 'dp', fwd)]
    ppermute x7, waiting for transfers between devices: 30 us -> 26.4 us  [on_device(): got_b = lax.ppermute(send_b, 'dp', bwd)]
  transfers between devices with their start and end apart: 49 -> 49, of which waited for: 38 -> 35; matrix products, arithmetic and copies ran while one was open for 16% -> 21% of each run, Pallas kernels for 0% -> 0%
where the time goes in v4:
time: 337 us; the launch traced here: 331 us
  waiting for transfers between devices  181 us (54%)
  starting transfers between devices  61.3 us (18%)
  other arithmetic  28.5 us (8%)
  local copies, waits for them, and re-layouts  27.9 us (8%)
  matrix products  25.5 us (8%)
  between operations  6.19 us (2%)
    ppermute x7, waiting for transfers between devices, on_device(): got_a = lax.ppermute(sum_a, 'dp', fwd)  50.7 us
    ppermute x7, waiting for transfers between devices, on_device(): send_a = lax.ppermute(send_a, 'dp', fwd)  48 us
    ppermute x7, waiting for transfers between devices, on_device(): got_a = lax.ppermute(send_a, 'dp', fwd)  46.2 us
    ppermute x7, waiting for transfers between devices, on_device(): got_b = lax.ppermute(send_b, 'dp', bwd)  26.4 us
    unnamed x25, local copies, waits for them, and re-layouts  23.6 us
    dot_general x16, matrix products, spread(): jnp.dot(placing_t[:, k * cap:(k + 1) * cap], chunk, preferred_element_typ...  16.4 us
    ppermute x5, starting transfers between devices, all_sum(): v = v + lax.ppermute(v, axis, [(i, i ^ k) for i in range(n)])  12.9 us
    ppermute x7, starting transfers between devices, on_device(): got_b = lax.ppermute(send_b, 'dp', bwd)  10.9 us
  transfers between devices with their start and end apart: 49, of which 35 were waited for; matrix products, arithmetic and copies ran while one was open for 21% of the time, Pallas kernels for 0%

profile of v4, /device:TPU:0, one launch (start us, length us, event | category | flops | bytes accessed | tf_op | source)
XLA Modules:
  0.0 330.9 jit_solution(7857648694320323779)
XLA Ops:
  0.6 3.1 collective-permute-start
  7.3 3.4 %fusion = bf16[288,8192]{1,0:T(8,128)(2,1)S(1)} fusion(bf16[192,16384]{1,0:T(8,128)(2,1)} %bitcast.51, s32[192]{0:T(256)S(1)} %fusion.50), kind=kOutput, calls=%fused_computation.17 | convolution fusion | flops 906024960 | bytes 7865088 | tf_op jit(solution)/shard_map/dot_general | solution.py:74
  10.9 2.0 collective-permute-start.9
  12.9 3.6 %fusion.2 = bf16[288,8192]{1,0:T(8,128)(2,1)} fusion(bf16[192,16384]{1,0:T(8,128)(2,1)S(1)} %bitcast.52, s32[192]{0:T(256)S(1)} %fusion.50), kind=kOutput, calls=%fused_computation.19 | convolution fusion | flops 906024960 | bytes 7865344 | tf_op jit(solution)/shard_map/dot_general | solution.py:73
  18.6 2.3 slice_add_fusion
  21.1 6.1 %collective-permute-done.9 = bf16[36,8192]{1,0:T(8,128)(2,1)S(1)} collective-permute-done((bf16[36,8192]{1,0:T(8,128)(2,1)S(1)}, bf16[36,8192]{1,0:T(8,128)(2,1)S(1)}, u32[]{:S(2)}, u32[]{:S(2)}) %collective-permute-start.9) | collective-permute-done | bytes 589856 | tf_op jit(solution)/shard_map/ppermute | solution.py:80
  28.4 1.7 collective-permute-start.10
  30.1 6.5 %collective-permute-done.2 = bf16[36,8192]{1,0:T(8,128)(2,1)S(1)} collective-permute-done((bf16[36,8192]{1,0:T(8,128)(2,1)S(1)}, bf16[36,8192]{1,0:T(8,128)(2,1)S(1)}, u32[]{:S(2)}, u32[]{:S(2)}) %collective-permute-start.2) | collective-permute-done | bytes 589856 | tf_op jit(solution)/shard_map/ppermute | solution.py:79
  38.3 5.4 %collective-permute-done.10 = bf16[36,8192]{1,0:T(8,128)(2,1)S(1)} collective-permute-done((bf16[36,8192]{1,0:T(8,128)(2,1)S(1)}, bf16[36,8192]{1,0:T(8,128)(2,1)S(1)}, u32[]{:S(2)}, u32[]{:S(2)}) %collective-permute-start.10) | collective-permute-done | bytes 589856 | tf_op jit(solution)/shard_map/ppermute | solution.py:80
  45.4 7.2 %collective-permute-done.3 = bf16[36,8192]{1,0:T(8,128)(2,1)S(1)} collective-permute-done((bf16[36,8192]{1,0:T(8,128)(2,1)S(1)}, bf16[36,8192]{1,0:T(8,128)(2,1)S(1)}, u32[]{:S(2)}, u32[]{:S(2)}) %collective-permute-start.3) | collective-permute-done | bytes 589856 | tf_op jit(solution)/shard_map/ppermute | solution.py:79
  54.7 4.0 %collective-permute-done.11 = bf16[36,8192]{1,0:T(8,128)(2,1)S(1)} collective-permute-done((bf16[36,8192]{1,0:T(8,128)(2,1)S(1)}, bf16[36,8192]{1,0:T(8,128)(2,1)S(1)}, u32[]{:S(2)}, u32[]{:S(2)}) %collective-permute-start.11) | collective-permute-done | bytes 589856 | tf_op jit(solution)/shard_map/ppermute | solution.py:80
  60.3 8.4 %collective-permute-done.4 = bf16[36,8192]{1,0:T(8,128)(2,1)S(1)} collective-permute-done((bf16[36,8192]{1,0:T(8,128)(2,1)S(1)}, bf16[36,8192]{1,0:T(8,128)(2,1)S(1)}, u32[]{:S(2)}, u32[]{:S(2)}) %collective-permute-start.4) | collective-permute-done | bytes 589856 | tf_op jit(solution)/shard_map/ppermute | solution.py:79
  69.6 3.9 %collective-permute-done.12 = bf16[36,8192]{1,0:T(8,128)(2,1)S(1)} collective-permute-done((bf16[36,8192]{1,0:T(8,128)(2,1)S(1)}, bf16[36,8192]{1,0:T(8,128)(2,1)S(1)}, u32[]{:S(2)}, u32[]{:S(2)}) %collective-permute-start.12) | collective-permute-done | bytes 589856 | tf_op jit(solution)/shard_map/ppermute | solution.py:80
  75.2 8.3 %collective-permute-done.5 = bf16[36,8192]{1,0:T(8,128)(2,1)S(1)} collective-permute-done((bf16[36,8192]{1,0:T(8,128)(2,1)S(1)}, bf16[36,8192]{1,0:T(8,128)(2,1)S(1)}, u32[]{:S(2)}, u32[]{:S(2)}) %collective-permute-start.5) | collective-permute-done | bytes 589856 | tf_op jit(solution)/shard_map/ppermute | solution.py:79
  84.5 4.0 %collective-permute-done.13 = bf16[36,8192]{1,0:T(8,128)(2,1)S(1)} collective-permute-done((bf16[36,8192]{1,0:T(8,128)(2,1)S(1)}, bf16[36,8192]{1,0:T(8,128)(2,1)S(1)}, u32[]{:S(2)}, u32[]{:S(2)}) %collective-permute-start.13) | collective-permute-done | bytes 589856 | tf_op jit(solution)/shard_map/ppermute | solution.py:80
  90.1 8.4 %collective-permute-done.6 = bf16[36,8192]{1,0:T(8,128)(2,1)S(1)} collective-permute-done((bf16[36,8192]{1,0:T(8,128)(2,1)S(1)}, bf16[36,8192]{1,0:T(8,128)(2,1)S(1)}, u32[]{:S(2)}, u32[]{:S(2)}) %collective-permute-start.6) | collective-permute-done | bytes 589856 | tf_op jit(solution)/shard_map/ppermute | solution.py:79
  99.4 2.9 collective-permute-done.14
  104.8 7.4 %collective-permute-done.7 = bf16[36,8192]{1,0:T(8,128)(2,1)S(1)} collective-permute-done((bf16[36,8192]{1,0:T(8,128)(2,1)S(1)}, bf16[36,8192]{1,0:T(8,128)(2,1)S(1)}, u32[]{:S(2)}, u32[]{:S(2)}) %collective-permute-start.7) | collective-permute-done | bytes 589856 | tf_op jit(solution)/shard_map/ppermute | solution.py:79
  115.9 2.9 copy.33
  118.8 2.8 copy.34
  121.7 1.6 gather_fusion.1
  123.3 4.6 %copy.31 = f32[1,36,16384]{2,1,0:T(8,128)} copy(f32[1,36,16384]{2,0,1:T(1,128)} %param.14) | data formatting | bytes 4718592
  128.0 2.0 multiply_reduce_fusion
  130.1 2.2 multiply_reduce_fusion.1
  133.6 2.7 collective-permute-start.16
  137.8 2.8 collective-permute-start.17
  142.1 3.8 %collective-permute-start.18 = (f32[1,1]{1,0:T(1,128)}, f32[1,1]{1,0:T(1,128)}, u32[]{:S(2)}, u32[]{:S(2)}) collective-permute-start(f32[1,1]{1,0:T(1,128)} %add.319), channel_id=1, source_target_pairs={{0,16},{4,20},{8,24},{12,28},{16,0},{20,4},{24,8},{28,12},{1,17},{... | collective-permute-start | bytes 20 | tf_op jit(solution)/shard_map/ppermute | solution.py:41
  149.1 2.7 collective-permute-start.20
  153.5 4.9 %fusion.60 = (bf16[36,8192]{1,0:T(8,128)(2,1)S(1)}, f32[36,8192]{1,0:T(8,128)S(1)}, f32[36,8192]{1,0:T(8,128)S(1)}, f32[36,8192]{1,0:T(8,128)S(1)}, bf16[36,8192...) fusion(f32[36,16384]{1,0:T(8,128)} %bitcast.48, ...), kind=kLoop, calls=%fused_computation.150 | loop fusion | flops 13565952 | bytes 17694868 | tf_op jit(solution)/shard_map/convert_element_type | solution.py:113
  159.5 1.5 collective-permute-start.35
  163.3 3.8 %copy.20 = f32[1,36,16384]{2,0,1:T(1,128)} copy(f32[1,36,16384]{2,1,0:T(8,128)S(1)} %get-tuple-element.32) | data formatting | bytes 4718592
  167.1 3.8 %copy.21 = f32[1,36,16384]{2,0,1:T(1,128)} copy(f32[1,36,16384]{2,1,0:T(8,128)S(1)} %get-tuple-element.33) | data formatting | bytes 4718592
  174.2 3.8 %copy.22 = f32[1,36,16384]{2,0,1:T(1,128)} copy(f32[1,36,16384]{2,1,0:T(8,128)S(1)} %maximum_bitcast_fusion.3) | data formatting | bytes 4718592
  181.4 7.3 %collective-permute-done.21 = bf16[36,8192]{1,0:T(8,128)(2,1)S(1)} collective-permute-done((bf16[36,8192]{1,0:T(8,128)(2,1)S(1)}, bf16[36,8192]{1,0:T(8,128)(2,1)S(1)}, u32[]{:S(2)}, u32[]{:S(2)}) %collective-permute-start.21) | collective-permute-done | bytes 589856 | tf_op jit(solution)/shard_map/ppermute | solution.py:124
  193.2 3.9 %collective-permute-done.36 = bf16[24,8192]{1,0:T(8,128)(2,1)S(1)} collective-permute-done((bf16[24,8192]{1,0:T(8,128)(2,1)S(1)}, bf16[24,8192]{1,0:T(8,128)(2,1)S(1)}, u32[]{:S(2)}, u32[]{:S(2)}) %collective-permute-start.36) | collective-permute-done | bytes 393248 | tf_op jit(solution)/shard_map/ppermute | solution.py:126
  200.3 10.8 %collective-permute-done.22 = bf16[36,8192]{1,0:T(8,128)(2,1)S(1)} collective-permute-done((bf16[36,8192]{1,0:T(8,128)(2,1)S(1)}, bf16[36,8192]{1,0:T(8,128)(2,1)S(1)}, u32[]{:S(2)}, u32[]{:S(2)}) %collective-permute-start.22) | collective-permute-done | bytes 589856 | tf_op jit(solution)/shard_map/ppermute | solution.py:124
  215.3 4.3 %collective-permute-done.37 = bf16[24,8192]{1,0:T(8,128)(2,1)S(1)} collective-permute-done((bf16[24,8192]{1,0:T(8,128)(2,1)S(1)}, bf16[24,8192]{1,0:T(8,128)(2,1)S(1)}, u32[]{:S(2)}, u32[]{:S(2)}) %collective-permute-start.37) | collective-permute-done | bytes 393248 | tf_op jit(solution)/shard_map/ppermute | solution.py:126
  222.8 16.9 %collective-permute-done.38 = bf16[24,8192]{1,0:T(8,128)(2,1)S(1)} collective-permute-done((bf16[24,8192]{1,0:T(8,128)(2,1)S(1)}, bf16[24,8192]{1,0:T(8,128)(2,1)S(1)}, u32[]{:S(2)}, u32[]{:S(2)}) %collective-permute-start.38) | collective-permute-done | bytes 393248 | tf_op jit(solution)/shard_map/ppermute | solution.py:126
  246.7 5.1 %collective-permute-done.39 = bf16[24,8192]{1,0:T(8,128)(2,1)S(1)} collective-permute-done((bf16[24,8192]{1,0:T(8,128)(2,1)S(1)}, bf16[24,8192]{1,0:T(8,128)(2,1)S(1)}, u32[]{:S(2)}, u32[]{:S(2)}) %collective-permute-start.39) | collective-permute-done | bytes 393248 | tf_op jit(solution)/shard_map/ppermute | solution.py:126
  254.8 11.1 %collective-permute-done.24 = bf16[36,8192]{1,0:T(8,128)(2,1)S(1)} collective-permute-done((bf16[36,8192]{1,0:T(8,128)(2,1)S(1)}, bf16[36,8192]{1,0:T(8,128)(2,1)S(1)}, u32[]{:S(2)}, u32[]{:S(2)}) %collective-permute-start.24) | collective-permute-done | bytes 589856 | tf_op jit(solution)/shard_map/ppermute | solution.py:124
  270.1 4.3 %collective-permute-done.40 = bf16[24,8192]{1,0:T(8,128)(2,1)S(1)} collective-permute-done((bf16[24,8192]{1,0:T(8,128)(2,1)S(1)}, bf16[24,8192]{1,0:T(8,128)(2,1)S(1)}, u32[]{:S(2)}, u32[]{:S(2)}) %collective-permute-start.40) | collective-permute-done | bytes 393248 | tf_op jit(solution)/shard_map/ppermute | solution.py:126
  277.3 16.3 %collective-permute-done.41 = bf16[24,8192]{1,0:T(8,128)(2,1)S(1)} collective-permute-done((bf16[24,8192]{1,0:T(8,128)(2,1)S(1)}, bf16[24,8192]{1,0:T(8,128)(2,1)S(1)}, u32[]{:S(2)}, u32[]{:S(2)}) %collective-permute-start.41) | collective-permute-done | bytes 393248 | tf_op jit(solution)/shard_map/ppermute | solution.py:126
  293.6 1.8 collective-permute-done.48
  296.7 1.6 collective-permute-start.26
  300.9 10.7 %collective-permute-done.26 = bf16[36,8192]{1,0:T(8,128)(2,1)S(1)} collective-permute-done((bf16[36,8192]{1,0:T(8,128)(2,1)S(1)}, bf16[36,8192]{1,0:T(8,128)(2,1)S(1)}, u32[]{:S(2)}, u32[]{:S(2)}) %collective-permute-start.26) | collective-permute-done | bytes 589856 | tf_op jit(solution)/shard_map/ppermute | solution.py:124
  311.6 1.6 collective-permute-start.27
  316.0 8.0 %collective-permute-done.27 = bf16[36,8192]{1,0:T(8,128)(2,1)S(1)} collective-permute-done((bf16[36,8192]{1,0:T(8,128)(2,1)S(1)}, bf16[36,8192]{1,0:T(8,128)(2,1)S(1)}, u32[]{:S(2)}, u32[]{:S(2)}) %collective-permute-start.27) | collective-permute-done | bytes 589856 | tf_op jit(solution)/shard_map/ppermute | solution.py:124
  327.4 3.3 %maximum_bitcast_fusion = bf16[1,192,16384]{2,1,0:T(8,128)(2,1)} fusion(bf16[192,8192]{1,0:T(8,128)(2,1)S(1)} %convolution_add_fusion, bf16[192,8192]{1,0:T(8,128)(2,1)S(1)} %convolution_add_fusion.7), kind=kLoop, calls=%fused_computation.16 | loop fusion | flops 12582912 | bytes 12582912 | tf_op jit(solution)/shard_map/broadcast_in_dim | solution.py:137
  (151 shorter events, 82.9 us)
Async XLA Ops:
  0.6 17.5 %collective-permute-start = (bf16[8,128]{1,0:T(8,128)(2,1)S(1)}, bf16[8,128]{1,0:T(8,128)(2,1)S(1)}, u32[]{:S(2)}, u32[]{:S(2)}) collective-permute-start(bf16[8,128]{1,0:T(8,128)(2,1)S(1)} %broadcast_in_dim.15), channel_id=1, source_target_pairs={{0,8},{8,16},{16,24},{24,28},{28,20},{20,12},{12,4},{4,0},{1,9},{9... | collective-permute-start | bytes 6152 | tf_op jit(solution)/shard_map/ppermute | solution.py:63
  3.7 14.4 %collective-permute-start.1 = (bf16[8,128]{1,0:T(8,128)(2,1)S(1)}, bf16[8,128]{1,0:T(8,128)(2,1)S(1)}, u32[]{:S(2)}, u32[]{:S(2)}) collective-permute-start(bf16[8,128]{1,0:T(8,128)(2,1)S(1)} %broadcast_in_dim.15), channel_id=1, source_target_pairs={{8,0},{16,8},{24,16},{28,24},{20,28},{12,20},{4,12},{0,4},{9,1},{1... | collective-permute-start | bytes 6152 | tf_op jit(solution)/shard_map/ppermute | solution.py:63
  10.9 16.2 %collective-permute-start.9 = (bf16[36,8192]{1,0:T(8,128)(2,1)S(1)}, bf16[36,8192]{1,0:T(8,128)(2,1)S(1)}, u32[]{:S(2)}, u32[]{:S(2)}) collective-permute-start(bf16[36,8192]{1,0:T(8,128)(2,1)S(1)} %slice.275), channel_id=1, source_target_pairs={{8,0},{16,8},{24,16},{28,24},{20,28},{12,20},{4,12},{0,4},{9,1},{1... | collective-permute-start | bytes 1769480 | tf_op jit(solution)/shard_map/ppermute | solution.py:80
  20.9 15.7 %collective-permute-start.2 = (bf16[36,8192]{1,0:T(8,128)(2,1)S(1)}, bf16[36,8192]{1,0:T(8,128)(2,1)S(1)}, u32[]{:S(2)}, u32[]{:S(2)}) collective-permute-start(bf16[36,8192]{1,0:T(8,128)(2,1)S(1)} %slice_add_fusion), channel_id=1, source_target_pairs={{0,8},{8,16},{16,24},{24,28},{28,20},{20,12},{12,4},{4,0},{1,9},{9... | collective-permute-start | bytes 1769480 | tf_op jit(solution)/shard_map/ppermute | solution.py:79
  28.4 15.3 %collective-permute-start.10 = (bf16[36,8192]{1,0:T(8,128)(2,1)S(1)}, bf16[36,8192]{1,0:T(8,128)(2,1)S(1)}, u32[]{:S(2)}, u32[]{:S(2)}) collective-permute-start(bf16[36,8192]{1,0:T(8,128)(2,1)S(1)} %add_convert_fusion.5), channel_id=1, source_target_pairs={{8,0},{16,8},{24,16},{28,24},{20,28},{12,20},{4,12},{0,4},{9,1},{1... | collective-permute-start | bytes 1769480 | tf_op jit(solution)/shard_map/ppermute | solution.py:80
  37.8 14.8 %collective-permute-start.3 = (bf16[36,8192]{1,0:T(8,128)(2,1)S(1)}, bf16[36,8192]{1,0:T(8,128)(2,1)S(1)}, u32[]{:S(2)}, u32[]{:S(2)}) collective-permute-start(bf16[36,8192]{1,0:T(8,128)(2,1)S(1)} %add_convert_fusion.11), channel_id=1, source_target_pairs={{0,8},{8,16},{16,24},{24,28},{28,20},{20,12},{12,4},{4,0},{1,9},{9... | collective-permute-start | bytes 1769480 | tf_op jit(solution)/shard_map/ppermute | solution.py:79
  44.0 14.7 %collective-permute-start.11 = (bf16[36,8192]{1,0:T(8,128)(2,1)S(1)}, bf16[36,8192]{1,0:T(8,128)(2,1)S(1)}, u32[]{:S(2)}, u32[]{:S(2)}) collective-permute-start(bf16[36,8192]{1,0:T(8,128)(2,1)S(1)} %add_convert_fusion.4), channel_id=1, source_target_pairs={{8,0},{16,8},{24,16},{28,24},{20,28},{12,20},{4,12},{0,4},{9,1},{1... | collective-permute-start | bytes 1769480 | tf_op jit(solution)/shard_map/ppermute | solution.py:80
  54.0 14.7 %collective-permute-start.4 = (bf16[36,8192]{1,0:T(8,128)(2,1)S(1)}, bf16[36,8192]{1,0:T(8,128)(2,1)S(1)}, u32[]{:S(2)}, u32[]{:S(2)}) collective-permute-start(bf16[36,8192]{1,0:T(8,128)(2,1)S(1)} %add_convert_fusion.10), channel_id=1, source_target_pairs={{0,8},{8,16},{16,24},{24,28},{28,20},{20,12},{12,4},{4,0},{1,9},{9... | collective-permute-start | bytes 1769480 | tf_op jit(solution)/shard_map/ppermute | solution.py:79
  58.8 14.7 %collective-permute-start.12 = (bf16[36,8192]{1,0:T(8,128)(2,1)S(1)}, bf16[36,8192]{1,0:T(8,128)(2,1)S(1)}, u32[]{:S(2)}, u32[]{:S(2)}) collective-permute-start(bf16[36,8192]{1,0:T(8,128)(2,1)S(1)} %add_convert_fusion.3), channel_id=1, source_target_pairs={{8,0},{16,8},{24,16},{28,24},{20,28},{12,20},{4,12},{0,4},{9,1},{1... | collective-permute-start | bytes 1769480 | tf_op jit(solution)/shard_map/ppermute | solution.py:80
  68.9 14.6 %collective-permute-start.5 = (bf16[36,8192]{1,0:T(8,128)(2,1)S(1)}, bf16[36,8192]{1,0:T(8,128)(2,1)S(1)}, u32[]{:S(2)}, u32[]{:S(2)}) collective-permute-start(bf16[36,8192]{1,0:T(8,128)(2,1)S(1)} %add_convert_fusion.9), channel_id=1, source_target_pairs={{0,8},{8,16},{16,24},{24,28},{28,20},{20,12},{12,4},{4,0},{1,9},{9... | collective-permute-start | bytes 1769480 | tf_op jit(solution)/shard_map/ppermute | solution.py:79
  73.8 14.7 %collective-permute-start.13 = (bf16[36,8192]{1,0:T(8,128)(2,1)S(1)}, bf16[36,8192]{1,0:T(8,128)(2,1)S(1)}, u32[]{:S(2)}, u32[]{:S(2)}) collective-permute-start(bf16[36,8192]{1,0:T(8,128)(2,1)S(1)} %add_convert_fusion.2), channel_id=1, source_target_pairs={{8,0},{16,8},{24,16},{28,24},{20,28},{12,20},{4,12},{0,4},{9,1},{1... | collective-permute-start | bytes 1769480 | tf_op jit(solution)/shard_map/ppermute | solution.py:80
  83.8 14.7 %collective-permute-start.6 = (bf16[36,8192]{1,0:T(8,128)(2,1)S(1)}, bf16[36,8192]{1,0:T(8,128)(2,1)S(1)}, u32[]{:S(2)}, u32[]{:S(2)}) collective-permute-start(bf16[36,8192]{1,0:T(8,128)(2,1)S(1)} %add_convert_fusion.8), channel_id=1, source_target_pairs={{0,8},{8,16},{16,24},{24,28},{28,20},{20,12},{12,4},{4,0},{1,9},{9... | collective-permute-start | bytes 1769480 | tf_op jit(solution)/shard_map/ppermute | solution.py:79
  88.7 13.7 %collective-permute-start.14 = (bf16[36,8192]{1,0:T(8,128)(2,1)S(1)}, bf16[36,8192]{1,0:T(8,128)(2,1)S(1)}, u32[]{:S(2)}, u32[]{:S(2)}) collective-permute-start(bf16[36,8192]{1,0:T(8,128)(2,1)S(1)} %add_convert_fusion.1), channel_id=1, source_target_pairs={{8,0},{16,8},{24,16},{28,24},{20,28},{12,20},{4,12},{0,4},{9,1},{1... | collective-permute-start | bytes 1769480 | tf_op jit(solution)/shard_map/ppermute | solution.py:80
  98.7 13.5 %collective-permute-start.7 = (bf16[36,8192]{1,0:T(8,128)(2,1)S(1)}, bf16[36,8192]{1,0:T(8,128)(2,1)S(1)}, u32[]{:S(2)}, u32[]{:S(2)}) collective-permute-start(bf16[36,8192]{1,0:T(8,128)(2,1)S(1)} %add_convert_fusion.7), channel_id=1, source_target_pairs={{0,8},{8,16},{16,24},{24,28},{28,20},{20,12},{12,4},{4,0},{1,9},{9... | collective-permute-start | bytes 1769480 | tf_op jit(solution)/shard_map/ppermute | solution.py:79
  103.4 24.6 %collective-permute-start.15 = (bf16[36,8192]{1,0:T(8,128)(2,1)}, bf16[36,8192]{1,0:T(8,128)(2,1)S(1)}, u32[]{:S(2)}, u32[]{:S(2)}) collective-permute-start(bf16[36,8192]{1,0:T(8,128)(2,1)} %add_convert_fusion), channel_id=1, source_target_pairs={{8,0},{16,8},{24,16},{28,24},{20,28},{12,20},{4,12},{0,4},{9,1},{1... | collective-permute-start | bytes 1769480 | tf_op jit(solution)/shard_map/ppermute | solution.py:80
  113.3 16.8 %collective-permute-start.8 = (bf16[36,8192]{1,0:T(8,128)(2,1)}, bf16[36,8192]{1,0:T(8,128)(2,1)}, u32[]{:S(2)}, u32[]{:S(2)}) collective-permute-start(bf16[36,8192]{1,0:T(8,128)(2,1)} %add_convert_fusion.6), channel_id=1, source_target_pairs={{0,8},{8,16},{16,24},{24,28},{28,20},{20,12},{12,4},{4,0},{1,9},{9... | collective-permute-start | bytes 1769480 | tf_op jit(solution)/shard_map/ppermute | solution.py:79
  133.6 3.6 %collective-permute-start.16 = (f32[1,1]{1,0:T(1,128)}, f32[1,1]{1,0:T(1,128)}, u32[]{:S(2)}, u32[]{:S(2)}) collective-permute-start(f32[1,1]{1,0:T(1,128)} %bitcast.3), channel_id=1, source_target_pairs={{0,4},{4,0},{8,12},{12,8},{16,20},{20,16},{24,28},{28,24},{1,5},{5... | collective-permute-start | bytes 20 | tf_op jit(solution)/shard_map/ppermute | solution.py:41
  137.8 3.6 %collective-permute-start.17 = (f32[1,1]{1,0:T(1,128)}, f32[1,1]{1,0:T(1,128)}, u32[]{:S(2)}, u32[]{:S(2)}) collective-permute-start(f32[1,1]{1,0:T(1,128)} %add.318), channel_id=1, source_target_pairs={{0,8},{4,12},{8,0},{12,4},{16,24},{20,28},{24,16},{28,20},{1,9},{5... | collective-permute-start | bytes 20 | tf_op jit(solution)/shard_map/ppermute | solution.py:41
  142.1 4.5 %collective-permute-start.18 = (f32[1,1]{1,0:T(1,128)}, f32[1,1]{1,0:T(1,128)}, u32[]{:S(2)}, u32[]{:S(2)}) collective-permute-start(f32[1,1]{1,0:T(1,128)} %add.319), channel_id=1, source_target_pairs={{0,16},{4,20},{8,24},{12,28},{16,0},{20,4},{24,8},{28,12},{1,17},{... | collective-permute-start | bytes 20 | tf_op jit(solution)/shard_map/ppermute | solution.py:41
  149.1 3.6 %collective-permute-start.20 = (f32[1,1]{1,0:T(1,128)}, f32[1,1]{1,0:T(1,128)}, u32[]{:S(2)}, u32[]{:S(2)}) collective-permute-start(f32[1,1]{1,0:T(1,128)} %add.321), channel_id=1, source_target_pairs={{0,2},{1,3},{2,0},{3,1},{4,6},{5,7},{6,4},{7,5},{8,10},{9,11},{10,... | collective-permute-start | bytes 20 | tf_op jit(solution)/shard_map/ppermute | solution.py:41
  159.5 19.5 %collective-permute-start.35 = (bf16[24,8192]{1,0:T(8,128)(2,1)S(1)}, bf16[24,8192]{1,0:T(8,128)(2,1)S(1)}, u32[]{:S(2)}, u32[]{:S(2)}) collective-permute-start(bf16[24,8192]{1,0:T(8,128)(2,1)S(1)} %slice.295), channel_id=1, source_target_pairs={{0,8},{8,16},{16,24},{24,28},{28,20},{20,12},{12,4},{4,0},{1,9},{9... | collective-permute-start | bytes 1179656 | tf_op jit(solution)/shard_map/ppermute | solution.py:126
  162.0 18.6 %collective-permute-start.42 = (bf16[24,8192]{1,0:T(8,128)(2,1)S(1)}, bf16[24,8192]{1,0:T(8,128)(2,1)S(1)}, u32[]{:S(2)}, u32[]{:S(2)}) collective-permute-start(bf16[24,8192]{1,0:T(8,128)(2,1)S(1)} %slice.304), channel_id=1, source_target_pairs={{8,0},{16,8},{24,16},{28,24},{20,28},{12,20},{4,12},{0,4},{9,1},{1... | collective-permute-start | bytes 1179656 | tf_op jit(solution)/shard_map/ppermute | solution.py:127
  171.0 17.7 %collective-permute-start.21 = (bf16[36,8192]{1,0:T(8,128)(2,1)S(1)}, bf16[36,8192]{1,0:T(8,128)(2,1)S(1)}, u32[]{:S(2)}, u32[]{:S(2)}) collective-permute-start(bf16[36,8192]{1,0:T(8,128)(2,1)S(1)} %get-tuple-element.20), channel_id=1, source_target_pairs={{0,8},{8,16},{16,24},{24,28},{28,20},{20,12},{12,4},{4,0},{1,9},{9... | collective-permute-start | bytes 1769480 | tf_op jit(solution)/shard_map/ppermute | solution.py:124
  173.4 17.7 %collective-permute-start.28 = (bf16[36,8192]{1,0:T(8,128)(2,1)S(1)}, bf16[36,8192]{1,0:T(8,128)(2,1)S(1)}, u32[]{:S(2)}, u32[]{:S(2)}) collective-permute-start(bf16[36,8192]{1,0:T(8,128)(2,1)S(1)} %get-tuple-element.28), channel_id=1, source_target_pairs={{8,0},{16,8},{24,16},{28,24},{20,28},{12,20},{4,12},{0,4},{9,1},{1... | collective-permute-start | bytes 1769480 | tf_op jit(solution)/shard_map/ppermute | solution.py:125
  179.1 17.9 %collective-permute-start.36 = (bf16[24,8192]{1,0:T(8,128)(2,1)S(1)}, bf16[24,8192]{1,0:T(8,128)(2,1)S(1)}, u32[]{:S(2)}, u32[]{:S(2)}) collective-permute-start(bf16[24,8192]{1,0:T(8,128)(2,1)S(1)} %add_convert_fusion.23), channel_id=1, source_target_pairs={{0,8},{8,16},{16,24},{24,28},{28,20},{20,12},{12,4},{4,0},{1,9},{9... | collective-permute-start | bytes 1179656 | tf_op jit(solution)/shard_map/ppermute | solution.py:126
  180.7 18.8 %collective-permute-start.43 = (bf16[24,8192]{1,0:T(8,128)(2,1)S(1)}, bf16[24,8192]{1,0:T(8,128)(2,1)S(1)}, u32[]{:S(2)}, u32[]{:S(2)}) collective-permute-start(bf16[24,8192]{1,0:T(8,128)(2,1)S(1)} %add_convert_fusion.17), channel_id=1, source_target_pairs={{8,0},{16,8},{24,16},{28,24},{20,28},{12,20},{4,12},{0,4},{9,1},{1... | collective-permute-start | bytes 1179656 | tf_op jit(solution)/shard_map/ppermute | solution.py:127
  188.6 22.5 %collective-permute-start.22 = (bf16[36,8192]{1,0:T(8,128)(2,1)S(1)}, bf16[36,8192]{1,0:T(8,128)(2,1)S(1)}, u32[]{:S(2)}, u32[]{:S(2)}) collective-permute-start(bf16[36,8192]{1,0:T(8,128)(2,1)S(1)} %collective-permute-done.21), channel_id=1, source_target_pairs={{0,8},{8,16},{16,24},{24,28},{28,20},{20,12},{12,4},{4,0},{1,9},{9... | collective-permute-start | bytes 1769480 | tf_op jit(solution)/shard_map/ppermute | solution.py:124
  191.1 22.5 %collective-permute-start.29 = (bf16[36,8192]{1,0:T(8,128)(2,1)S(1)}, bf16[36,8192]{1,0:T(8,128)(2,1)S(1)}, u32[]{:S(2)}, u32[]{:S(2)}) collective-permute-start(bf16[36,8192]{1,0:T(8,128)(2,1)S(1)} %collective-permute-done.28), channel_id=1, source_target_pairs={{8,0},{16,8},{24,16},{28,24},{20,28},{12,20},{4,12},{0,4},{9,1},{1... | collective-permute-start | bytes 1769480 | tf_op jit(solution)/shard_map/ppermute | solution.py:125
  197.2 22.4 %collective-permute-start.37 = (bf16[24,8192]{1,0:T(8,128)(2,1)S(1)}, bf16[24,8192]{1,0:T(8,128)(2,1)S(1)}, u32[]{:S(2)}, u32[]{:S(2)}) collective-permute-start(bf16[24,8192]{1,0:T(8,128)(2,1)S(1)} %add_convert_fusion.22), channel_id=1, source_target_pairs={{0,8},{8,16},{16,24},{24,28},{28,20},{20,12},{12,4},{4,0},{1,9},{9... | collective-permute-start | bytes 1179656 | tf_op jit(solution)/shard_map/ppermute | solution.py:126
  199.6 22.4 %collective-permute-start.44 = (bf16[24,8192]{1,0:T(8,128)(2,1)S(1)}, bf16[24,8192]{1,0:T(8,128)(2,1)S(1)}, u32[]{:S(2)}, u32[]{:S(2)}) collective-permute-start(bf16[24,8192]{1,0:T(8,128)(2,1)S(1)} %add_convert_fusion.16), channel_id=1, source_target_pairs={{8,0},{16,8},{24,16},{28,24},{20,28},{12,20},{4,12},{0,4},{9,1},{1... | collective-permute-start | bytes 1179656 | tf_op jit(solution)/shard_map/ppermute | solution.py:127
  211.1 31.5 %collective-permute-start.23 = (bf16[36,8192]{1,0:T(8,128)(2,1)S(1)}, bf16[36,8192]{1,0:T(8,128)(2,1)S(1)}, u32[]{:S(2)}, u32[]{:S(2)}) collective-permute-start(bf16[36,8192]{1,0:T(8,128)(2,1)S(1)} %collective-permute-done.22), channel_id=1, source_target_pairs={{0,8},{8,16},{16,24},{24,28},{28,20},{20,12},{12,4},{4,0},{1,9},{9... | collective-permute-start | bytes 1769480 | tf_op jit(solution)/shard_map/ppermute | solution.py:124
  213.6 31.5 %collective-permute-start.30 = (bf16[36,8192]{1,0:T(8,128)(2,1)S(1)}, bf16[36,8192]{1,0:T(8,128)(2,1)S(1)}, u32[]{:S(2)}, u32[]{:S(2)}) collective-permute-start(bf16[36,8192]{1,0:T(8,128)(2,1)S(1)} %collective-permute-done.29), channel_id=1, source_target_pairs={{8,0},{16,8},{24,16},{28,24},{20,28},{12,20},{4,12},{0,4},{9,1},{1... | collective-permute-start | bytes 1769480 | tf_op jit(solution)/shard_map/ppermute | solution.py:125
  219.6 20.0 %collective-permute-start.38 = (bf16[24,8192]{1,0:T(8,128)(2,1)S(1)}, bf16[24,8192]{1,0:T(8,128)(2,1)S(1)}, u32[]{:S(2)}, u32[]{:S(2)}) collective-permute-start(bf16[24,8192]{1,0:T(8,128)(2,1)S(1)} %add_convert_fusion.21), channel_id=1, source_target_pairs={{0,8},{8,16},{16,24},{24,28},{28,20},{20,12},{12,4},{4,0},{1,9},{9... | collective-permute-start | bytes 1179656 | tf_op jit(solution)/shard_map/ppermute | solution.py:126
  222.1 19.7 %collective-permute-start.45 = (bf16[24,8192]{1,0:T(8,128)(2,1)S(1)}, bf16[24,8192]{1,0:T(8,128)(2,1)S(1)}, u32[]{:S(2)}, u32[]{:S(2)}) collective-permute-start(bf16[24,8192]{1,0:T(8,128)(2,1)S(1)} %add_convert_fusion.15), channel_id=1, source_target_pairs={{8,0},{16,8},{24,16},{28,24},{20,28},{12,20},{4,12},{0,4},{9,1},{1... | collective-permute-start | bytes 1179656 | tf_op jit(solution)/shard_map/ppermute | solution.py:127
  239.8 12.1 %collective-permute-start.39 = (bf16[24,8192]{1,0:T(8,128)(2,1)S(1)}, bf16[24,8192]{1,0:T(8,128)(2,1)S(1)}, u32[]{:S(2)}, u32[]{:S(2)}) collective-permute-start(bf16[24,8192]{1,0:T(8,128)(2,1)S(1)} %add_convert_fusion.20), channel_id=1, source_target_pairs={{0,8},{8,16},{16,24},{24,28},{28,20},{20,12},{12,4},{4,0},{1,9},{9... | collective-permute-start | bytes 1179656 | tf_op jit(solution)/shard_map/ppermute | solution.py:126
  241.9 12.1 %collective-permute-start.46 = (bf16[24,8192]{1,0:T(8,128)(2,1)S(1)}, bf16[24,8192]{1,0:T(8,128)(2,1)S(1)}, u32[]{:S(2)}, u32[]{:S(2)}) collective-permute-start(bf16[24,8192]{1,0:T(8,128)(2,1)S(1)} %add_convert_fusion.14), channel_id=1, source_target_pairs={{8,0},{16,8},{24,16},{28,24},{20,28},{12,20},{4,12},{0,4},{9,1},{1... | collective-permute-start | bytes 1179656 | tf_op jit(solution)/shard_map/ppermute | solution.py:127
  242.6 23.3 %collective-permute-start.24 = (bf16[36,8192]{1,0:T(8,128)(2,1)S(1)}, bf16[36,8192]{1,0:T(8,128)(2,1)S(1)}, u32[]{:S(2)}, u32[]{:S(2)}) collective-permute-start(bf16[36,8192]{1,0:T(8,128)(2,1)S(1)} %collective-permute-done.23), channel_id=1, source_target_pairs={{0,8},{8,16},{16,24},{24,28},{28,20},{20,12},{12,4},{4,0},{1,9},{9... | collective-permute-start | bytes 1769480 | tf_op jit(solution)/shard_map/ppermute | solution.py:124
  245.0 23.3 %collective-permute-start.31 = (bf16[36,8192]{1,0:T(8,128)(2,1)S(1)}, bf16[36,8192]{1,0:T(8,128)(2,1)S(1)}, u32[]{:S(2)}, u32[]{:S(2)}) collective-permute-start(bf16[36,8192]{1,0:T(8,128)(2,1)S(1)} %collective-permute-done.30), channel_id=1, source_target_pairs={{8,0},{16,8},{24,16},{28,24},{20,28},{12,20},{4,12},{0,4},{9,1},{1... | collective-permute-start | bytes 1769480 | tf_op jit(solution)/shard_map/ppermute | solution.py:125
  252.0 22.4 %collective-permute-start.40 = (bf16[24,8192]{1,0:T(8,128)(2,1)S(1)}, bf16[24,8192]{1,0:T(8,128)(2,1)S(1)}, u32[]{:S(2)}, u32[]{:S(2)}) collective-permute-start(bf16[24,8192]{1,0:T(8,128)(2,1)S(1)} %add_convert_fusion.19), channel_id=1, source_target_pairs={{0,8},{8,16},{16,24},{24,28},{28,20},{20,12},{12,4},{4,0},{1,9},{9... | collective-permute-start | bytes 1179656 | tf_op jit(solution)/shard_map/ppermute | solution.py:126
  254.1 22.4 %collective-permute-start.47 = (bf16[24,8192]{1,0:T(8,128)(2,1)S(1)}, bf16[24,8192]{1,0:T(8,128)(2,1)S(1)}, u32[]{:S(2)}, u32[]{:S(2)}) collective-permute-start(bf16[24,8192]{1,0:T(8,128)(2,1)S(1)} %add_convert_fusion.13), channel_id=1, source_target_pairs={{8,0},{16,8},{24,16},{28,24},{20,28},{12,20},{4,12},{0,4},{9,1},{1... | collective-permute-start | bytes 1179656 | tf_op jit(solution)/shard_map/ppermute | solution.py:127
  265.9 30.8 %collective-permute-start.25 = (bf16[36,8192]{1,0:T(8,128)(2,1)S(1)}, bf16[36,8192]{1,0:T(8,128)(2,1)S(1)}, u32[]{:S(2)}, u32[]{:S(2)}) collective-permute-start(bf16[36,8192]{1,0:T(8,128)(2,1)S(1)} %collective-permute-done.24), channel_id=1, source_target_pairs={{0,8},{8,16},{16,24},{24,28},{28,20},{20,12},{12,4},{4,0},{1,9},{9... | collective-permute-start | bytes 1769480 | tf_op jit(solution)/shard_map/ppermute | solution.py:124
  268.4 31.0 %collective-permute-start.32 = (bf16[36,8192]{1,0:T(8,128)(2,1)S(1)}, bf16[36,8192]{1,0:T(8,128)(2,1)S(1)}, u32[]{:S(2)}, u32[]{:S(2)}) collective-permute-start(bf16[36,8192]{1,0:T(8,128)(2,1)S(1)} %collective-permute-done.31), channel_id=1, source_target_pairs={{8,0},{16,8},{24,16},{28,24},{20,28},{12,20},{4,12},{0,4},{9,1},{1... | collective-permute-start | bytes 1769480 | tf_op jit(solution)/shard_map/ppermute | solution.py:125
  274.4 19.1 %collective-permute-start.41 = (bf16[24,8192]{1,0:T(8,128)(2,1)S(1)}, bf16[24,8192]{1,0:T(8,128)(2,1)S(1)}, u32[]{:S(2)}, u32[]{:S(2)}) collective-permute-start(bf16[24,8192]{1,0:T(8,128)(2,1)S(1)} %add_convert_fusion.18), channel_id=1, source_target_pairs={{0,8},{8,16},{16,24},{24,28},{28,20},{20,12},{12,4},{4,0},{1,9},{9... | collective-permute-start | bytes 1179656 | tf_op jit(solution)/shard_map/ppermute | solution.py:126
  276.6 18.8 %collective-permute-start.48 = (bf16[24,8192]{1,0:T(8,128)(2,1)S(1)}, bf16[24,8192]{1,0:T(8,128)(2,1)S(1)}, u32[]{:S(2)}, u32[]{:S(2)}) collective-permute-start(bf16[24,8192]{1,0:T(8,128)(2,1)S(1)} %add_convert_fusion.12), channel_id=1, source_target_pairs={{8,0},{16,8},{24,16},{28,24},{20,28},{12,20},{4,12},{0,4},{9,1},{1... | collective-permute-start | bytes 1179656 | tf_op jit(solution)/shard_map/ppermute | solution.py:127
  296.7 14.9 %collective-permute-start.26 = (bf16[36,8192]{1,0:T(8,128)(2,1)S(1)}, bf16[36,8192]{1,0:T(8,128)(2,1)S(1)}, u32[]{:S(2)}, u32[]{:S(2)}) collective-permute-start(bf16[36,8192]{1,0:T(8,128)(2,1)S(1)} %collective-permute-done.25), channel_id=1, source_target_pairs={{0,8},{8,16},{16,24},{24,28},{28,20},{20,12},{12,4},{4,0},{1,9},{9... | collective-permute-start | bytes 1769480 | tf_op jit(solution)/shard_map/ppermute | solution.py:124
  299.4 14.9 %collective-permute-start.33 = (bf16[36,8192]{1,0:T(8,128)(2,1)S(1)}, bf16[36,8192]{1,0:T(8,128)(2,1)S(1)}, u32[]{:S(2)}, u32[]{:S(2)}) collective-permute-start(bf16[36,8192]{1,0:T(8,128)(2,1)S(1)} %collective-permute-done.32), channel_id=1, source_target_pairs={{8,0},{16,8},{24,16},{28,24},{20,28},{12,20},{4,12},{0,4},{9,1},{1... | collective-permute-start | bytes 1769480 | tf_op jit(solution)/shard_map/ppermute | solution.py:125
  311.6 12.3 %collective-permute-start.27 = (bf16[36,8192]{1,0:T(8,128)(2,1)S(1)}, bf16[36,8192]{1,0:T(8,128)(2,1)S(1)}, u32[]{:S(2)}, u32[]{:S(2)}) collective-permute-start(bf16[36,8192]{1,0:T(8,128)(2,1)S(1)} %collective-permute-done.26), channel_id=1, source_target_pairs={{0,8},{8,16},{16,24},{24,28},{28,20},{20,12},{12,4},{4,0},{1,9},{9... | collective-permute-start | bytes 1769480 | tf_op jit(solution)/shard_map/ppermute | solution.py:124
  314.3 12.1 %collective-permute-start.34 = (bf16[36,8192]{1,0:T(8,128)(2,1)S(1)}, bf16[36,8192]{1,0:T(8,128)(2,1)S(1)}, u32[]{:S(2)}, u32[]{:S(2)}) collective-permute-start(bf16[36,8192]{1,0:T(8,128)(2,1)S(1)} %collective-permute-done.33), channel_id=1, source_target_pairs={{8,0},{16,8},{24,16},{28,24},{20,28},{12,20},{4,12},{0,4},{9,1},{1... | collective-permute-start | bytes 1769480 | tf_op jit(solution)/shard_map/ppermute | solution.py:125
  (10 other events, 94.2 us)

commit v5 on v4

--- a/solution.py
+++ b/solution.py
@@ -125,6 +125,10 @@
             send_b = lax.ppermute(send_b, "dp", bwd)
             got_a = lax.ppermute(sum_a, "dp", fwd)
             got_b = lax.ppermute(sum_b, "dp", bwd)
+            if t == 0:
+                new_master, new_first, new_second, send_a, send_b = lax.optimization_barrier(
+                    (new_master, new_first, new_second, send_a, send_b)
+                )
             out_a = out_a + spread(send_a, n - 1 - t)
             out_b = out_b + spread(send_b, 1 + t)
             fin_a = got_a.astype(jnp.float32) + avg_l[(2 * n - 2 - t) % n].astype(jnp.float32)

time: 337 us -> 336 us (level)
    ppermute x7, waiting for transfers between devices: 48 us -> 42.8 us  [on_device(): send_a = lax.ppermute(send_a, 'dp', fwd)]
  transfers between devices with their start and end apart: 49 -> 49, of which waited for: 35 -> 37; matrix products, arithmetic and copies ran while one was open for 21% -> 21% of each run, Pallas kernels for 0% -> 0%
where the time goes in v5:
time: 336 us; the launch traced here: 330 us
  waiting for transfers between devices  180 us (54%)
  starting transfers between devices  61.1 us (18%)
  other arithmetic  28.5 us (8%)
  local copies, waits for them, and re-layouts  27.9 us (8%)
  matrix products  25.5 us (8%)
  between operations  6.17 us (2%)
    ppermute x7, waiting for transfers between devices, on_device(): got_a = lax.ppermute(sum_a, 'dp', fwd)  51.8 us
    ppermute x7, waiting for transfers between devices, on_device(): got_a = lax.ppermute(send_a, 'dp', fwd)  46.1 us
    ppermute x7, waiting for transfers between devices, on_device(): send_a = lax.ppermute(send_a, 'dp', fwd)  42.8 us
    ppermute x7, waiting for transfers between devices, on_device(): got_b = lax.ppermute(send_b, 'dp', bwd)  26.4 us
    unnamed x25, local copies, waits for them, and re-layouts  23.6 us
    dot_general x16, matrix products, spread(): jnp.dot(placing_t[:, k * cap:(k + 1) * cap], chunk, preferred_element_typ...  16.4 us
    ppermute x5, starting transfers between devices, all_sum(): v = v + lax.ppermute(v, axis, [(i, i ^ k) for i in range(n)])  12.8 us
    ppermute x7, starting transfers between devices, on_device(): got_b = lax.ppermute(send_b, 'dp', bwd)  10.8 us
  transfers between devices with their start and end apart: 49, of which 37 were waited for; matrix products, arithmetic and copies ran while one was open for 21% of the time, Pallas kernels for 0%

profile of v5, /device:TPU:0, one launch (start us, length us, event | category | flops | bytes accessed | tf_op | source)
XLA Modules:
  0.0 329.7 jit_solution(4260912667597998397)
XLA Ops:
  0.6 3.1 collective-permute-start
  7.3 3.4 %fusion = bf16[288,8192]{1,0:T(8,128)(2,1)S(1)} fusion(bf16[192,16384]{1,0:T(8,128)(2,1)} %bitcast.51, s32[192]{0:T(256)S(1)} %fusion.50), kind=kOutput, calls=%fused_computation.17 | convolution fusion | flops 906024960 | bytes 7865088 | tf_op jit(solution)/shard_map/dot_general | solution.py:74
  10.9 2.0 collective-permute-start.9
  12.9 3.6 %fusion.2 = bf16[288,8192]{1,0:T(8,128)(2,1)} fusion(bf16[192,16384]{1,0:T(8,128)(2,1)S(1)} %bitcast.52, s32[192]{0:T(256)S(1)} %fusion.50), kind=kOutput, calls=%fused_computation.19 | convolution fusion | flops 906024960 | bytes 7865344 | tf_op jit(solution)/shard_map/dot_general | solution.py:73
  18.6 2.3 slice_add_fusion
  21.0 6.1 %collective-permute-done.9 = bf16[36,8192]{1,0:T(8,128)(2,1)S(1)} collective-permute-done((bf16[36,8192]{1,0:T(8,128)(2,1)S(1)}, bf16[36,8192]{1,0:T(8,128)(2,1)S(1)}, u32[]{:S(2)}, u32[]{:S(2)}) %collective-permute-start.9) | collective-permute-done | bytes 589856 | tf_op jit(solution)/shard_map/ppermute | solution.py:80
  28.4 1.7 collective-permute-start.10
  30.1 6.5 %collective-permute-done.2 = bf16[36,8192]{1,0:T(8,128)(2,1)S(1)} collective-permute-done((bf16[36,8192]{1,0:T(8,128)(2,1)S(1)}, bf16[36,8192]{1,0:T(8,128)(2,1)S(1)}, u32[]{:S(2)}, u32[]{:S(2)}) %collective-permute-start.2) | collective-permute-done | bytes 589856 | tf_op jit(solution)/shard_map/ppermute | solution.py:79
  38.3 5.4 %collective-permute-done.10 = bf16[36,8192]{1,0:T(8,128)(2,1)S(1)} collective-permute-done((bf16[36,8192]{1,0:T(8,128)(2,1)S(1)}, bf16[36,8192]{1,0:T(8,128)(2,1)S(1)}, u32[]{:S(2)}, u32[]{:S(2)}) %collective-permute-start.10) | collective-permute-done | bytes 589856 | tf_op jit(solution)/shard_map/ppermute | solution.py:80
  45.4 7.2 %collective-permute-done.3 = bf16[36,8192]{1,0:T(8,128)(2,1)S(1)} collective-permute-done((bf16[36,8192]{1,0:T(8,128)(2,1)S(1)}, bf16[36,8192]{1,0:T(8,128)(2,1)S(1)}, u32[]{:S(2)}, u32[]{:S(2)}) %collective-permute-start.3) | collective-permute-done | bytes 589856 | tf_op jit(solution)/shard_map/ppermute | solution.py:79
  54.7 4.0 %collective-permute-done.11 = bf16[36,8192]{1,0:T(8,128)(2,1)S(1)} collective-permute-done((bf16[36,8192]{1,0:T(8,128)(2,1)S(1)}, bf16[36,8192]{1,0:T(8,128)(2,1)S(1)}, u32[]{:S(2)}, u32[]{:S(2)}) %collective-permute-start.11) | collective-permute-done | bytes 589856 | tf_op jit(solution)/shard_map/ppermute | solution.py:80
  60.3 8.4 %collective-permute-done.4 = bf16[36,8192]{1,0:T(8,128)(2,1)S(1)} collective-permute-done((bf16[36,8192]{1,0:T(8,128)(2,1)S(1)}, bf16[36,8192]{1,0:T(8,128)(2,1)S(1)}, u32[]{:S(2)}, u32[]{:S(2)}) %collective-permute-start.4) | collective-permute-done | bytes 589856 | tf_op jit(solution)/shard_map/ppermute | solution.py:79
  69.6 3.9 %collective-permute-done.12 = bf16[36,8192]{1,0:T(8,128)(2,1)S(1)} collective-permute-done((bf16[36,8192]{1,0:T(8,128)(2,1)S(1)}, bf16[36,8192]{1,0:T(8,128)(2,1)S(1)}, u32[]{:S(2)}, u32[]{:S(2)}) %collective-permute-start.12) | collective-permute-done | bytes 589856 | tf_op jit(solution)/shard_map/ppermute | solution.py:80
  75.2 8.3 %collective-permute-done.5 = bf16[36,8192]{1,0:T(8,128)(2,1)S(1)} collective-permute-done((bf16[36,8192]{1,0:T(8,128)(2,1)S(1)}, bf16[36,8192]{1,0:T(8,128)(2,1)S(1)}, u32[]{:S(2)}, u32[]{:S(2)}) %collective-permute-start.5) | collective-permute-done | bytes 589856 | tf_op jit(solution)/shard_map/ppermute | solution.py:79
  84.5 4.0 %collective-permute-done.13 = bf16[36,8192]{1,0:T(8,128)(2,1)S(1)} collective-permute-done((bf16[36,8192]{1,0:T(8,128)(2,1)S(1)}, bf16[36,8192]{1,0:T(8,128)(2,1)S(1)}, u32[]{:S(2)}, u32[]{:S(2)}) %collective-permute-start.13) | collective-permute-done | bytes 589856 | tf_op jit(solution)/shard_map/ppermute | solution.py:80
  90.1 8.4 %collective-permute-done.6 = bf16[36,8192]{1,0:T(8,128)(2,1)S(1)} collective-permute-done((bf16[36,8192]{1,0:T(8,128)(2,1)S(1)}, bf16[36,8192]{1,0:T(8,128)(2,1)S(1)}, u32[]{:S(2)}, u32[]{:S(2)}) %collective-permute-start.6) | collective-permute-done | bytes 589856 | tf_op jit(solution)/shard_map/ppermute | solution.py:79
  99.4 2.9 collective-permute-done.14
  104.8 7.4 %collective-permute-done.7 = bf16[36,8192]{1,0:T(8,128)(2,1)S(1)} collective-permute-done((bf16[36,8192]{1,0:T(8,128)(2,1)S(1)}, bf16[36,8192]{1,0:T(8,128)(2,1)S(1)}, u32[]{:S(2)}, u32[]{:S(2)}) %collective-permute-start.7) | collective-permute-done | bytes 589856 | tf_op jit(solution)/shard_map/ppermute | solution.py:79
  115.9 2.9 copy.33
  118.8 2.8 copy.34
  121.7 1.6 gather_fusion.1
  123.3 4.6 %copy.31 = f32[1,36,16384]{2,1,0:T(8,128)} copy(f32[1,36,16384]{2,0,1:T(1,128)} %param.14) | data formatting | bytes 4718592
  128.0 2.0 multiply_reduce_fusion
  130.1 2.2 multiply_reduce_fusion.1
  133.6 2.7 collective-permute-start.16
  137.9 2.8 collective-permute-start.17
  142.1 3.8 %collective-permute-start.18 = (f32[1,1]{1,0:T(1,128)}, f32[1,1]{1,0:T(1,128)}, u32[]{:S(2)}, u32[]{:S(2)}) collective-permute-start(f32[1,1]{1,0:T(1,128)} %add.319), channel_id=1, source_target_pairs={{0,16},{4,20},{8,24},{12,28},{16,0},{20,4},{24,8},{28,12},{1,17},{... | collective-permute-start | bytes 20 | tf_op jit(solution)/shard_map/ppermute | solution.py:41
  149.1 2.7 collective-permute-start.20
  153.5 4.9 %fusion.60 = (bf16[36,8192]{1,0:T(8,128)(2,1)S(1)}, f32[36,8192]{1,0:T(8,128)S(1)}, f32[36,8192]{1,0:T(8,128)S(1)}, f32[36,8192]{1,0:T(8,128)S(1)}, bf16[36,8192...) fusion(f32[36,16384]{1,0:T(8,128)} %bitcast.45, ...), kind=kLoop, calls=%fused_computation.150 | loop fusion | flops 13565952 | bytes 17694868 | tf_op jit(solution)/shard_map/convert_element_type | solution.py:113
  167.3 4.3 %collective-permute-done.35 = bf16[24,8192]{1,0:T(8,128)(2,1)S(1)} collective-permute-done((bf16[24,8192]{1,0:T(8,128)(2,1)S(1)}, bf16[24,8192]{1,0:T(8,128)(2,1)S(1)}, u32[]{:S(2)}, u32[]{:S(2)}) %collective-permute-start.35) | collective-permute-done | bytes 393248 | tf_op jit(solution)/shard_map/ppermute | solution.py:126
  174.9 10.7 %collective-permute-done.21 = bf16[36,8192]{1,0:T(8,128)(2,1)S(1)} collective-permute-done((bf16[36,8192]{1,0:T(8,128)(2,1)S(1)}, bf16[36,8192]{1,0:T(8,128)(2,1)S(1)}, u32[]{:S(2)}, u32[]{:S(2)}) %collective-permute-start.21) | collective-permute-done | bytes 589856 | tf_op jit(solution)/shard_map/ppermute | solution.py:124
  185.7 2.5 collective-permute-done.22
  188.2 1.6 collective-permute-start.23
  191.7 3.8 %copy.20 = f32[1,36,16384]{2,0,1:T(1,128)} copy(f32[1,36,16384]{2,1,0:T(8,128)S(1)} %bitcast.47) | data formatting | bytes 4718592
  195.6 3.8 %copy.21 = f32[1,36,16384]{2,0,1:T(1,128)} copy(f32[1,36,16384]{2,1,0:T(8,128)S(1)} %bitcast.46) | data formatting | bytes 4718592
  199.4 3.8 %copy.22 = f32[1,36,16384]{2,0,1:T(1,128)} copy(f32[1,36,16384]{2,1,0:T(8,128)S(1)} %bitcast.48) | data formatting | bytes 4718592
  204.4 1.6 collective-permute-start.37
  212.3 4.2 %collective-permute-done.37 = bf16[24,8192]{1,0:T(8,128)(2,1)S(1)} collective-permute-done((bf16[24,8192]{1,0:T(8,128)(2,1)S(1)}, bf16[24,8192]{1,0:T(8,128)(2,1)S(1)}, u32[]{:S(2)}, u32[]{:S(2)}) %collective-permute-start.37) | collective-permute-done | bytes 393248 | tf_op jit(solution)/shard_map/ppermute | solution.py:126
  219.9 17.4 %collective-permute-done.38 = bf16[24,8192]{1,0:T(8,128)(2,1)S(1)} collective-permute-done((bf16[24,8192]{1,0:T(8,128)(2,1)S(1)}, bf16[24,8192]{1,0:T(8,128)(2,1)S(1)}, u32[]{:S(2)}, u32[]{:S(2)}) %collective-permute-start.38) | collective-permute-done | bytes 393248 | tf_op jit(solution)/shard_map/ppermute | solution.py:126
  244.6 4.8 %collective-permute-done.39 = bf16[24,8192]{1,0:T(8,128)(2,1)S(1)} collective-permute-done((bf16[24,8192]{1,0:T(8,128)(2,1)S(1)}, bf16[24,8192]{1,0:T(8,128)(2,1)S(1)}, u32[]{:S(2)}, u32[]{:S(2)}) %collective-permute-start.39) | collective-permute-done | bytes 393248 | tf_op jit(solution)/shard_map/ppermute | solution.py:126
  252.5 11.0 %collective-permute-done.25 = bf16[36,8192]{1,0:T(8,128)(2,1)S(1)} collective-permute-done((bf16[36,8192]{1,0:T(8,128)(2,1)S(1)}, bf16[36,8192]{1,0:T(8,128)(2,1)S(1)}, u32[]{:S(2)}, u32[]{:S(2)}) %collective-permute-start.25) | collective-permute-done | bytes 589856 | tf_op jit(solution)/shard_map/ppermute | solution.py:124
  267.6 4.3 %collective-permute-done.40 = bf16[24,8192]{1,0:T(8,128)(2,1)S(1)} collective-permute-done((bf16[24,8192]{1,0:T(8,128)(2,1)S(1)}, bf16[24,8192]{1,0:T(8,128)(2,1)S(1)}, u32[]{:S(2)}, u32[]{:S(2)}) %collective-permute-start.40) | collective-permute-done | bytes 393248 | tf_op jit(solution)/shard_map/ppermute | solution.py:126
  274.9 16.7 %collective-permute-done.41 = bf16[24,8192]{1,0:T(8,128)(2,1)S(1)} collective-permute-done((bf16[24,8192]{1,0:T(8,128)(2,1)S(1)}, bf16[24,8192]{1,0:T(8,128)(2,1)S(1)}, u32[]{:S(2)}, u32[]{:S(2)}) %collective-permute-start.41) | collective-permute-done | bytes 393248 | tf_op jit(solution)/shard_map/ppermute | solution.py:126
  291.7 1.9 collective-permute-done.48
  295.0 1.6 collective-permute-start.27
  299.1 10.7 %collective-permute-done.27 = bf16[36,8192]{1,0:T(8,128)(2,1)S(1)} collective-permute-done((bf16[36,8192]{1,0:T(8,128)(2,1)S(1)}, bf16[36,8192]{1,0:T(8,128)(2,1)S(1)}, u32[]{:S(2)}, u32[]{:S(2)}) %collective-permute-start.27) | collective-permute-done | bytes 589856 | tf_op jit(solution)/shard_map/ppermute | solution.py:124
  314.0 8.7 %collective-permute-done.28 = bf16[36,8192]{1,0:T(8,128)(2,1)S(1)} collective-permute-done((bf16[36,8192]{1,0:T(8,128)(2,1)S(1)}, bf16[36,8192]{1,0:T(8,128)(2,1)S(1)}, u32[]{:S(2)}, u32[]{:S(2)}) %collective-permute-start.28) | collective-permute-done | bytes 589856 | tf_op jit(solution)/shard_map/ppermute | solution.py:124
  326.2 3.3 %maximum_bitcast_fusion = bf16[1,192,16384]{2,1,0:T(8,128)(2,1)} fusion(bf16[192,8192]{1,0:T(8,128)(2,1)S(1)} %convolution_add_fusion, bf16[192,8192]{1,0:T(8,128)(2,1)S(1)} %convolution_add_fusion.7), kind=kLoop, calls=%fused_computation.16 | loop fusion | flops 12582912 | bytes 12582912 | tf_op jit(solution)/shard_map/broadcast_in_dim | solution.py:141
  (151 shorter events, 84.6 us)
Async XLA Ops:
  0.6 17.5 %collective-permute-start = (bf16[8,128]{1,0:T(8,128)(2,1)S(1)}, bf16[8,128]{1,0:T(8,128)(2,1)S(1)}, u32[]{:S(2)}, u32[]{:S(2)}) collective-permute-start(bf16[8,128]{1,0:T(8,128)(2,1)S(1)} %broadcast_in_dim.15), channel_id=1, source_target_pairs={{0,8},{8,16},{16,24},{24,28},{28,20},{20,12},{12,4},{4,0},{1,9},{9... | collective-permute-start | bytes 6152 | tf_op jit(solution)/shard_map/ppermute | solution.py:63
  3.7 14.4 %collective-permute-start.1 = (bf16[8,128]{1,0:T(8,128)(2,1)S(1)}, bf16[8,128]{1,0:T(8,128)(2,1)S(1)}, u32[]{:S(2)}, u32[]{:S(2)}) collective-permute-start(bf16[8,128]{1,0:T(8,128)(2,1)S(1)} %broadcast_in_dim.15), channel_id=1, source_target_pairs={{8,0},{16,8},{24,16},{28,24},{20,28},{12,20},{4,12},{0,4},{9,1},{1... | collective-permute-start | bytes 6152 | tf_op jit(solution)/shard_map/ppermute | solution.py:63
  10.9 16.3 %collective-permute-start.9 = (bf16[36,8192]{1,0:T(8,128)(2,1)S(1)}, bf16[36,8192]{1,0:T(8,128)(2,1)S(1)}, u32[]{:S(2)}, u32[]{:S(2)}) collective-permute-start(bf16[36,8192]{1,0:T(8,128)(2,1)S(1)} %slice.275), channel_id=1, source_target_pairs={{8,0},{16,8},{24,16},{28,24},{20,28},{12,20},{4,12},{0,4},{9,1},{1... | collective-permute-start | bytes 1769480 | tf_op jit(solution)/shard_map/ppermute | solution.py:80
  20.9 15.7 %collective-permute-start.2 = (bf16[36,8192]{1,0:T(8,128)(2,1)S(1)}, bf16[36,8192]{1,0:T(8,128)(2,1)S(1)}, u32[]{:S(2)}, u32[]{:S(2)}) collective-permute-start(bf16[36,8192]{1,0:T(8,128)(2,1)S(1)} %slice_add_fusion), channel_id=1, source_target_pairs={{0,8},{8,16},{16,24},{24,28},{28,20},{20,12},{12,4},{4,0},{1,9},{9... | collective-permute-start | bytes 1769480 | tf_op jit(solution)/shard_map/ppermute | solution.py:79
  28.4 15.3 %collective-permute-start.10 = (bf16[36,8192]{1,0:T(8,128)(2,1)S(1)}, bf16[36,8192]{1,0:T(8,128)(2,1)S(1)}, u32[]{:S(2)}, u32[]{:S(2)}) collective-permute-start(bf16[36,8192]{1,0:T(8,128)(2,1)S(1)} %add_convert_fusion.5), channel_id=1, source_target_pairs={{8,0},{16,8},{24,16},{28,24},{20,28},{12,20},{4,12},{0,4},{9,1},{1... | collective-permute-start | bytes 1769480 | tf_op jit(solution)/shard_map/ppermute | solution.py:80
  37.8 14.8 %collective-permute-start.3 = (bf16[36,8192]{1,0:T(8,128)(2,1)S(1)}, bf16[36,8192]{1,0:T(8,128)(2,1)S(1)}, u32[]{:S(2)}, u32[]{:S(2)}) collective-permute-start(bf16[36,8192]{1,0:T(8,128)(2,1)S(1)} %add_convert_fusion.11), channel_id=1, source_target_pairs={{0,8},{8,16},{16,24},{24,28},{28,20},{20,12},{12,4},{4,0},{1,9},{9... | collective-permute-start | bytes 1769480 | tf_op jit(solution)/shard_map/ppermute | solution.py:79
  44.0 14.7 %collective-permute-start.11 = (bf16[36,8192]{1,0:T(8,128)(2,1)S(1)}, bf16[36,8192]{1,0:T(8,128)(2,1)S(1)}, u32[]{:S(2)}, u32[]{:S(2)}) collective-permute-start(bf16[36,8192]{1,0:T(8,128)(2,1)S(1)} %add_convert_fusion.4), channel_id=1, source_target_pairs={{8,0},{16,8},{24,16},{28,24},{20,28},{12,20},{4,12},{0,4},{9,1},{1... | collective-permute-start | bytes 1769480 | tf_op jit(solution)/shard_map/ppermute | solution.py:80
  54.0 14.7 %collective-permute-start.4 = (bf16[36,8192]{1,0:T(8,128)(2,1)S(1)}, bf16[36,8192]{1,0:T(8,128)(2,1)S(1)}, u32[]{:S(2)}, u32[]{:S(2)}) collective-permute-start(bf16[36,8192]{1,0:T(8,128)(2,1)S(1)} %add_convert_fusion.10), channel_id=1, source_target_pairs={{0,8},{8,16},{16,24},{24,28},{28,20},{20,12},{12,4},{4,0},{1,9},{9... | collective-permute-start | bytes 1769480 | tf_op jit(solution)/shard_map/ppermute | solution.py:79
  58.9 14.7 %collective-permute-start.12 = (bf16[36,8192]{1,0:T(8,128)(2,1)S(1)}, bf16[36,8192]{1,0:T(8,128)(2,1)S(1)}, u32[]{:S(2)}, u32[]{:S(2)}) collective-permute-start(bf16[36,8192]{1,0:T(8,128)(2,1)S(1)} %add_convert_fusion.3), channel_id=1, source_target_pairs={{8,0},{16,8},{24,16},{28,24},{20,28},{12,20},{4,12},{0,4},{9,1},{1... | collective-permute-start | bytes 1769480 | tf_op jit(solution)/shard_map/ppermute | solution.py:80
  68.8 14.6 %collective-permute-start.5 = (bf16[36,8192]{1,0:T(8,128)(2,1)S(1)}, bf16[36,8192]{1,0:T(8,128)(2,1)S(1)}, u32[]{:S(2)}, u32[]{:S(2)}) collective-permute-start(bf16[36,8192]{1,0:T(8,128)(2,1)S(1)} %add_convert_fusion.9), channel_id=1, source_target_pairs={{0,8},{8,16},{16,24},{24,28},{28,20},{20,12},{12,4},{4,0},{1,9},{9... | collective-permute-start | bytes 1769480 | tf_op jit(solution)/shard_map/ppermute | solution.py:79
  73.8 14.7 %collective-permute-start.13 = (bf16[36,8192]{1,0:T(8,128)(2,1)S(1)}, bf16[36,8192]{1,0:T(8,128)(2,1)S(1)}, u32[]{:S(2)}, u32[]{:S(2)}) collective-permute-start(bf16[36,8192]{1,0:T(8,128)(2,1)S(1)} %add_convert_fusion.2), channel_id=1, source_target_pairs={{8,0},{16,8},{24,16},{28,24},{20,28},{12,20},{4,12},{0,4},{9,1},{1... | collective-permute-start | bytes 1769480 | tf_op jit(solution)/shard_map/ppermute | solution.py:80
  83.7 14.7 %collective-permute-start.6 = (bf16[36,8192]{1,0:T(8,128)(2,1)S(1)}, bf16[36,8192]{1,0:T(8,128)(2,1)S(1)}, u32[]{:S(2)}, u32[]{:S(2)}) collective-permute-start(bf16[36,8192]{1,0:T(8,128)(2,1)S(1)} %add_convert_fusion.8), channel_id=1, source_target_pairs={{0,8},{8,16},{16,24},{24,28},{28,20},{20,12},{12,4},{4,0},{1,9},{9... | collective-permute-start | bytes 1769480 | tf_op jit(solution)/shard_map/ppermute | solution.py:79
  88.7 13.7 %collective-permute-start.14 = (bf16[36,8192]{1,0:T(8,128)(2,1)S(1)}, bf16[36,8192]{1,0:T(8,128)(2,1)S(1)}, u32[]{:S(2)}, u32[]{:S(2)}) collective-permute-start(bf16[36,8192]{1,0:T(8,128)(2,1)S(1)} %add_convert_fusion.1), channel_id=1, source_target_pairs={{8,0},{16,8},{24,16},{28,24},{20,28},{12,20},{4,12},{0,4},{9,1},{1... | collective-permute-start | bytes 1769480 | tf_op jit(solution)/shard_map/ppermute | solution.py:80
  98.6 13.5 %collective-permute-start.7 = (bf16[36,8192]{1,0:T(8,128)(2,1)S(1)}, bf16[36,8192]{1,0:T(8,128)(2,1)S(1)}, u32[]{:S(2)}, u32[]{:S(2)}) collective-permute-start(bf16[36,8192]{1,0:T(8,128)(2,1)S(1)} %add_convert_fusion.7), channel_id=1, source_target_pairs={{0,8},{8,16},{16,24},{24,28},{28,20},{20,12},{12,4},{4,0},{1,9},{9... | collective-permute-start | bytes 1769480 | tf_op jit(solution)/shard_map/ppermute | solution.py:79
  103.4 24.6 %collective-permute-start.15 = (bf16[36,8192]{1,0:T(8,128)(2,1)}, bf16[36,8192]{1,0:T(8,128)(2,1)S(1)}, u32[]{:S(2)}, u32[]{:S(2)}) collective-permute-start(bf16[36,8192]{1,0:T(8,128)(2,1)} %add_convert_fusion), channel_id=1, source_target_pairs={{8,0},{16,8},{24,16},{28,24},{20,28},{12,20},{4,12},{0,4},{9,1},{1... | collective-permute-start | bytes 1769480 | tf_op jit(solution)/shard_map/ppermute | solution.py:80
  113.2 16.8 %collective-permute-start.8 = (bf16[36,8192]{1,0:T(8,128)(2,1)}, bf16[36,8192]{1,0:T(8,128)(2,1)}, u32[]{:S(2)}, u32[]{:S(2)}) collective-permute-start(bf16[36,8192]{1,0:T(8,128)(2,1)} %add_convert_fusion.6), channel_id=1, source_target_pairs={{0,8},{8,16},{16,24},{24,28},{28,20},{20,12},{12,4},{4,0},{1,9},{9... | collective-permute-start | bytes 1769480 | tf_op jit(solution)/shard_map/ppermute | solution.py:79
  133.6 3.6 %collective-permute-start.16 = (f32[1,1]{1,0:T(1,128)}, f32[1,1]{1,0:T(1,128)}, u32[]{:S(2)}, u32[]{:S(2)}) collective-permute-start(f32[1,1]{1,0:T(1,128)} %bitcast.3), channel_id=1, source_target_pairs={{0,4},{4,0},{8,12},{12,8},{16,20},{20,16},{24,28},{28,24},{1,5},{5... | collective-permute-start | bytes 20 | tf_op jit(solution)/shard_map/ppermute | solution.py:41
  137.9 3.6 %collective-permute-start.17 = (f32[1,1]{1,0:T(1,128)}, f32[1,1]{1,0:T(1,128)}, u32[]{:S(2)}, u32[]{:S(2)}) collective-permute-start(f32[1,1]{1,0:T(1,128)} %add.318), channel_id=1, source_target_pairs={{0,8},{4,12},{8,0},{12,4},{16,24},{20,28},{24,16},{28,20},{1,9},{5... | collective-permute-start | bytes 20 | tf_op jit(solution)/shard_map/ppermute | solution.py:41
  142.1 4.5 %collective-permute-start.18 = (f32[1,1]{1,0:T(1,128)}, f32[1,1]{1,0:T(1,128)}, u32[]{:S(2)}, u32[]{:S(2)}) collective-permute-start(f32[1,1]{1,0:T(1,128)} %add.319), channel_id=1, source_target_pairs={{0,16},{4,20},{8,24},{12,28},{16,0},{20,4},{24,8},{28,12},{1,17},{... | collective-permute-start | bytes 20 | tf_op jit(solution)/shard_map/ppermute | solution.py:41
  149.1 3.6 %collective-permute-start.20 = (f32[1,1]{1,0:T(1,128)}, f32[1,1]{1,0:T(1,128)}, u32[]{:S(2)}, u32[]{:S(2)}) collective-permute-start(f32[1,1]{1,0:T(1,128)} %add.321), channel_id=1, source_target_pairs={{0,2},{1,3},{2,0},{3,1},{4,6},{5,7},{6,4},{7,5},{8,10},{9,11},{10,... | collective-permute-start | bytes 20 | tf_op jit(solution)/shard_map/ppermute | solution.py:41
  159.5 12.1 %collective-permute-start.35 = (bf16[24,8192]{1,0:T(8,128)(2,1)S(1)}, bf16[24,8192]{1,0:T(8,128)(2,1)S(1)}, u32[]{:S(2)}, u32[]{:S(2)}) collective-permute-start(bf16[24,8192]{1,0:T(8,128)(2,1)S(1)} %slice.295), channel_id=1, source_target_pairs={{0,8},{8,16},{16,24},{24,28},{28,20},{20,12},{12,4},{4,0},{1,9},{9... | collective-permute-start | bytes 1179656 | tf_op jit(solution)/shard_map/ppermute | solution.py:126
  162.1 12.1 %collective-permute-start.42 = (bf16[24,8192]{1,0:T(8,128)(2,1)S(1)}, bf16[24,8192]{1,0:T(8,128)(2,1)S(1)}, u32[]{:S(2)}, u32[]{:S(2)}) collective-permute-start(bf16[24,8192]{1,0:T(8,128)(2,1)S(1)} %slice.304), channel_id=1, source_target_pairs={{8,0},{16,8},{24,16},{28,24},{20,28},{12,20},{4,12},{0,4},{9,1},{1... | collective-permute-start | bytes 1179656 | tf_op jit(solution)/shard_map/ppermute | solution.py:127
  162.7 22.9 %collective-permute-start.21 = (bf16[36,8192]{1,0:T(8,128)(2,1)S(1)}, bf16[36,8192]{1,0:T(8,128)(2,1)S(1)}, u32[]{:S(2)}, u32[]{:S(2)}) collective-permute-start(bf16[36,8192]{1,0:T(8,128)(2,1)S(1)} %get-tuple-element.30), channel_id=1, source_target_pairs={{0,8},{8,16},{16,24},{24,28},{28,20},{20,12},{12,4},{4,0},{1,9},{9... | collective-permute-start | bytes 1769480 | tf_op jit(solution)/shard_map/ppermute | solution.py:124
  164.1 24.1 %collective-permute-start.22 = (bf16[36,8192]{1,0:T(8,128)(2,1)S(1)}, bf16[36,8192]{1,0:T(8,128)(2,1)S(1)}, u32[]{:S(2)}, u32[]{:S(2)}) collective-permute-start(bf16[36,8192]{1,0:T(8,128)(2,1)S(1)} %get-tuple-element.38), channel_id=1, source_target_pairs={{8,0},{16,8},{24,16},{28,24},{20,28},{12,20},{4,12},{0,4},{9,1},{1... | collective-permute-start | bytes 1769480 | tf_op jit(solution)/shard_map/ppermute | solution.py:125
  171.7 32.5 %collective-permute-start.36 = (bf16[24,8192]{1,0:T(8,128)(2,1)S(1)}, bf16[24,8192]{1,0:T(8,128)(2,1)S(1)}, u32[]{:S(2)}, u32[]{:S(2)}) collective-permute-start(bf16[24,8192]{1,0:T(8,128)(2,1)S(1)} %add_convert_fusion.23), channel_id=1, source_target_pairs={{0,8},{8,16},{16,24},{24,28},{28,20},{20,12},{12,4},{4,0},{1,9},{9... | collective-permute-start | bytes 1179656 | tf_op jit(solution)/shard_map/ppermute | solution.py:126
  174.3 31.7 %collective-permute-start.43 = (bf16[24,8192]{1,0:T(8,128)(2,1)S(1)}, bf16[24,8192]{1,0:T(8,128)(2,1)S(1)}, u32[]{:S(2)}, u32[]{:S(2)}) collective-permute-start(bf16[24,8192]{1,0:T(8,128)(2,1)S(1)} %add_convert_fusion.17), channel_id=1, source_target_pairs={{8,0},{16,8},{24,16},{28,24},{20,28},{12,20},{4,12},{0,4},{9,1},{1... | collective-permute-start | bytes 1179656 | tf_op jit(solution)/shard_map/ppermute | solution.py:127
  188.2 19.9 %collective-permute-start.23 = (bf16[36,8192]{1,0:T(8,128)(2,1)S(1)}, bf16[36,8192]{1,0:T(8,128)(2,1)S(1)}, u32[]{:S(2)}, u32[]{:S(2)}) collective-permute-start(bf16[36,8192]{1,0:T(8,128)(2,1)S(1)} %collective-permute-done.21), channel_id=1, source_target_pairs={{0,8},{8,16},{16,24},{24,28},{28,20},{20,12},{12,4},{4,0},{1,9},{9... | collective-permute-start | bytes 1769480 | tf_op jit(solution)/shard_map/ppermute | solution.py:124
  190.8 19.9 %collective-permute-start.29 = (bf16[36,8192]{1,0:T(8,128)(2,1)S(1)}, bf16[36,8192]{1,0:T(8,128)(2,1)S(1)}, u32[]{:S(2)}, u32[]{:S(2)}) collective-permute-start(bf16[36,8192]{1,0:T(8,128)(2,1)S(1)} %collective-permute-done.22), channel_id=1, source_target_pairs={{8,0},{16,8},{24,16},{28,24},{20,28},{12,20},{4,12},{0,4},{9,1},{1... | collective-permute-start | bytes 1769480 | tf_op jit(solution)/shard_map/ppermute | solution.py:125
  204.4 12.2 %collective-permute-start.37 = (bf16[24,8192]{1,0:T(8,128)(2,1)S(1)}, bf16[24,8192]{1,0:T(8,128)(2,1)S(1)}, u32[]{:S(2)}, u32[]{:S(2)}) collective-permute-start(bf16[24,8192]{1,0:T(8,128)(2,1)S(1)} %add_convert_fusion.22), channel_id=1, source_target_pairs={{0,8},{8,16},{16,24},{24,28},{28,20},{20,12},{12,4},{4,0},{1,9},{9... | collective-permute-start | bytes 1179656 | tf_op jit(solution)/shard_map/ppermute | solution.py:126
  206.1 13.0 %collective-permute-start.44 = (bf16[24,8192]{1,0:T(8,128)(2,1)S(1)}, bf16[24,8192]{1,0:T(8,128)(2,1)S(1)}, u32[]{:S(2)}, u32[]{:S(2)}) collective-permute-start(bf16[24,8192]{1,0:T(8,128)(2,1)S(1)} %add_convert_fusion.16), channel_id=1, source_target_pairs={{8,0},{16,8},{24,16},{28,24},{20,28},{12,20},{4,12},{0,4},{9,1},{1... | collective-permute-start | bytes 1179656 | tf_op jit(solution)/shard_map/ppermute | solution.py:127
  208.1 32.1 %collective-permute-start.24 = (bf16[36,8192]{1,0:T(8,128)(2,1)S(1)}, bf16[36,8192]{1,0:T(8,128)(2,1)S(1)}, u32[]{:S(2)}, u32[]{:S(2)}) collective-permute-start(bf16[36,8192]{1,0:T(8,128)(2,1)S(1)} %collective-permute-done.23), channel_id=1, source_target_pairs={{0,8},{8,16},{16,24},{24,28},{28,20},{20,12},{12,4},{4,0},{1,9},{9... | collective-permute-start | bytes 1769480 | tf_op jit(solution)/shard_map/ppermute | solution.py:124
  210.7 32.2 %collective-permute-start.30 = (bf16[36,8192]{1,0:T(8,128)(2,1)S(1)}, bf16[36,8192]{1,0:T(8,128)(2,1)S(1)}, u32[]{:S(2)}, u32[]{:S(2)}) collective-permute-start(bf16[36,8192]{1,0:T(8,128)(2,1)S(1)} %collective-permute-done.29), channel_id=1, source_target_pairs={{8,0},{16,8},{24,16},{28,24},{20,28},{12,20},{4,12},{0,4},{9,1},{1... | collective-permute-start | bytes 1769480 | tf_op jit(solution)/shard_map/ppermute | solution.py:125
  216.7 20.6 %collective-permute-start.38 = (bf16[24,8192]{1,0:T(8,128)(2,1)S(1)}, bf16[24,8192]{1,0:T(8,128)(2,1)S(1)}, u32[]{:S(2)}, u32[]{:S(2)}) collective-permute-start(bf16[24,8192]{1,0:T(8,128)(2,1)S(1)} %add_convert_fusion.21), channel_id=1, source_target_pairs={{0,8},{8,16},{16,24},{24,28},{28,20},{20,12},{12,4},{4,0},{1,9},{9... | collective-permute-start | bytes 1179656 | tf_op jit(solution)/shard_map/ppermute | solution.py:126
  219.2 20.3 %collective-permute-start.45 = (bf16[24,8192]{1,0:T(8,128)(2,1)S(1)}, bf16[24,8192]{1,0:T(8,128)(2,1)S(1)}, u32[]{:S(2)}, u32[]{:S(2)}) collective-permute-start(bf16[24,8192]{1,0:T(8,128)(2,1)S(1)} %add_convert_fusion.15), channel_id=1, source_target_pairs={{8,0},{16,8},{24,16},{28,24},{20,28},{12,20},{4,12},{0,4},{9,1},{1... | collective-permute-start | bytes 1179656 | tf_op jit(solution)/shard_map/ppermute | solution.py:127
  237.3 12.1 %collective-permute-start.39 = (bf16[24,8192]{1,0:T(8,128)(2,1)S(1)}, bf16[24,8192]{1,0:T(8,128)(2,1)S(1)}, u32[]{:S(2)}, u32[]{:S(2)}) collective-permute-start(bf16[24,8192]{1,0:T(8,128)(2,1)S(1)} %add_convert_fusion.20), channel_id=1, source_target_pairs={{0,8},{8,16},{16,24},{24,28},{28,20},{20,12},{12,4},{4,0},{1,9},{9... | collective-permute-start | bytes 1179656 | tf_op jit(solution)/shard_map/ppermute | solution.py:126
  239.6 12.1 %collective-permute-start.46 = (bf16[24,8192]{1,0:T(8,128)(2,1)S(1)}, bf16[24,8192]{1,0:T(8,128)(2,1)S(1)}, u32[]{:S(2)}, u32[]{:S(2)}) collective-permute-start(bf16[24,8192]{1,0:T(8,128)(2,1)S(1)} %add_convert_fusion.14), channel_id=1, source_target_pairs={{8,0},{16,8},{24,16},{28,24},{20,28},{12,20},{4,12},{0,4},{9,1},{1... | collective-permute-start | bytes 1179656 | tf_op jit(solution)/shard_map/ppermute | solution.py:127
  240.3 23.2 %collective-permute-start.25 = (bf16[36,8192]{1,0:T(8,128)(2,1)S(1)}, bf16[36,8192]{1,0:T(8,128)(2,1)S(1)}, u32[]{:S(2)}, u32[]{:S(2)}) collective-permute-start(bf16[36,8192]{1,0:T(8,128)(2,1)S(1)} %collective-permute-done.24), channel_id=1, source_target_pairs={{0,8},{8,16},{16,24},{24,28},{28,20},{20,12},{12,4},{4,0},{1,9},{9... | collective-permute-start | bytes 1769480 | tf_op jit(solution)/shard_map/ppermute | solution.py:124
  242.9 23.1 %collective-permute-start.31 = (bf16[36,8192]{1,0:T(8,128)(2,1)S(1)}, bf16[36,8192]{1,0:T(8,128)(2,1)S(1)}, u32[]{:S(2)}, u32[]{:S(2)}) collective-permute-start(bf16[36,8192]{1,0:T(8,128)(2,1)S(1)} %collective-permute-done.30), channel_id=1, source_target_pairs={{8,0},{16,8},{24,16},{28,24},{20,28},{12,20},{4,12},{0,4},{9,1},{1... | collective-permute-start | bytes 1769480 | tf_op jit(solution)/shard_map/ppermute | solution.py:125
  249.5 22.4 %collective-permute-start.40 = (bf16[24,8192]{1,0:T(8,128)(2,1)S(1)}, bf16[24,8192]{1,0:T(8,128)(2,1)S(1)}, u32[]{:S(2)}, u32[]{:S(2)}) collective-permute-start(bf16[24,8192]{1,0:T(8,128)(2,1)S(1)} %add_convert_fusion.19), channel_id=1, source_target_pairs={{0,8},{8,16},{16,24},{24,28},{28,20},{20,12},{12,4},{4,0},{1,9},{9... | collective-permute-start | bytes 1179656 | tf_op jit(solution)/shard_map/ppermute | solution.py:126
  251.8 22.4 %collective-permute-start.47 = (bf16[24,8192]{1,0:T(8,128)(2,1)S(1)}, bf16[24,8192]{1,0:T(8,128)(2,1)S(1)}, u32[]{:S(2)}, u32[]{:S(2)}) collective-permute-start(bf16[24,8192]{1,0:T(8,128)(2,1)S(1)} %add_convert_fusion.13), channel_id=1, source_target_pairs={{8,0},{16,8},{24,16},{28,24},{20,28},{12,20},{4,12},{0,4},{9,1},{1... | collective-permute-start | bytes 1179656 | tf_op jit(solution)/shard_map/ppermute | solution.py:127
  263.5 31.5 %collective-permute-start.26 = (bf16[36,8192]{1,0:T(8,128)(2,1)S(1)}, bf16[36,8192]{1,0:T(8,128)(2,1)S(1)}, u32[]{:S(2)}, u32[]{:S(2)}) collective-permute-start(bf16[36,8192]{1,0:T(8,128)(2,1)S(1)} %collective-permute-done.25), channel_id=1, source_target_pairs={{0,8},{8,16},{16,24},{24,28},{28,20},{20,12},{12,4},{4,0},{1,9},{9... | collective-permute-start | bytes 1769480 | tf_op jit(solution)/shard_map/ppermute | solution.py:124
  265.9 31.7 %collective-permute-start.32 = (bf16[36,8192]{1,0:T(8,128)(2,1)S(1)}, bf16[36,8192]{1,0:T(8,128)(2,1)S(1)}, u32[]{:S(2)}, u32[]{:S(2)}) collective-permute-start(bf16[36,8192]{1,0:T(8,128)(2,1)S(1)} %collective-permute-done.31), channel_id=1, source_target_pairs={{8,0},{16,8},{24,16},{28,24},{20,28},{12,20},{4,12},{0,4},{9,1},{1... | collective-permute-start | bytes 1769480 | tf_op jit(solution)/shard_map/ppermute | solution.py:125
  272.0 19.6 %collective-permute-start.41 = (bf16[24,8192]{1,0:T(8,128)(2,1)S(1)}, bf16[24,8192]{1,0:T(8,128)(2,1)S(1)}, u32[]{:S(2)}, u32[]{:S(2)}) collective-permute-start(bf16[24,8192]{1,0:T(8,128)(2,1)S(1)} %add_convert_fusion.18), channel_id=1, source_target_pairs={{0,8},{8,16},{16,24},{24,28},{28,20},{20,12},{12,4},{4,0},{1,9},{9... | collective-permute-start | bytes 1179656 | tf_op jit(solution)/shard_map/ppermute | solution.py:126
  274.3 19.4 %collective-permute-start.48 = (bf16[24,8192]{1,0:T(8,128)(2,1)S(1)}, bf16[24,8192]{1,0:T(8,128)(2,1)S(1)}, u32[]{:S(2)}, u32[]{:S(2)}) collective-permute-start(bf16[24,8192]{1,0:T(8,128)(2,1)S(1)} %add_convert_fusion.12), channel_id=1, source_target_pairs={{8,0},{16,8},{24,16},{28,24},{20,28},{12,20},{4,12},{0,4},{9,1},{1... | collective-permute-start | bytes 1179656 | tf_op jit(solution)/shard_map/ppermute | solution.py:127
  295.0 14.9 %collective-permute-start.27 = (bf16[36,8192]{1,0:T(8,128)(2,1)S(1)}, bf16[36,8192]{1,0:T(8,128)(2,1)S(1)}, u32[]{:S(2)}, u32[]{:S(2)}) collective-permute-start(bf16[36,8192]{1,0:T(8,128)(2,1)S(1)} %collective-permute-done.26), channel_id=1, source_target_pairs={{0,8},{8,16},{16,24},{24,28},{28,20},{20,12},{12,4},{4,0},{1,9},{9... | collective-permute-start | bytes 1769480 | tf_op jit(solution)/shard_map/ppermute | solution.py:124
  297.6 14.9 %collective-permute-start.33 = (bf16[36,8192]{1,0:T(8,128)(2,1)S(1)}, bf16[36,8192]{1,0:T(8,128)(2,1)S(1)}, u32[]{:S(2)}, u32[]{:S(2)}) collective-permute-start(bf16[36,8192]{1,0:T(8,128)(2,1)S(1)} %collective-permute-done.32), channel_id=1, source_target_pairs={{8,0},{16,8},{24,16},{28,24},{20,28},{12,20},{4,12},{0,4},{9,1},{1... | collective-permute-start | bytes 1769480 | tf_op jit(solution)/shard_map/ppermute | solution.py:125
  309.9 12.9 %collective-permute-start.28 = (bf16[36,8192]{1,0:T(8,128)(2,1)S(1)}, bf16[36,8192]{1,0:T(8,128)(2,1)S(1)}, u32[]{:S(2)}, u32[]{:S(2)}) collective-permute-start(bf16[36,8192]{1,0:T(8,128)(2,1)S(1)} %collective-permute-done.27), channel_id=1, source_target_pairs={{0,8},{8,16},{16,24},{24,28},{28,20},{20,12},{12,4},{4,0},{1,9},{9... | collective-permute-start | bytes 1769480 | tf_op jit(solution)/shard_map/ppermute | solution.py:124
  312.5 12.7 %collective-permute-start.34 = (bf16[36,8192]{1,0:T(8,128)(2,1)S(1)}, bf16[36,8192]{1,0:T(8,128)(2,1)S(1)}, u32[]{:S(2)}, u32[]{:S(2)}) collective-permute-start(bf16[36,8192]{1,0:T(8,128)(2,1)S(1)} %collective-permute-done.33), channel_id=1, source_target_pairs={{8,0},{16,8},{24,16},{28,24},{20,28},{12,20},{4,12},{0,4},{9,1},{1... | collective-permute-start | bytes 1769480 | tf_op jit(solution)/shard_map/ppermute | solution.py:125
  (10 other events, 94.2 us)

commit v6 on v5

--- a/solution.py
+++ b/solution.py
@@ -82,7 +82,7 @@
             acc_b = got_b.astype(jnp.float32) + right[(2 + t) % n].astype(jnp.float32)
             if t < n - 2:
                 send_a, send_b = acc_a.astype(jnp.bfloat16), acc_b.astype(jnp.bfloat16)
-        total_sq = all_sum(all_sum((jnp.sum(acc_a * acc_a) + jnp.sum(acc_b * acc_b)).reshape(1, 1), "dp", n), "mp", blocks)[0, 0]
+        total_sq = all_sum(all_sum((jnp.sum(acc_a * acc_a) + jnp.sum(acc_b * acc_b)).reshape(1, 1), "mp", blocks), "dp", n)[0, 0]
         clip_factor = jnp.minimum(1.0, math.sqrt(blocks * nseg * seg) / (jnp.sqrt(total_sq) + 1e-06))
         in_use = valid.astype(jnp.float32)[:, None]
 

time: 336 us -> 330 us (0.982)
  waiting for transfers between devices: 180 us -> 174 us
    ppermute x7, waiting for transfers between devices: 51.8 us -> 47.2 us  [on_device(): got_a = lax.ppermute(sum_a, 'dp', fwd)]
where the time goes in v6:
time: 330 us; the launch traced here: 324 us
  waiting for transfers between devices  174 us (53%)
  starting transfers between devices  61.4 us (19%)
  other arithmetic  28.5 us (9%)
  local copies, waits for them, and re-layouts  27.9 us (8%)
  matrix products  25.5 us (8%)
  between operations  6.16 us (2%)
    ppermute x7, waiting for transfers between devices, on_device(): got_a = lax.ppermute(sum_a, 'dp', fwd)  47.2 us
    ppermute x7, waiting for transfers between devices, on_device(): got_a = lax.ppermute(send_a, 'dp', fwd)  46.1 us
    ppermute x7, waiting for transfers between devices, on_device(): send_a = lax.ppermute(send_a, 'dp', fwd)  40.2 us
    ppermute x7, waiting for transfers between devices, on_device(): got_b = lax.ppermute(send_b, 'dp', bwd)  26.4 us
    unnamed x25, local copies, waits for them, and re-layouts  23.6 us
    dot_general x16, matrix products, spread(): jnp.dot(placing_t[:, k * cap:(k + 1) * cap], chunk, preferred_element_typ...  16.4 us
    ppermute x5, starting transfers between devices, all_sum(): v = v + lax.ppermute(v, axis, [(i, i ^ k) for i in range(n)])  12.8 us
    ppermute x7, starting transfers between devices, on_device(): got_b = lax.ppermute(send_b, 'dp', bwd)  10.8 us
  transfers between devices with their start and end apart: 49, of which 37 were waited for; matrix products, arithmetic and copies ran while one was open for 21% of the time, Pallas kernels for 0%

profile of v6, /device:TPU:0, one launch (start us, length us, event | category | flops | bytes accessed | tf_op | source)
XLA Modules:
  0.0 323.9 jit_solution(12426760406722242966)
XLA Ops:
  0.6 3.1 collective-permute-start
  7.3 3.4 %fusion = bf16[288,8192]{1,0:T(8,128)(2,1)S(1)} fusion(bf16[192,16384]{1,0:T(8,128)(2,1)} %bitcast.51, s32[192]{0:T(256)S(1)} %fusion.50), kind=kOutput, calls=%fused_computation.17 | convolution fusion | flops 906024960 | bytes 7865088 | tf_op jit(solution)/shard_map/dot_general | solution.py:74
  10.9 2.0 collective-permute-start.9
  12.9 3.6 %fusion.2 = bf16[288,8192]{1,0:T(8,128)(2,1)} fusion(bf16[192,16384]{1,0:T(8,128)(2,1)S(1)} %bitcast.52, s32[192]{0:T(256)S(1)} %fusion.50), kind=kOutput, calls=%fused_computation.19 | convolution fusion | flops 906024960 | bytes 7865344 | tf_op jit(solution)/shard_map/dot_general | solution.py:73
  18.6 2.3 slice_add_fusion
  21.0 6.1 %collective-permute-done.9 = bf16[36,8192]{1,0:T(8,128)(2,1)S(1)} collective-permute-done((bf16[36,8192]{1,0:T(8,128)(2,1)S(1)}, bf16[36,8192]{1,0:T(8,128)(2,1)S(1)}, u32[]{:S(2)}, u32[]{:S(2)}) %collective-permute-start.9) | collective-permute-done | bytes 589856 | tf_op jit(solution)/shard_map/ppermute | solution.py:80
  28.4 1.7 collective-permute-start.10
  30.1 6.5 %collective-permute-done.2 = bf16[36,8192]{1,0:T(8,128)(2,1)S(1)} collective-permute-done((bf16[36,8192]{1,0:T(8,128)(2,1)S(1)}, bf16[36,8192]{1,0:T(8,128)(2,1)S(1)}, u32[]{:S(2)}, u32[]{:S(2)}) %collective-permute-start.2) | collective-permute-done | bytes 589856 | tf_op jit(solution)/shard_map/ppermute | solution.py:79
  38.3 5.4 %collective-permute-done.10 = bf16[36,8192]{1,0:T(8,128)(2,1)S(1)} collective-permute-done((bf16[36,8192]{1,0:T(8,128)(2,1)S(1)}, bf16[36,8192]{1,0:T(8,128)(2,1)S(1)}, u32[]{:S(2)}, u32[]{:S(2)}) %collective-permute-start.10) | collective-permute-done | bytes 589856 | tf_op jit(solution)/shard_map/ppermute | solution.py:80
  45.4 7.2 %collective-permute-done.3 = bf16[36,8192]{1,0:T(8,128)(2,1)S(1)} collective-permute-done((bf16[36,8192]{1,0:T(8,128)(2,1)S(1)}, bf16[36,8192]{1,0:T(8,128)(2,1)S(1)}, u32[]{:S(2)}, u32[]{:S(2)}) %collective-permute-start.3) | collective-permute-done | bytes 589856 | tf_op jit(solution)/shard_map/ppermute | solution.py:79
  54.7 4.0 %collective-permute-done.11 = bf16[36,8192]{1,0:T(8,128)(2,1)S(1)} collective-permute-done((bf16[36,8192]{1,0:T(8,128)(2,1)S(1)}, bf16[36,8192]{1,0:T(8,128)(2,1)S(1)}, u32[]{:S(2)}, u32[]{:S(2)}) %collective-permute-start.11) | collective-permute-done | bytes 589856 | tf_op jit(solution)/shard_map/ppermute | solution.py:80
  60.3 8.4 %collective-permute-done.4 = bf16[36,8192]{1,0:T(8,128)(2,1)S(1)} collective-permute-done((bf16[36,8192]{1,0:T(8,128)(2,1)S(1)}, bf16[36,8192]{1,0:T(8,128)(2,1)S(1)}, u32[]{:S(2)}, u32[]{:S(2)}) %collective-permute-start.4) | collective-permute-done | bytes 589856 | tf_op jit(solution)/shard_map/ppermute | solution.py:79
  69.6 3.9 %collective-permute-done.12 = bf16[36,8192]{1,0:T(8,128)(2,1)S(1)} collective-permute-done((bf16[36,8192]{1,0:T(8,128)(2,1)S(1)}, bf16[36,8192]{1,0:T(8,128)(2,1)S(1)}, u32[]{:S(2)}, u32[]{:S(2)}) %collective-permute-start.12) | collective-permute-done | bytes 589856 | tf_op jit(solution)/shard_map/ppermute | solution.py:80
  75.2 8.3 %collective-permute-done.5 = bf16[36,8192]{1,0:T(8,128)(2,1)S(1)} collective-permute-done((bf16[36,8192]{1,0:T(8,128)(2,1)S(1)}, bf16[36,8192]{1,0:T(8,128)(2,1)S(1)}, u32[]{:S(2)}, u32[]{:S(2)}) %collective-permute-start.5) | collective-permute-done | bytes 589856 | tf_op jit(solution)/shard_map/ppermute | solution.py:79
  84.5 4.0 %collective-permute-done.13 = bf16[36,8192]{1,0:T(8,128)(2,1)S(1)} collective-permute-done((bf16[36,8192]{1,0:T(8,128)(2,1)S(1)}, bf16[36,8192]{1,0:T(8,128)(2,1)S(1)}, u32[]{:S(2)}, u32[]{:S(2)}) %collective-permute-start.13) | collective-permute-done | bytes 589856 | tf_op jit(solution)/shard_map/ppermute | solution.py:80
  90.1 8.4 %collective-permute-done.6 = bf16[36,8192]{1,0:T(8,128)(2,1)S(1)} collective-permute-done((bf16[36,8192]{1,0:T(8,128)(2,1)S(1)}, bf16[36,8192]{1,0:T(8,128)(2,1)S(1)}, u32[]{:S(2)}, u32[]{:S(2)}) %collective-permute-start.6) | collective-permute-done | bytes 589856 | tf_op jit(solution)/shard_map/ppermute | solution.py:79
  99.4 2.9 collective-permute-done.14
  104.8 7.4 %collective-permute-done.7 = bf16[36,8192]{1,0:T(8,128)(2,1)S(1)} collective-permute-done((bf16[36,8192]{1,0:T(8,128)(2,1)S(1)}, bf16[36,8192]{1,0:T(8,128)(2,1)S(1)}, u32[]{:S(2)}, u32[]{:S(2)}) %collective-permute-start.7) | collective-permute-done | bytes 589856 | tf_op jit(solution)/shard_map/ppermute | solution.py:79
  115.9 2.9 copy.33
  118.8 2.8 copy.34
  121.7 1.6 gather_fusion.1
  123.3 4.6 %copy.31 = f32[1,36,16384]{2,1,0:T(8,128)} copy(f32[1,36,16384]{2,0,1:T(1,128)} %param.14) | data formatting | bytes 4718592
  128.0 2.0 multiply_reduce_fusion
  130.1 2.2 multiply_reduce_fusion.1
  135.5 2.7 collective-permute-start.17
  139.7 2.7 collective-permute-start.18
  144.0 2.8 collective-permute-start.19
  148.2 3.8 %collective-permute-start.20 = (f32[1,1]{1,0:T(1,128)}, f32[1,1]{1,0:T(1,128)}, u32[]{:S(2)}, u32[]{:S(2)}) collective-permute-start(f32[1,1]{1,0:T(1,128)} %add.321), channel_id=1, source_target_pairs={{0,16},{4,20},{8,24},{12,28},{16,0},{20,4},{24,8},{28,12},{1,17},{... | collective-permute-start | bytes 20 | tf_op jit(solution)/shard_map/ppermute | solution.py:41
  153.5 4.9 %fusion.60 = (bf16[36,8192]{1,0:T(8,128)(2,1)S(1)}, f32[36,8192]{1,0:T(8,128)S(1)}, f32[36,8192]{1,0:T(8,128)S(1)}, f32[36,8192]{1,0:T(8,128)S(1)}, bf16[36,8192...) fusion(f32[36,16384]{1,0:T(8,128)} %bitcast.45, ...), kind=kLoop, calls=%fused_computation.150 | loop fusion | flops 13565952 | bytes 17694868 | tf_op jit(solution)/shard_map/convert_element_type | solution.py:113
  167.3 4.3 %collective-permute-done.35 = bf16[24,8192]{1,0:T(8,128)(2,1)S(1)} collective-permute-done((bf16[24,8192]{1,0:T(8,128)(2,1)S(1)}, bf16[24,8192]{1,0:T(8,128)(2,1)S(1)}, u32[]{:S(2)}, u32[]{:S(2)}) %collective-permute-start.35) | collective-permute-done | bytes 393248 | tf_op jit(solution)/shard_map/ppermute | solution.py:126
  174.9 10.7 %collective-permute-done.21 = bf16[36,8192]{1,0:T(8,128)(2,1)S(1)} collective-permute-done((bf16[36,8192]{1,0:T(8,128)(2,1)S(1)}, bf16[36,8192]{1,0:T(8,128)(2,1)S(1)}, u32[]{:S(2)}, u32[]{:S(2)}) %collective-permute-start.21) | collective-permute-done | bytes 589856 | tf_op jit(solution)/shard_map/ppermute | solution.py:124
  185.7 2.5 collective-permute-done.22
  191.7 3.8 %copy.20 = f32[1,36,16384]{2,0,1:T(1,128)} copy(f32[1,36,16384]{2,1,0:T(8,128)S(1)} %bitcast.47) | data formatting | bytes 4718592
  195.6 3.8 %copy.21 = f32[1,36,16384]{2,0,1:T(1,128)} copy(f32[1,36,16384]{2,1,0:T(8,128)S(1)} %bitcast.46) | data formatting | bytes 4718592
  199.4 3.8 %copy.22 = f32[1,36,16384]{2,0,1:T(1,128)} copy(f32[1,36,16384]{2,1,0:T(8,128)S(1)} %bitcast.48) | data formatting | bytes 4718592
  204.4 1.6 collective-permute-start.37
  212.3 4.2 %collective-permute-done.37 = bf16[24,8192]{1,0:T(8,128)(2,1)S(1)} collective-permute-done((bf16[24,8192]{1,0:T(8,128)(2,1)S(1)}, bf16[24,8192]{1,0:T(8,128)(2,1)S(1)}, u32[]{:S(2)}, u32[]{:S(2)}) %collective-permute-start.37) | collective-permute-done | bytes 393248 | tf_op jit(solution)/shard_map/ppermute | solution.py:126
  219.9 16.2 %collective-permute-done.38 = bf16[24,8192]{1,0:T(8,128)(2,1)S(1)} collective-permute-done((bf16[24,8192]{1,0:T(8,128)(2,1)S(1)}, bf16[24,8192]{1,0:T(8,128)(2,1)S(1)}, u32[]{:S(2)}, u32[]{:S(2)}) %collective-permute-start.38) | collective-permute-done | bytes 393248 | tf_op jit(solution)/shard_map/ppermute | solution.py:126
  243.7 4.6 %collective-permute-done.39 = bf16[24,8192]{1,0:T(8,128)(2,1)S(1)} collective-permute-done((bf16[24,8192]{1,0:T(8,128)(2,1)S(1)}, bf16[24,8192]{1,0:T(8,128)(2,1)S(1)}, u32[]{:S(2)}, u32[]{:S(2)}) %collective-permute-start.39) | collective-permute-done | bytes 393248 | tf_op jit(solution)/shard_map/ppermute | solution.py:126
  251.6 10.7 %collective-permute-done.25 = bf16[36,8192]{1,0:T(8,128)(2,1)S(1)} collective-permute-done((bf16[36,8192]{1,0:T(8,128)(2,1)S(1)}, bf16[36,8192]{1,0:T(8,128)(2,1)S(1)}, u32[]{:S(2)}, u32[]{:S(2)}) %collective-permute-start.25) | collective-permute-done | bytes 589856 | tf_op jit(solution)/shard_map/ppermute | solution.py:124
  266.5 4.2 %collective-permute-done.40 = bf16[24,8192]{1,0:T(8,128)(2,1)S(1)} collective-permute-done((bf16[24,8192]{1,0:T(8,128)(2,1)S(1)}, bf16[24,8192]{1,0:T(8,128)(2,1)S(1)}, u32[]{:S(2)}, u32[]{:S(2)}) %collective-permute-start.40) | collective-permute-done | bytes 393248 | tf_op jit(solution)/shard_map/ppermute | solution.py:126
  274.1 13.5 %collective-permute-done.41 = bf16[24,8192]{1,0:T(8,128)(2,1)S(1)} collective-permute-done((bf16[24,8192]{1,0:T(8,128)(2,1)S(1)}, bf16[24,8192]{1,0:T(8,128)(2,1)S(1)}, u32[]{:S(2)}, u32[]{:S(2)}) %collective-permute-start.41) | collective-permute-done | bytes 393248 | tf_op jit(solution)/shard_map/ppermute | solution.py:126
  287.7 2.2 collective-permute-done.48
  291.2 1.6 collective-permute-start.27
  295.4 10.7 %collective-permute-done.27 = bf16[36,8192]{1,0:T(8,128)(2,1)S(1)} collective-permute-done((bf16[36,8192]{1,0:T(8,128)(2,1)S(1)}, bf16[36,8192]{1,0:T(8,128)(2,1)S(1)}, u32[]{:S(2)}, u32[]{:S(2)}) %collective-permute-start.27) | collective-permute-done | bytes 589856 | tf_op jit(solution)/shard_map/ppermute | solution.py:124
  310.3 6.4 %collective-permute-done.28 = bf16[36,8192]{1,0:T(8,128)(2,1)S(1)} collective-permute-done((bf16[36,8192]{1,0:T(8,128)(2,1)S(1)}, bf16[36,8192]{1,0:T(8,128)(2,1)S(1)}, u32[]{:S(2)}, u32[]{:S(2)}) %collective-permute-start.28) | collective-permute-done | bytes 589856 | tf_op jit(solution)/shard_map/ppermute | solution.py:124
  317.7 1.6 collective-permute-done.34
  320.4 3.3 %maximum_bitcast_fusion = bf16[1,192,16384]{2,1,0:T(8,128)(2,1)} fusion(bf16[192,8192]{1,0:T(8,128)(2,1)S(1)} %convolution_add_fusion, bf16[192,8192]{1,0:T(8,128)(2,1)S(1)} %convolution_add_fusion.7), kind=kLoop, calls=%fused_computation.16 | loop fusion | flops 12582912 | bytes 12582912 | tf_op jit(solution)/shard_map/broadcast_in_dim | solution.py:141
  (151 shorter events, 85.7 us)
Async XLA Ops:
  0.6 17.5 %collective-permute-start = (bf16[8,128]{1,0:T(8,128)(2,1)S(1)}, bf16[8,128]{1,0:T(8,128)(2,1)S(1)}, u32[]{:S(2)}, u32[]{:S(2)}) collective-permute-start(bf16[8,128]{1,0:T(8,128)(2,1)S(1)} %broadcast_in_dim.15), channel_id=1, source_target_pairs={{0,8},{8,16},{16,24},{24,28},{28,20},{20,12},{12,4},{4,0},{1,9},{9... | collective-permute-start | bytes 6152 | tf_op jit(solution)/shard_map/ppermute | solution.py:63
  3.7 14.4 %collective-permute-start.1 = (bf16[8,128]{1,0:T(8,128)(2,1)S(1)}, bf16[8,128]{1,0:T(8,128)(2,1)S(1)}, u32[]{:S(2)}, u32[]{:S(2)}) collective-permute-start(bf16[8,128]{1,0:T(8,128)(2,1)S(1)} %broadcast_in_dim.15), channel_id=1, source_target_pairs={{8,0},{16,8},{24,16},{28,24},{20,28},{12,20},{4,12},{0,4},{9,1},{1... | collective-permute-start | bytes 6152 | tf_op jit(solution)/shard_map/ppermute | solution.py:63
  10.9 16.3 %collective-permute-start.9 = (bf16[36,8192]{1,0:T(8,128)(2,1)S(1)}, bf16[36,8192]{1,0:T(8,128)(2,1)S(1)}, u32[]{:S(2)}, u32[]{:S(2)}) collective-permute-start(bf16[36,8192]{1,0:T(8,128)(2,1)S(1)} %slice.275), channel_id=1, source_target_pairs={{8,0},{16,8},{24,16},{28,24},{20,28},{12,20},{4,12},{0,4},{9,1},{1... | collective-permute-start | bytes 1769480 | tf_op jit(solution)/shard_map/ppermute | solution.py:80
  20.9 15.7 %collective-permute-start.2 = (bf16[36,8192]{1,0:T(8,128)(2,1)S(1)}, bf16[36,8192]{1,0:T(8,128)(2,1)S(1)}, u32[]{:S(2)}, u32[]{:S(2)}) collective-permute-start(bf16[36,8192]{1,0:T(8,128)(2,1)S(1)} %slice_add_fusion), channel_id=1, source_target_pairs={{0,8},{8,16},{16,24},{24,28},{28,20},{20,12},{12,4},{4,0},{1,9},{9... | collective-permute-start | bytes 1769480 | tf_op jit(solution)/shard_map/ppermute | solution.py:79
  28.4 15.3 %collective-permute-start.10 = (bf16[36,8192]{1,0:T(8,128)(2,1)S(1)}, bf16[36,8192]{1,0:T(8,128)(2,1)S(1)}, u32[]{:S(2)}, u32[]{:S(2)}) collective-permute-start(bf16[36,8192]{1,0:T(8,128)(2,1)S(1)} %add_convert_fusion.5), channel_id=1, source_target_pairs={{8,0},{16,8},{24,16},{28,24},{20,28},{12,20},{4,12},{0,4},{9,1},{1... | collective-permute-start | bytes 1769480 | tf_op jit(solution)/shard_map/ppermute | solution.py:80
  37.8 14.8 %collective-permute-start.3 = (bf16[36,8192]{1,0:T(8,128)(2,1)S(1)}, bf16[36,8192]{1,0:T(8,128)(2,1)S(1)}, u32[]{:S(2)}, u32[]{:S(2)}) collective-permute-start(bf16[36,8192]{1,0:T(8,128)(2,1)S(1)} %add_convert_fusion.11), channel_id=1, source_target_pairs={{0,8},{8,16},{16,24},{24,28},{28,20},{20,12},{12,4},{4,0},{1,9},{9... | collective-permute-start | bytes 1769480 | tf_op jit(solution)/shard_map/ppermute | solution.py:79
  44.0 14.7 %collective-permute-start.11 = (bf16[36,8192]{1,0:T(8,128)(2,1)S(1)}, bf16[36,8192]{1,0:T(8,128)(2,1)S(1)}, u32[]{:S(2)}, u32[]{:S(2)}) collective-permute-start(bf16[36,8192]{1,0:T(8,128)(2,1)S(1)} %add_convert_fusion.4), channel_id=1, source_target_pairs={{8,0},{16,8},{24,16},{28,24},{20,28},{12,20},{4,12},{0,4},{9,1},{1... | collective-permute-start | bytes 1769480 | tf_op jit(solution)/shard_map/ppermute | solution.py:80
  54.0 14.7 %collective-permute-start.4 = (bf16[36,8192]{1,0:T(8,128)(2,1)S(1)}, bf16[36,8192]{1,0:T(8,128)(2,1)S(1)}, u32[]{:S(2)}, u32[]{:S(2)}) collective-permute-start(bf16[36,8192]{1,0:T(8,128)(2,1)S(1)} %add_convert_fusion.10), channel_id=1, source_target_pairs={{0,8},{8,16},{16,24},{24,28},{28,20},{20,12},{12,4},{4,0},{1,9},{9... | collective-permute-start | bytes 1769480 | tf_op jit(solution)/shard_map/ppermute | solution.py:79
  58.9 14.7 %collective-permute-start.12 = (bf16[36,8192]{1,0:T(8,128)(2,1)S(1)}, bf16[36,8192]{1,0:T(8,128)(2,1)S(1)}, u32[]{:S(2)}, u32[]{:S(2)}) collective-permute-start(bf16[36,8192]{1,0:T(8,128)(2,1)S(1)} %add_convert_fusion.3), channel_id=1, source_target_pairs={{8,0},{16,8},{24,16},{28,24},{20,28},{12,20},{4,12},{0,4},{9,1},{1... | collective-permute-start | bytes 1769480 | tf_op jit(solution)/shard_map/ppermute | solution.py:80
  68.8 14.6 %collective-permute-start.5 = (bf16[36,8192]{1,0:T(8,128)(2,1)S(1)}, bf16[36,8192]{1,0:T(8,128)(2,1)S(1)}, u32[]{:S(2)}, u32[]{:S(2)}) collective-permute-start(bf16[36,8192]{1,0:T(8,128)(2,1)S(1)} %add_convert_fusion.9), channel_id=1, source_target_pairs={{0,8},{8,16},{16,24},{24,28},{28,20},{20,12},{12,4},{4,0},{1,9},{9... | collective-permute-start | bytes 1769480 | tf_op jit(solution)/shard_map/ppermute | solution.py:79
  73.8 14.7 %collective-permute-start.13 = (bf16[36,8192]{1,0:T(8,128)(2,1)S(1)}, bf16[36,8192]{1,0:T(8,128)(2,1)S(1)}, u32[]{:S(2)}, u32[]{:S(2)}) collective-permute-start(bf16[36,8192]{1,0:T(8,128)(2,1)S(1)} %add_convert_fusion.2), channel_id=1, source_target_pairs={{8,0},{16,8},{24,16},{28,24},{20,28},{12,20},{4,12},{0,4},{9,1},{1... | collective-permute-start | bytes 1769480 | tf_op jit(solution)/shard_map/ppermute | solution.py:80
  83.7 14.7 %collective-permute-start.6 = (bf16[36,8192]{1,0:T(8,128)(2,1)S(1)}, bf16[36,8192]{1,0:T(8,128)(2,1)S(1)}, u32[]{:S(2)}, u32[]{:S(2)}) collective-permute-start(bf16[36,8192]{1,0:T(8,128)(2,1)S(1)} %add_convert_fusion.8), channel_id=1, source_target_pairs={{0,8},{8,16},{16,24},{24,28},{28,20},{20,12},{12,4},{4,0},{1,9},{9... | collective-permute-start | bytes 1769480 | tf_op jit(solution)/shard_map/ppermute | solution.py:79
  88.7 13.7 %collective-permute-start.14 = (bf16[36,8192]{1,0:T(8,128)(2,1)S(1)}, bf16[36,8192]{1,0:T(8,128)(2,1)S(1)}, u32[]{:S(2)}, u32[]{:S(2)}) collective-permute-start(bf16[36,8192]{1,0:T(8,128)(2,1)S(1)} %add_convert_fusion.1), channel_id=1, source_target_pairs={{8,0},{16,8},{24,16},{28,24},{20,28},{12,20},{4,12},{0,4},{9,1},{1... | collective-permute-start | bytes 1769480 | tf_op jit(solution)/shard_map/ppermute | solution.py:80
  98.6 13.5 %collective-permute-start.7 = (bf16[36,8192]{1,0:T(8,128)(2,1)S(1)}, bf16[36,8192]{1,0:T(8,128)(2,1)S(1)}, u32[]{:S(2)}, u32[]{:S(2)}) collective-permute-start(bf16[36,8192]{1,0:T(8,128)(2,1)S(1)} %add_convert_fusion.7), channel_id=1, source_target_pairs={{0,8},{8,16},{16,24},{24,28},{28,20},{20,12},{12,4},{4,0},{1,9},{9... | collective-permute-start | bytes 1769480 | tf_op jit(solution)/shard_map/ppermute | solution.py:79
  103.4 24.6 %collective-permute-start.15 = (bf16[36,8192]{1,0:T(8,128)(2,1)}, bf16[36,8192]{1,0:T(8,128)(2,1)S(1)}, u32[]{:S(2)}, u32[]{:S(2)}) collective-permute-start(bf16[36,8192]{1,0:T(8,128)(2,1)} %add_convert_fusion), channel_id=1, source_target_pairs={{8,0},{16,8},{24,16},{28,24},{20,28},{12,20},{4,12},{0,4},{9,1},{1... | collective-permute-start | bytes 1769480 | tf_op jit(solution)/shard_map/ppermute | solution.py:80
  113.2 16.8 %collective-permute-start.8 = (bf16[36,8192]{1,0:T(8,128)(2,1)}, bf16[36,8192]{1,0:T(8,128)(2,1)}, u32[]{:S(2)}, u32[]{:S(2)}) collective-permute-start(bf16[36,8192]{1,0:T(8,128)(2,1)} %add_convert_fusion.6), channel_id=1, source_target_pairs={{0,8},{8,16},{16,24},{24,28},{28,20},{20,12},{12,4},{4,0},{1,9},{9... | collective-permute-start | bytes 1769480 | tf_op jit(solution)/shard_map/ppermute | solution.py:79
  135.5 3.6 %collective-permute-start.17 = (f32[1,1]{1,0:T(1,128)}, f32[1,1]{1,0:T(1,128)}, u32[]{:S(2)}, u32[]{:S(2)}) collective-permute-start(f32[1,1]{1,0:T(1,128)} %add.318), channel_id=1, source_target_pairs={{0,2},{1,3},{2,0},{3,1},{4,6},{5,7},{6,4},{7,5},{8,10},{9,11},{10,... | collective-permute-start | bytes 20 | tf_op jit(solution)/shard_map/ppermute | solution.py:41
  139.7 3.6 %collective-permute-start.18 = (f32[1,1]{1,0:T(1,128)}, f32[1,1]{1,0:T(1,128)}, u32[]{:S(2)}, u32[]{:S(2)}) collective-permute-start(f32[1,1]{1,0:T(1,128)} %add.319), channel_id=1, source_target_pairs={{0,4},{4,0},{8,12},{12,8},{16,20},{20,16},{24,28},{28,24},{1,5},{5... | collective-permute-start | bytes 20 | tf_op jit(solution)/shard_map/ppermute | solution.py:41
  144.0 3.6 %collective-permute-start.19 = (f32[1,1]{1,0:T(1,128)}, f32[1,1]{1,0:T(1,128)}, u32[]{:S(2)}, u32[]{:S(2)}) collective-permute-start(f32[1,1]{1,0:T(1,128)} %add.320), channel_id=1, source_target_pairs={{0,8},{4,12},{8,0},{12,4},{16,24},{20,28},{24,16},{28,20},{1,9},{5... | collective-permute-start | bytes 20 | tf_op jit(solution)/shard_map/ppermute | solution.py:41
  148.2 4.5 %collective-permute-start.20 = (f32[1,1]{1,0:T(1,128)}, f32[1,1]{1,0:T(1,128)}, u32[]{:S(2)}, u32[]{:S(2)}) collective-permute-start(f32[1,1]{1,0:T(1,128)} %add.321), channel_id=1, source_target_pairs={{0,16},{4,20},{8,24},{12,28},{16,0},{20,4},{24,8},{28,12},{1,17},{... | collective-permute-start | bytes 20 | tf_op jit(solution)/shard_map/ppermute | solution.py:41
  159.5 12.1 %collective-permute-start.35 = (bf16[24,8192]{1,0:T(8,128)(2,1)S(1)}, bf16[24,8192]{1,0:T(8,128)(2,1)S(1)}, u32[]{:S(2)}, u32[]{:S(2)}) collective-permute-start(bf16[24,8192]{1,0:T(8,128)(2,1)S(1)} %slice.295), channel_id=1, source_target_pairs={{0,8},{8,16},{16,24},{24,28},{28,20},{20,12},{12,4},{4,0},{1,9},{9... | collective-permute-start | bytes 1179656 | tf_op jit(solution)/shard_map/ppermute | solution.py:126
  162.1 12.1 %collective-permute-start.42 = (bf16[24,8192]{1,0:T(8,128)(2,1)S(1)}, bf16[24,8192]{1,0:T(8,128)(2,1)S(1)}, u32[]{:S(2)}, u32[]{:S(2)}) collective-permute-start(bf16[24,8192]{1,0:T(8,128)(2,1)S(1)} %slice.304), channel_id=1, source_target_pairs={{8,0},{16,8},{24,16},{28,24},{20,28},{12,20},{4,12},{0,4},{9,1},{1... | collective-permute-start | bytes 1179656 | tf_op jit(solution)/shard_map/ppermute | solution.py:127
  162.7 22.9 %collective-permute-start.21 = (bf16[36,8192]{1,0:T(8,128)(2,1)S(1)}, bf16[36,8192]{1,0:T(8,128)(2,1)S(1)}, u32[]{:S(2)}, u32[]{:S(2)}) collective-permute-start(bf16[36,8192]{1,0:T(8,128)(2,1)S(1)} %get-tuple-element.30), channel_id=1, source_target_pairs={{0,8},{8,16},{16,24},{24,28},{28,20},{20,12},{12,4},{4,0},{1,9},{9... | collective-permute-start | bytes 1769480 | tf_op jit(solution)/shard_map/ppermute | solution.py:124
  164.1 24.1 %collective-permute-start.22 = (bf16[36,8192]{1,0:T(8,128)(2,1)S(1)}, bf16[36,8192]{1,0:T(8,128)(2,1)S(1)}, u32[]{:S(2)}, u32[]{:S(2)}) collective-permute-start(bf16[36,8192]{1,0:T(8,128)(2,1)S(1)} %get-tuple-element.38), channel_id=1, source_target_pairs={{8,0},{16,8},{24,16},{28,24},{20,28},{12,20},{4,12},{0,4},{9,1},{1... | collective-permute-start | bytes 1769480 | tf_op jit(solution)/shard_map/ppermute | solution.py:125
  171.7 32.5 %collective-permute-start.36 = (bf16[24,8192]{1,0:T(8,128)(2,1)S(1)}, bf16[24,8192]{1,0:T(8,128)(2,1)S(1)}, u32[]{:S(2)}, u32[]{:S(2)}) collective-permute-start(bf16[24,8192]{1,0:T(8,128)(2,1)S(1)} %add_convert_fusion.23), channel_id=1, source_target_pairs={{0,8},{8,16},{16,24},{24,28},{28,20},{20,12},{12,4},{4,0},{1,9},{9... | collective-permute-start | bytes 1179656 | tf_op jit(solution)/shard_map/ppermute | solution.py:126
  174.3 31.7 %collective-permute-start.43 = (bf16[24,8192]{1,0:T(8,128)(2,1)S(1)}, bf16[24,8192]{1,0:T(8,128)(2,1)S(1)}, u32[]{:S(2)}, u32[]{:S(2)}) collective-permute-start(bf16[24,8192]{1,0:T(8,128)(2,1)S(1)} %add_convert_fusion.17), channel_id=1, source_target_pairs={{8,0},{16,8},{24,16},{28,24},{20,28},{12,20},{4,12},{0,4},{9,1},{1... | collective-permute-start | bytes 1179656 | tf_op jit(solution)/shard_map/ppermute | solution.py:127
  188.2 19.9 %collective-permute-start.23 = (bf16[36,8192]{1,0:T(8,128)(2,1)S(1)}, bf16[36,8192]{1,0:T(8,128)(2,1)S(1)}, u32[]{:S(2)}, u32[]{:S(2)}) collective-permute-start(bf16[36,8192]{1,0:T(8,128)(2,1)S(1)} %collective-permute-done.21), channel_id=1, source_target_pairs={{0,8},{8,16},{16,24},{24,28},{28,20},{20,12},{12,4},{4,0},{1,9},{9... | collective-permute-start | bytes 1769480 | tf_op jit(solution)/shard_map/ppermute | solution.py:124
  190.8 19.9 %collective-permute-start.29 = (bf16[36,8192]{1,0:T(8,128)(2,1)S(1)}, bf16[36,8192]{1,0:T(8,128)(2,1)S(1)}, u32[]{:S(2)}, u32[]{:S(2)}) collective-permute-start(bf16[36,8192]{1,0:T(8,128)(2,1)S(1)} %collective-permute-done.22), channel_id=1, source_target_pairs={{8,0},{16,8},{24,16},{28,24},{20,28},{12,20},{4,12},{0,4},{9,1},{1... | collective-permute-start | bytes 1769480 | tf_op jit(solution)/shard_map/ppermute | solution.py:125
  204.4 12.2 %collective-permute-start.37 = (bf16[24,8192]{1,0:T(8,128)(2,1)S(1)}, bf16[24,8192]{1,0:T(8,128)(2,1)S(1)}, u32[]{:S(2)}, u32[]{:S(2)}) collective-permute-start(bf16[24,8192]{1,0:T(8,128)(2,1)S(1)} %add_convert_fusion.22), channel_id=1, source_target_pairs={{0,8},{8,16},{16,24},{24,28},{28,20},{20,12},{12,4},{4,0},{1,9},{9... | collective-permute-start | bytes 1179656 | tf_op jit(solution)/shard_map/ppermute | solution.py:126
  206.1 13.0 %collective-permute-start.44 = (bf16[24,8192]{1,0:T(8,128)(2,1)S(1)}, bf16[24,8192]{1,0:T(8,128)(2,1)S(1)}, u32[]{:S(2)}, u32[]{:S(2)}) collective-permute-start(bf16[24,8192]{1,0:T(8,128)(2,1)S(1)} %add_convert_fusion.16), channel_id=1, source_target_pairs={{8,0},{16,8},{24,16},{28,24},{20,28},{12,20},{4,12},{0,4},{9,1},{1... | collective-permute-start | bytes 1179656 | tf_op jit(solution)/shard_map/ppermute | solution.py:127
  208.1 31.3 %collective-permute-start.24 = (bf16[36,8192]{1,0:T(8,128)(2,1)S(1)}, bf16[36,8192]{1,0:T(8,128)(2,1)S(1)}, u32[]{:S(2)}, u32[]{:S(2)}) collective-permute-start(bf16[36,8192]{1,0:T(8,128)(2,1)S(1)} %collective-permute-done.23), channel_id=1, source_target_pairs={{0,8},{8,16},{16,24},{24,28},{28,20},{20,12},{12,4},{4,0},{1,9},{9... | collective-permute-start | bytes 1769480 | tf_op jit(solution)/shard_map/ppermute | solution.py:124
  210.7 31.4 %collective-permute-start.30 = (bf16[36,8192]{1,0:T(8,128)(2,1)S(1)}, bf16[36,8192]{1,0:T(8,128)(2,1)S(1)}, u32[]{:S(2)}, u32[]{:S(2)}) collective-permute-start(bf16[36,8192]{1,0:T(8,128)(2,1)S(1)} %collective-permute-done.29), channel_id=1, source_target_pairs={{8,0},{16,8},{24,16},{28,24},{20,28},{12,20},{4,12},{0,4},{9,1},{1... | collective-permute-start | bytes 1769480 | tf_op jit(solution)/shard_map/ppermute | solution.py:125
  216.7 19.5 %collective-permute-start.38 = (bf16[24,8192]{1,0:T(8,128)(2,1)S(1)}, bf16[24,8192]{1,0:T(8,128)(2,1)S(1)}, u32[]{:S(2)}, u32[]{:S(2)}) collective-permute-start(bf16[24,8192]{1,0:T(8,128)(2,1)S(1)} %add_convert_fusion.21), channel_id=1, source_target_pairs={{0,8},{8,16},{16,24},{24,28},{28,20},{20,12},{12,4},{4,0},{1,9},{9... | collective-permute-start | bytes 1179656 | tf_op jit(solution)/shard_map/ppermute | solution.py:126
  219.2 19.5 %collective-permute-start.45 = (bf16[24,8192]{1,0:T(8,128)(2,1)S(1)}, bf16[24,8192]{1,0:T(8,128)(2,1)S(1)}, u32[]{:S(2)}, u32[]{:S(2)}) collective-permute-start(bf16[24,8192]{1,0:T(8,128)(2,1)S(1)} %add_convert_fusion.15), channel_id=1, source_target_pairs={{8,0},{16,8},{24,16},{28,24},{20,28},{12,20},{4,12},{0,4},{9,1},{1... | collective-permute-start | bytes 1179656 | tf_op jit(solution)/shard_map/ppermute | solution.py:127
  236.2 12.1 %collective-permute-start.39 = (bf16[24,8192]{1,0:T(8,128)(2,1)S(1)}, bf16[24,8192]{1,0:T(8,128)(2,1)S(1)}, u32[]{:S(2)}, u32[]{:S(2)}) collective-permute-start(bf16[24,8192]{1,0:T(8,128)(2,1)S(1)} %add_convert_fusion.20), channel_id=1, source_target_pairs={{0,8},{8,16},{16,24},{24,28},{28,20},{20,12},{12,4},{4,0},{1,9},{9... | collective-permute-start | bytes 1179656 | tf_op jit(solution)/shard_map/ppermute | solution.py:126
  238.8 12.1 %collective-permute-start.46 = (bf16[24,8192]{1,0:T(8,128)(2,1)S(1)}, bf16[24,8192]{1,0:T(8,128)(2,1)S(1)}, u32[]{:S(2)}, u32[]{:S(2)}) collective-permute-start(bf16[24,8192]{1,0:T(8,128)(2,1)S(1)} %add_convert_fusion.14), channel_id=1, source_target_pairs={{8,0},{16,8},{24,16},{28,24},{20,28},{12,20},{4,12},{0,4},{9,1},{1... | collective-permute-start | bytes 1179656 | tf_op jit(solution)/shard_map/ppermute | solution.py:127
  239.4 22.9 %collective-permute-start.25 = (bf16[36,8192]{1,0:T(8,128)(2,1)S(1)}, bf16[36,8192]{1,0:T(8,128)(2,1)S(1)}, u32[]{:S(2)}, u32[]{:S(2)}) collective-permute-start(bf16[36,8192]{1,0:T(8,128)(2,1)S(1)} %collective-permute-done.24), channel_id=1, source_target_pairs={{0,8},{8,16},{16,24},{24,28},{28,20},{20,12},{12,4},{4,0},{1,9},{9... | collective-permute-start | bytes 1769480 | tf_op jit(solution)/shard_map/ppermute | solution.py:124
  242.0 22.9 %collective-permute-start.31 = (bf16[36,8192]{1,0:T(8,128)(2,1)S(1)}, bf16[36,8192]{1,0:T(8,128)(2,1)S(1)}, u32[]{:S(2)}, u32[]{:S(2)}) collective-permute-start(bf16[36,8192]{1,0:T(8,128)(2,1)S(1)} %collective-permute-done.30), channel_id=1, source_target_pairs={{8,0},{16,8},{24,16},{28,24},{20,28},{12,20},{4,12},{0,4},{9,1},{1... | collective-permute-start | bytes 1769480 | tf_op jit(solution)/shard_map/ppermute | solution.py:125
  248.4 22.4 %collective-permute-start.40 = (bf16[24,8192]{1,0:T(8,128)(2,1)S(1)}, bf16[24,8192]{1,0:T(8,128)(2,1)S(1)}, u32[]{:S(2)}, u32[]{:S(2)}) collective-permute-start(bf16[24,8192]{1,0:T(8,128)(2,1)S(1)} %add_convert_fusion.19), channel_id=1, source_target_pairs={{0,8},{8,16},{16,24},{24,28},{28,20},{20,12},{12,4},{4,0},{1,9},{9... | collective-permute-start | bytes 1179656 | tf_op jit(solution)/shard_map/ppermute | solution.py:126
  251.0 22.4 %collective-permute-start.47 = (bf16[24,8192]{1,0:T(8,128)(2,1)S(1)}, bf16[24,8192]{1,0:T(8,128)(2,1)S(1)}, u32[]{:S(2)}, u32[]{:S(2)}) collective-permute-start(bf16[24,8192]{1,0:T(8,128)(2,1)S(1)} %add_convert_fusion.13), channel_id=1, source_target_pairs={{8,0},{16,8},{24,16},{28,24},{20,28},{12,20},{4,12},{0,4},{9,1},{1... | collective-permute-start | bytes 1179656 | tf_op jit(solution)/shard_map/ppermute | solution.py:127
  262.4 28.9 %collective-permute-start.26 = (bf16[36,8192]{1,0:T(8,128)(2,1)S(1)}, bf16[36,8192]{1,0:T(8,128)(2,1)S(1)}, u32[]{:S(2)}, u32[]{:S(2)}) collective-permute-start(bf16[36,8192]{1,0:T(8,128)(2,1)S(1)} %collective-permute-done.25), channel_id=1, source_target_pairs={{0,8},{8,16},{16,24},{24,28},{28,20},{20,12},{12,4},{4,0},{1,9},{9... | collective-permute-start | bytes 1769480 | tf_op jit(solution)/shard_map/ppermute | solution.py:124
  264.9 28.9 %collective-permute-start.32 = (bf16[36,8192]{1,0:T(8,128)(2,1)S(1)}, bf16[36,8192]{1,0:T(8,128)(2,1)S(1)}, u32[]{:S(2)}, u32[]{:S(2)}) collective-permute-start(bf16[36,8192]{1,0:T(8,128)(2,1)S(1)} %collective-permute-done.31), channel_id=1, source_target_pairs={{8,0},{16,8},{24,16},{28,24},{20,28},{12,20},{4,12},{0,4},{9,1},{1... | collective-permute-start | bytes 1769480 | tf_op jit(solution)/shard_map/ppermute | solution.py:125
  270.9 16.7 %collective-permute-start.41 = (bf16[24,8192]{1,0:T(8,128)(2,1)S(1)}, bf16[24,8192]{1,0:T(8,128)(2,1)S(1)}, u32[]{:S(2)}, u32[]{:S(2)}) collective-permute-start(bf16[24,8192]{1,0:T(8,128)(2,1)S(1)} %add_convert_fusion.18), channel_id=1, source_target_pairs={{0,8},{8,16},{16,24},{24,28},{28,20},{20,12},{12,4},{4,0},{1,9},{9... | collective-permute-start | bytes 1179656 | tf_op jit(solution)/shard_map/ppermute | solution.py:126
  273.4 16.5 %collective-permute-start.48 = (bf16[24,8192]{1,0:T(8,128)(2,1)S(1)}, bf16[24,8192]{1,0:T(8,128)(2,1)S(1)}, u32[]{:S(2)}, u32[]{:S(2)}) collective-permute-start(bf16[24,8192]{1,0:T(8,128)(2,1)S(1)} %add_convert_fusion.12), channel_id=1, source_target_pairs={{8,0},{16,8},{24,16},{28,24},{20,28},{12,20},{4,12},{0,4},{9,1},{1... | collective-permute-start | bytes 1179656 | tf_op jit(solution)/shard_map/ppermute | solution.py:127
  291.2 14.9 %collective-permute-start.27 = (bf16[36,8192]{1,0:T(8,128)(2,1)S(1)}, bf16[36,8192]{1,0:T(8,128)(2,1)S(1)}, u32[]{:S(2)}, u32[]{:S(2)}) collective-permute-start(bf16[36,8192]{1,0:T(8,128)(2,1)S(1)} %collective-permute-done.26), channel_id=1, source_target_pairs={{0,8},{8,16},{16,24},{24,28},{28,20},{20,12},{12,4},{4,0},{1,9},{9... | collective-permute-start | bytes 1769480 | tf_op jit(solution)/shard_map/ppermute | solution.py:124
  293.8 14.9 %collective-permute-start.33 = (bf16[36,8192]{1,0:T(8,128)(2,1)S(1)}, bf16[36,8192]{1,0:T(8,128)(2,1)S(1)}, u32[]{:S(2)}, u32[]{:S(2)}) collective-permute-start(bf16[36,8192]{1,0:T(8,128)(2,1)S(1)} %collective-permute-done.32), channel_id=1, source_target_pairs={{8,0},{16,8},{24,16},{28,24},{20,28},{12,20},{4,12},{0,4},{9,1},{1... | collective-permute-start | bytes 1769480 | tf_op jit(solution)/shard_map/ppermute | solution.py:125
  306.1 10.6 %collective-permute-start.28 = (bf16[36,8192]{1,0:T(8,128)(2,1)S(1)}, bf16[36,8192]{1,0:T(8,128)(2,1)S(1)}, u32[]{:S(2)}, u32[]{:S(2)}) collective-permute-start(bf16[36,8192]{1,0:T(8,128)(2,1)S(1)} %collective-permute-done.27), channel_id=1, source_target_pairs={{0,8},{8,16},{16,24},{24,28},{28,20},{20,12},{12,4},{4,0},{1,9},{9... | collective-permute-start | bytes 1769480 | tf_op jit(solution)/shard_map/ppermute | solution.py:124
  308.7 10.6 %collective-permute-start.34 = (bf16[36,8192]{1,0:T(8,128)(2,1)S(1)}, bf16[36,8192]{1,0:T(8,128)(2,1)S(1)}, u32[]{:S(2)}, u32[]{:S(2)}) collective-permute-start(bf16[36,8192]{1,0:T(8,128)(2,1)S(1)} %collective-permute-done.33), channel_id=1, source_target_pairs={{8,0},{16,8},{24,16},{28,24},{20,28},{12,20},{4,12},{0,4},{9,1},{1... | collective-permute-start | bytes 1769480 | tf_op jit(solution)/shard_map/ppermute | solution.py:125
  (10 other events, 94.2 us)
